TPU v7x, 256 devices: a whole 4x4x8 slice. The times are simulated.
256 devices in a mesh: req: 32 (over z, y), tp: 8 (over x, core).
Axes of the slice: x: 4, y: 4, z: 8, core: 2. Of those that a mesh axis runs over, the one named last changes fastest.
Arguments:
- queries: bfloat16 [16384, 7168], P('req', 'tp')
- keys_new: bfloat16 [16384, 7168], P('req', 'tp')
- values_new: bfloat16 [16384, 7168], P('req', 'tp'), may hold values from -6 to 6
- cache_keys: bfloat16 [64, 1024, 7168], P('req', None, 'tp'), may hold values from -6 to 6
- cache_values: bfloat16 [64, 1024, 7168], P('req', None, 'tp'), may hold values from -6 to 6
- out_proj: bfloat16 [7168, 3584], P('tp'), may hold values from -0.0625 to 0.0625
- req_lengths: int32 [32, 4], P('req'), may hold values from 1 to 415, as said below
- cache_owner: int32 [32, 2], P('req'), may hold values from 0 to 31, as said below
- cache_slot: int32 [32, 2], P('req'), may hold values from 0 to 1
- prior_len: int32 [32, 2], P('req'), may hold values from 1 to 1024, as said below
Outputs:
- mixed: bfloat16 [16384, 3584], P(('req', 'tp'))
- new_keys: bfloat16 [64, 192, 7168], P('req', None, 'tp')
- new_values: bfloat16 [64, 192, 7168], P('req', None, 'tp')
Inputs may be any that keep to these rules, and one draw needn't show every extreme that they name: `req_lengths`: each row sums to 512; each continuing request has at most 192 new tokens, and some continuing request has exactly 192; continuing requests have at least 48 new tokens; some request has exactly 415. `cache_owner`: A continuing request's owner is the req index just before or just after its own, counted around the axis (index 0 follows index 31); the two continuing requests of one index have different owners; every cache slot of every index is used by exactly one continuing request. `prior_len`: some continuing request has exactly 1024 prior tokens.
All inputs are finite; a program needn't handle non-finite values.
Results may differ from a plain program's by a relative error of at most 0.014.
Values may be sent and summed in bfloat16 or wider, within the bound.
No kernel may reach another device: no remote copies, remote signals or barrier semaphores. Data moves between devices by JAX's collectives and lax.ppermute only.
A program may use at most 128 MiB of HBM per device.

v0:
```python
import math

import jax
import jax.numpy as jnp
from jax import lax
from jax.sharding import PartitionSpec as P

HD = 224
NEWCAP = 192


shift_steps = (1, -1)
floor_value = -1e30


def shifted(value, axis, steps):
    count = lax.axis_size(axis)
    pairs = [(source, (source + steps) % count) for source in range(count)]
    return lax.ppermute(value, axis, pairs)


def attend_part(query_rows, key_rows, value_rows, live_mask, head_count):
    row_count = query_rows.shape[0]
    key_count = key_rows.shape[0]
    query_heads = query_rows.reshape(row_count, head_count, HD)
    key_heads = key_rows.reshape(key_count, head_count, HD)
    value_heads = value_rows.reshape(key_count, head_count, HD)
    scores = jnp.einsum(
        "thd,shd->hts", query_heads, key_heads, preferred_element_type=jnp.float32
    ) * (1.0 / math.sqrt(HD))
    scores = jnp.where(live_mask[None], scores, floor_value)
    row_top = jnp.max(scores, axis=2)
    weights = jnp.where(live_mask[None], jnp.exp(scores - row_top[:, :, None]), 0.0)
    row_total = jnp.sum(weights, axis=2)
    numerator = jnp.einsum(
        "hts,shd->thd",
        weights.astype(jnp.bfloat16),
        value_heads,
        preferred_element_type=jnp.float32,
    )
    return (numerator.reshape(row_count, head_count * HD), row_top.T, row_total.T)


def body(
    queries,
    keys_new,
    values_new,
    cache_keys,
    cache_values,
    out_proj,
    req_lengths,
    cache_owner,
    cache_slot,
    prior_len,
):
    tok_count = queries.shape[0]
    feat_width = queries.shape[1]
    head_count = feat_width // HD
    slot_count = cache_keys.shape[0]
    prior_rows = cache_keys.shape[1]
    req_lens = req_lengths[0]
    req_ends = jnp.cumsum(req_lens)
    starts = req_ends - req_lens
    positions = jnp.arange(tok_count, dtype=jnp.int32)
    segment = jnp.sum((positions[:, None] >= req_ends[None, :]).astype(jnp.int32), axis=1)
    own_live = (segment[:, None] == segment[None, :]) & (positions[None, :] <= positions[:, None])
    own_numer, own_top, own_total = attend_part(queries, keys_new, values_new, own_live, head_count)
    req_count = lax.axis_size("req")
    req_index = lax.axis_index("req")
    raw_offset = (cache_owner[0] - req_index + req_count) % req_count
    offset = jnp.where(raw_offset == req_count - 1, -1, raw_offset)
    row_marks = jnp.arange(NEWCAP, dtype=jnp.int32)
    slot_ids = jnp.arange(slot_count, dtype=jnp.int32)
    prior_marks = jnp.arange(prior_rows, dtype=jnp.int32)

    def rows_of(source, j):
        padded = jnp.pad(source, ((0, NEWCAP), (0, 0)))
        return lax.dynamic_slice_in_dim(padded, starts[j], NEWCAP, 0)

    valid_rows = [row_marks < req_lens[j] for j in range(slot_count)]
    query_rows = [rows_of(queries, j) for j in range(slot_count)]
    key_rows = [
        jnp.where(valid_rows[j][:, None], rows_of(keys_new, j), jnp.zeros((), jnp.bfloat16))
        for j in range(slot_count)
    ]
    value_rows = [
        jnp.where(valid_rows[j][:, None], rows_of(values_new, j), jnp.zeros((), jnp.bfloat16))
        for j in range(slot_count)
    ]
    tag_rows = [
        jnp.stack([cache_slot[0, j], jnp.int32(1), prior_len[0, j]]) for j in range(slot_count)
    ]

    def select_for(distance, items):
        chosen = jnp.zeros_like(items[0])
        for j in range(slot_count):
            chosen = jnp.where(offset[j] == distance, items[j], chosen)
        return chosen

    new_keys = jnp.zeros((slot_count, NEWCAP, feat_width), jnp.bfloat16)
    new_values = jnp.zeros((slot_count, NEWCAP, feat_width), jnp.bfloat16)
    chosen_keys = [jnp.zeros((prior_rows, feat_width), jnp.bfloat16) for j in range(slot_count)]
    chosen_values = [jnp.zeros((prior_rows, feat_width), jnp.bfloat16) for j in range(slot_count)]
    for distance in shift_steps:
        fetched_keys, fetched_values = shifted((cache_keys, cache_values), "req", -distance)
        for j in range(slot_count):
            is_owner = offset[j] == distance
            chosen_keys[j] = jnp.where(
                is_owner,
                lax.dynamic_index_in_dim(fetched_keys, cache_slot[0, j], 0, keepdims=False),
                chosen_keys[j],
            )
            chosen_values[j] = jnp.where(
                is_owner,
                lax.dynamic_index_in_dim(fetched_values, cache_slot[0, j], 0, keepdims=False),
                chosen_values[j],
            )
        got_keys, got_values, got_tag = shifted(
            (
                select_for(distance, key_rows),
                select_for(distance, value_rows),
                select_for(distance, tag_rows),
            ),
            "req",
            distance,
        )
        stored_keys = new_keys
        stored_values = new_values
        is_target = (slot_ids == got_tag[0]) & (got_tag[1] == 1)
        stored_keys = jnp.where(is_target[:, None, None], got_keys[None], stored_keys)
        stored_values = jnp.where(is_target[:, None, None], got_values[None], stored_values)
        new_keys = stored_keys
        new_values = stored_values
    results = []
    for j in range(slot_count):
        live_mask = jnp.broadcast_to(prior_marks[None, :] < prior_len[0, j], (NEWCAP, prior_rows))
        results.append(
            attend_part(query_rows[j], chosen_keys[j], chosen_values[j], live_mask, head_count)
        )
    full_numer = jnp.zeros((tok_count + NEWCAP, feat_width), jnp.float32)
    full_top = jnp.full((tok_count + NEWCAP, head_count), floor_value, jnp.float32)
    full_total = jnp.zeros((tok_count + NEWCAP, head_count), jnp.float32)
    for j in range(slot_count):
        keep = valid_rows[j][:, None]
        full_numer = lax.dynamic_update_slice_in_dim(
            full_numer, jnp.where(keep, results[j][0], 0.0), starts[j], 0
        )
        full_top = lax.dynamic_update_slice_in_dim(
            full_top, jnp.where(keep, results[j][1], floor_value), starts[j], 0
        )
        full_total = lax.dynamic_update_slice_in_dim(
            full_total, jnp.where(keep, results[j][2], 0.0), starts[j], 0
        )
    prior_numer = full_numer[:tok_count]
    prior_top = full_top[:tok_count]
    prior_total = full_total[:tok_count]
    both_top = jnp.maximum(own_top, prior_top)
    own_scale = jnp.exp(own_top - both_top)
    prior_scale = jnp.exp(prior_top - both_top)
    denominator = own_total * own_scale + prior_total * prior_scale
    numerator = (
        own_numer.reshape(tok_count, head_count, HD) * own_scale[:, :, None]
        + prior_numer.reshape(tok_count, head_count, HD) * prior_scale[:, :, None]
    )
    attended = (
        (numerator / denominator[:, :, None]).reshape(tok_count, feat_width).astype(jnp.bfloat16)
    )
    mixed = lax.psum_scatter(
        jnp.dot(attended, out_proj, preferred_element_type=jnp.float32).astype(jnp.bfloat16),
        "tp",
        scatter_dimension=0,
        tiled=True,
    )
    return (mixed, new_keys, new_values)


def solution(mesh):
    in_specs = (
        P("req", "tp"),
        P("req", "tp"),
        P("req", "tp"),
        P("req", None, "tp"),
        P("req", None, "tp"),
        P("tp", None),
        P("req", None),
        P("req", None),
        P("req", None),
        P("req", None),
    )
    out_specs = (P(("req", "tp"), None), P("req", None, "tp"), P("req", None, "tp"))
    return jax.shard_map(body, mesh=mesh, in_specs=in_specs, out_specs=out_specs, check_vma=False)
```

profile of v0, /device:TPU:8, one launch (start us, length us, event | category | flops | bytes accessed | tf_op | source)
XLA Modules:
  0.0 277.2 jit_solution(11570764835919608476)
XLA Ops:
  7.2 6.1 %copy.41 = bf16[2,1024,896]{1,2,0:T(8,128)(2,1)} copy(bf16[2,1024,896]{2,1,0:T(8,128)(2,1)} %param.13) | data formatting | bytes 7340032 | tf_op args[3]
  13.3 1.7 collective-permute-start
  15.7 6.1 %copy.45 = bf16[2,1024,896]{1,2,0:T(8,128)(2,1)} copy(bf16[2,1024,896]{2,1,0:T(8,128)(2,1)} %param.14) | data formatting | bytes 7340032 | tf_op args[4]
  21.8 1.3 collective-permute-start.2
  23.1 5.2 %collective-permute-start.3 = (bf16[2,1024,896]{1,2,0:T(8,128)(2,1)}, bf16[2,1024,896]{1,2,0:T(8,128)(2,1)}, u32[]{:S(2)}, u32[]{:S(2)}) collective-permute-start(bf16[2,1024,896]{1,2,0:T(8,128)(2,1)} %copy.45), channel_id=1, source_target_pairs={{0,248},{8,0},{16,8},{24,16},{32,24},{40,32},{48,40},{56,48},{64,5... | collective-permute-start | bytes 11010056 | tf_op jit(solution)/shard_map/ppermute | solution.py:19
  38.1 1.3 copy.37
  50.7 2.2 fusion
  54.0 42.2 %collective-permute-done = bf16[2,1024,896]{1,2,0:T(8,128)(2,1)} collective-permute-done((bf16[2,1024,896]{1,2,0:T(8,128)(2,1)}, bf16[2,1024,896]{1,2,0:T(8,128)(2,1)}, u32[]{:S(2)}, u32[]{:S(2)}) %collective-permute-start) | collective-permute-done | bytes 3670048 | tf_op jit(solution)/shard_map/ppermute | solution.py:19
  96.2 1.4 collective-permute-done.1
  97.6 75.9 %collective-permute-done.2 = bf16[2,1024,896]{1,2,0:T(8,128)(2,1)} collective-permute-done((bf16[2,1024,896]{1,2,0:T(8,128)(2,1)}, bf16[2,1024,896]{1,2,0:T(8,128)(2,1)}, u32[]{:S(2)}, u32[]{:S(2)}) %collective-permute-start.2) | collective-permute-done | bytes 3670048 | tf_op jit(solution)/shard_map/ppermute | solution.py:19
  174.8 6.8 %select_select_fusion = (bf16[1,1024,896]{1,2,0:T(8,128)(2,1)S(1)}, bf16[1,1024,896]{1,2,0:T(8,128)(2,1)}, bf16[1,1024,896]{1,2,0:T(8,128)(2,1)S(1)}, bf16[1,1024,896]{1,2,0:T(8,128)(2,1)S(1)}) fusion(bf16[2,1024,896]{1,2,0:T(8,128)(2,1)} %collective-permute-done.3, s32[]{:T(128)S(6)} %select_n.268, bf16[2,1024,896]{1,2,0:T(8,128)(2,1)} %collective-permute-done.2, ...), kind=kLoop, calls=%fused_computation.26 | loop fusion | flops 7340032 | bytes 22020108 | tf_op jit(solution)/shard_map/jit(_where)/select_n | solution.py:113
  186.7 2.0 fusion.3
  193.1 8.0 %dynamic_update_slice.20 = f32[704,896]{0,1:T(8,128)S(1)} dynamic-update-slice(f32[704,896]{0,1:T(8,128)S(1)} %broadcast_in_dim.210, f32[192,896]{0,1:T(8,128)} %copy.48, s32[]{:T(128)S(6)} %select_n.254, s32[]{:T(128)} %constant.64.clone.1) | dynamic-update-slice | bytes 1376260 | tf_op jit(solution)/shard_map/dynamic_update_slice | solution.py:145
  201.2 9.0 %dynamic_update_slice.21 = f32[704,896]{0,1:T(8,128)S(1)} dynamic-update-slice(f32[704,896]{0,1:T(8,128)S(1)} %dynamic_update_slice.20, f32[192,896]{0,1:T(8,128)} %copy.50, s32[]{:T(128)S(6)} %select_n.266, s32[]{:T(128)} %constant.64.clone.1) | dynamic-update-slice | bytes 1376260 | tf_op jit(solution)/shard_map/dynamic_update_slice | solution.py:145
  210.3 1.5 slice.105
  212.9 4.6 %fusion.18 = bf16[512,4,224]{0,2,1:T(8,128)(2,1)S(1)} fusion(f32[512,4,224]{0,2,1:T(8,128)} %bitcast.78, bf16[512,4,224]{0,2,1:T(8,128)(2,1)} %bitcast.79, f32[4,512,512]{1,2,0:T(8,128)} %copy-done, f32[4,512]{1,0:T(4,128)S(1)} %get-tuple-element.42, pred[512,512]{0,1:T(8,128)(4,1)S(1)} %copy-done.8, f32[512,4]{0,1:T(4,128)S(1)} %get-tuple-element.3, ...), kind=kOutput, calls=%fused_computation.25 | convolution fusion | flops 477298688 | bytes 8159232 | tf_op jit(solution)/shard_map/hts,shd->thd/dot_general | solution.py:35
  217.5 8.5 %convolution_convert_fusion = bf16[512,3584]{1,0:T(8,128)(2,1)} fusion(bf16[512,896]{0,1:T(8,128)(2,1)S(1)} %bitcast.84, bf16[896,3584]{1,0:T(8,128)(2,1)} %param.15), kind=kOutput, calls=%fused_computation | convolution fusion | flops 3290169344 | bytes 11010048 | tf_op jit(solution)/shard_map/dot_general | solution.py:169
  226.0 2.7 broadcast_select_fusion.5
  228.7 5.7 %collective-permute-start.4 = (s32[3]{0:T(128)S(1)}, s32[3]{0:T(128)S(1)}, u32[]{:S(2)}, u32[]{:S(2)}) collective-permute-start(s32[3]{0:T(128)S(1)} %broadcast_select_fusion.5), channel_id=1, source_target_pairs={{0,248},{8,0},{16,8},{24,16},{32,24},{40,32},{48,40},{56,48},{64,5... | collective-permute-start | bytes 44 | tf_op jit(solution)/shard_map/ppermute | solution.py:19
  235.6 5.2 %collective-permute-start.5 = (bf16[192,896]{1,0:T(8,128)(2,1)S(1)}, bf16[192,896]{1,0:T(8,128)(2,1)S(1)}, u32[]{:S(2)}, u32[]{:S(2)}) collective-permute-start(bf16[192,896]{1,0:T(8,128)(2,1)S(1)} %get-tuple-element.19), channel_id=1, source_target_pairs={{0,248},{8,0},{16,8},{24,16},{32,24},{40,32},{48,40},{56,48},{64,5... | collective-permute-start | bytes 1032200 | tf_op jit(solution)/shard_map/ppermute | solution.py:19
  240.9 2.0 collective-permute-start.8
  242.9 2.6 broadcast_select_fusion.3
  246.8 9.9 %collective-permute-done.6 = s32[3]{0:T(128)S(1)} collective-permute-done((s32[3]{0:T(128)S(1)}, s32[3]{0:T(128)S(1)}, u32[]{:S(2)}, u32[]{:S(2)}) %collective-permute-start.6) | collective-permute-done | bytes 44 | tf_op jit(solution)/shard_map/ppermute | solution.py:19
  260.5 9.8 %reduce-scatter.2.cloned.1.call-done = bf16[64,3584]{1,0:T(8,128)(2,1)} async-done(((bf16[512,3584]{1,0:T(8,128)(2,1)}), bf16[64,3584]{1,0:T(8,128)(2,1)}) %reduce-scatter.2.cloned.1.call-update) | async-done | bytes 458768 | tf_op jit(solution)/shard_map/reduce_scatter | solution.py:168
  (87 shorter events, 29.2 us)
Async XLA Ops:
  7.2 263.1 %reduce-scatter.2.cloned.1.call-start = ((), (), s32[]{:S(2)}) async-start(), calls=%async_computation.1 | async-start | bytes 4128768 | tf_op jit(solution)/shard_map/reduce_scatter | solution.py:168
  13.3 15.1 %copy-start.10 = (s32[1,2]{1,0:T(1,128)S(1)}, s32[1,2]{1,0:T(1,128)}, u32[]{:S(2)}) copy-start(s32[1,2]{1,0:T(1,128)} %param.18) | copy-start | bytes 28
  13.3 18.2 %copy-start.13 = (s32[1,2]{1,0:T(1,128)S(1)}, s32[1,2]{1,0:T(1,128)}, u32[]{:S(2)}) copy-start(s32[1,2]{1,0:T(1,128)} %param.17) | copy-start | bytes 28
  13.3 21.4 %copy-start.12 = (s32[1,4]{1,0:T(1,128)S(1)}, s32[1,4]{1,0:T(1,128)}, u32[]{:S(2)}) copy-start(s32[1,4]{1,0:T(1,128)} %param.16) | copy-start | bytes 52
  13.3 24.8 %copy-start.1 = (bf16[512,896]{1,0:T(8,128)(2,1)S(1)}, bf16[512,896]{1,0:T(8,128)(2,1)}, u32[]{:S(2)}) copy-start(bf16[512,896]{1,0:T(8,128)(2,1)} %param.10) | copy-start | bytes 2752516
  13.3 82.8 %collective-permute-start = (bf16[2,1024,896]{1,2,0:T(8,128)(2,1)}, bf16[2,1024,896]{1,2,0:T(8,128)(2,1)}, u32[]{:S(2)}, u32[]{:S(2)}) collective-permute-start(bf16[2,1024,896]{1,2,0:T(8,128)(2,1)} %copy.41), channel_id=1, source_target_pairs={{0,8},{8,16},{16,24},{24,32},{32,40},{40,48},{48,56},{56,64},{64,7... | collective-permute-start | bytes 11010056 | tf_op jit(solution)/shard_map/ppermute | solution.py:19
  15.0 82.6 %collective-permute-start.1 = (bf16[2,1024,896]{1,2,0:T(8,128)(2,1)}, bf16[2,1024,896]{1,2,0:T(8,128)(2,1)}, u32[]{:S(2)}, u32[]{:S(2)}) collective-permute-start(bf16[2,1024,896]{1,2,0:T(8,128)(2,1)} %copy.41), channel_id=1, source_target_pairs={{0,248},{8,0},{16,8},{24,16},{32,24},{40,32},{48,40},{56,48},{64,5... | collective-permute-start | bytes 11010056 | tf_op jit(solution)/shard_map/ppermute | solution.py:19
  21.8 20.8 %copy-start.4 = (bf16[512,896]{1,0:T(8,128)(2,1)S(1)}, bf16[512,896]{1,0:T(8,128)(2,1)}, u32[]{:S(2)}) copy-start(bf16[512,896]{1,0:T(8,128)(2,1)} %param.11) | copy-start | bytes 2752516
  21.8 151.6 %collective-permute-start.2 = (bf16[2,1024,896]{1,2,0:T(8,128)(2,1)}, bf16[2,1024,896]{1,2,0:T(8,128)(2,1)}, u32[]{:S(2)}, u32[]{:S(2)}) collective-permute-start(bf16[2,1024,896]{1,2,0:T(8,128)(2,1)} %copy.45), channel_id=1, source_target_pairs={{0,8},{8,16},{16,24},{24,32},{32,40},{40,48},{48,56},{56,64},{64,7... | collective-permute-start | bytes 11010056 | tf_op jit(solution)/shard_map/ppermute | solution.py:19
  23.1 151.6 %collective-permute-start.3 = (bf16[2,1024,896]{1,2,0:T(8,128)(2,1)}, bf16[2,1024,896]{1,2,0:T(8,128)(2,1)}, u32[]{:S(2)}, u32[]{:S(2)}) collective-permute-start(bf16[2,1024,896]{1,2,0:T(8,128)(2,1)} %copy.45), channel_id=1, source_target_pairs={{0,248},{8,0},{16,8},{24,16},{32,24},{40,32},{48,40},{56,48},{64,5... | collective-permute-start | bytes 11010056 | tf_op jit(solution)/shard_map/ppermute | solution.py:19
  38.1 5.9 %copy-start.2 = (bf16[512,896]{1,0:T(8,128)(2,1)S(1)}, bf16[512,896]{1,0:T(8,128)(2,1)}, u32[]{:S(2)}) copy-start(bf16[512,896]{1,0:T(8,128)(2,1)} %param.12) | copy-start | bytes 2752516
  40.8 5.8 %copy-start.11 = (s32[1,2]{1,0:T(1,128)S(1)}, s32[1,2]{1,0:T(1,128)}, u32[]{:S(2)}) copy-start(s32[1,2]{1,0:T(1,128)} %param.19) | copy-start | bytes 28
  41.2 9.5 %copy-start.9 = (bf16[512,896]{0,1:T(8,128)(2,1)S(1)}, bf16[512,896]{0,1:T(8,128)(2,1)}, u32[]{:S(2)}) copy-start(bf16[512,896]{0,1:T(8,128)(2,1)} %copy.37) | copy-start | bytes 2752516
  52.9 121.9 %copy-start = (f32[4,512,512]{1,2,0:T(8,128)}, f32[4,512,512]{1,2,0:T(8,128)S(1)}, u32[]{:S(2)}) copy-start(f32[4,512,512]{1,2,0:T(8,128)S(1)} %get-tuple-element.43) | copy-start | bytes 12582916
  186.7 2.9 %copy-start.6 = (bf16[1,1024,896]{1,2,0:T(8,128)(2,1)S(1)}, bf16[1,1024,896]{1,2,0:T(8,128)(2,1)}, u32[]{:S(2)}) copy-start(bf16[1,1024,896]{1,2,0:T(8,128)(2,1)} %get-tuple-element.9) | copy-start | bytes 5505028
  201.2 11.7 %copy-start.8 = (pred[512,512]{0,1:T(8,128)(4,1)S(1)}, pred[512,512]{0,1:T(8,128)(4,1)}, u32[]{:S(2)}) copy-start(pred[512,512]{0,1:T(8,128)(4,1)} %copy-done.7) | copy-start | bytes 786436
  226.0 8.5 %copy-start.3 = (bf16[512,896]{1,0:T(8,128)(2,1)S(1)}, bf16[512,896]{1,0:T(8,128)(2,1)}, u32[]{:S(2)}) copy-start(bf16[512,896]{1,0:T(8,128)(2,1)} %param.12) | copy-start | bytes 2752516
  226.0 8.5 %copy-start.5 = (bf16[512,896]{1,0:T(8,128)(2,1)S(1)}, bf16[512,896]{1,0:T(8,128)(2,1)}, u32[]{:S(2)}) copy-start(bf16[512,896]{1,0:T(8,128)(2,1)} %param.11) | copy-start | bytes 2752516
  228.7 16.8 %collective-permute-start.4 = (s32[3]{0:T(128)S(1)}, s32[3]{0:T(128)S(1)}, u32[]{:S(2)}, u32[]{:S(2)}) collective-permute-start(s32[3]{0:T(128)S(1)} %broadcast_select_fusion.5), channel_id=1, source_target_pairs={{0,248},{8,0},{16,8},{24,16},{32,24},{40,32},{48,40},{56,48},{64,5... | collective-permute-start | bytes 44 | tf_op jit(solution)/shard_map/ppermute | solution.py:19
  235.6 23.6 %collective-permute-start.5 = (bf16[192,896]{1,0:T(8,128)(2,1)S(1)}, bf16[192,896]{1,0:T(8,128)(2,1)S(1)}, u32[]{:S(2)}, u32[]{:S(2)}) collective-permute-start(bf16[192,896]{1,0:T(8,128)(2,1)S(1)} %get-tuple-element.19), channel_id=1, source_target_pairs={{0,248},{8,0},{16,8},{24,16},{32,24},{40,32},{48,40},{56,48},{64,5... | collective-permute-start | bytes 1032200 | tf_op jit(solution)/shard_map/ppermute | solution.py:19
  240.9 18.3 %collective-permute-start.7 = (bf16[192,896]{1,0:T(8,128)(2,1)S(1)}, bf16[192,896]{1,0:T(8,128)(2,1)S(1)}, u32[]{:S(2)}, u32[]{:S(2)}) collective-permute-start(bf16[192,896]{1,0:T(8,128)(2,1)S(1)} %get-tuple-element.18), channel_id=1, source_target_pairs={{0,8},{8,16},{16,24},{24,32},{32,40},{40,48},{48,56},{56,64},{64,7... | collective-permute-start | bytes 1032200 | tf_op jit(solution)/shard_map/ppermute | solution.py:19
  240.9 18.3 %collective-permute-start.8 = (bf16[192,896]{1,0:T(8,128)(2,1)S(1)}, bf16[192,896]{1,0:T(8,128)(2,1)S(1)}, u32[]{:S(2)}, u32[]{:S(2)}) collective-permute-start(bf16[192,896]{1,0:T(8,128)(2,1)S(1)} %get-tuple-element.10), channel_id=1, source_target_pairs={{0,248},{8,0},{16,8},{24,16},{32,24},{40,32},{48,40},{56,48},{64,5... | collective-permute-start | bytes 1032200 | tf_op jit(solution)/shard_map/ppermute | solution.py:19
  242.9 16.3 %collective-permute-start.9 = (bf16[192,896]{1,0:T(8,128)(2,1)S(1)}, bf16[192,896]{1,0:T(8,128)(2,1)S(1)}, u32[]{:S(2)}, u32[]{:S(2)}) collective-permute-start(bf16[192,896]{1,0:T(8,128)(2,1)S(1)} %get-tuple-element.11), channel_id=1, source_target_pairs={{0,8},{8,16},{16,24},{24,32},{32,40},{40,48},{48,56},{56,64},{64,7... | collective-permute-start | bytes 1032200 | tf_op jit(solution)/shard_map/ppermute | solution.py:19
  245.5 11.2 %collective-permute-start.6 = (s32[3]{0:T(128)S(1)}, s32[3]{0:T(128)S(1)}, u32[]{:S(2)}, u32[]{:S(2)}) collective-permute-start(s32[3]{0:T(128)S(1)} %broadcast_select_fusion.3), channel_id=1, source_target_pairs={{0,8},{8,16},{16,24},{24,32},{32,40},{40,48},{48,56},{56,64},{64,7... | collective-permute-start | bytes 44 | tf_op jit(solution)/shard_map/ppermute | solution.py:19
  (1 other events, 2.3 us)
Sparse Core Ops, SparseCore 0:
  226.1 44.1 reduce-scatter.1
where the time goes:
time: 278 us; the launch traced here: 277 us
  waiting for transfers between devices  141 us (51%)
  local copies, waits for them, and re-layouts  46.6 us (17%)
  between operations  26 us (9%)
  starting transfers between devices  22 us (8%)
  other arithmetic  22 us (8%)
  matrix products  20 us (7%)
    ppermute x10, waiting for transfers between devices, shifted(): return lax.ppermute(value, axis, pairs)  131 us
    ppermute x10, starting transfers between devices, shifted(): return lax.ppermute(value, axis, pairs)  22 us
    dynamic_update_slice x2, local copies, waits for them, and re-layouts, body(): lax.dynamic_update_slice_in_dim(full_numer, jnp.where(keep, results[j][0]...  17.1 us
    unnamed x33, local copies, waits for them, and re-layouts  16.3 us
    reduce_scatter x1, waiting for transfers between devices, body(): lax.psum_scatter(jnp.dot(attended, out_proj, preferred_element_type=jnp.f...  9.78 us
    dot_general x1, matrix products, body(): jnp.dot(attended, out_proj, preferred_element_type=jnp.float32)  8.49 us
    select_n x1, other arithmetic, body(): jnp.where(is_owner, lax.dynamic_index_in_dim(fetched_values, cache_slot[0...  6.84 us
    dot_general x3, matrix products, attend_part(): jnp.einsum('hts,shd->thd', weights.astype(jnp.bfloat16), value_heads, pre...  6.51 us
  transfers between devices with their start and end apart: 11, of which 6 were waited for; matrix products, arithmetic and copies ran while one was open for 11% of the time, Pallas kernels for 0%

commit v1 on v0

v1 whole, which is shorter than its diff:
```python
import math

import jax
import jax.numpy as jnp
from jax import lax
from jax.sharding import PartitionSpec as P

HD = 224
NEWCAP = 192


floor_value = -1e30


def shifted(value, axis, steps):
    count = lax.axis_size(axis)
    pairs = [(source, (source + steps) % count) for source in range(count)]
    return lax.ppermute(value, axis, pairs)


def attend_part(query_rows, key_rows, value_rows, live_mask, head_count):
    row_count = query_rows.shape[0]
    key_count = key_rows.shape[0]
    query_heads = query_rows.reshape(row_count, head_count, HD)
    key_heads = key_rows.reshape(key_count, head_count, HD)
    value_heads = value_rows.reshape(key_count, head_count, HD)
    scores = jnp.einsum(
        "thd,shd->hts", query_heads, key_heads, preferred_element_type=jnp.float32
    ) * (1.0 / math.sqrt(HD))
    scores = jnp.where(live_mask[None], scores, floor_value)
    row_top = jnp.max(scores, axis=2)
    weights = jnp.where(live_mask[None], jnp.exp(scores - row_top[:, :, None]), 0.0)
    row_total = jnp.sum(weights, axis=2)
    numerator = jnp.einsum(
        "hts,shd->thd",
        weights.astype(jnp.bfloat16),
        value_heads,
        preferred_element_type=jnp.float32,
    )
    return (numerator.reshape(row_count, head_count * HD), row_top.T, row_total.T)


def body(
    queries,
    keys_new,
    values_new,
    cache_keys,
    cache_values,
    out_proj,
    req_lengths,
    cache_owner,
    cache_slot,
    prior_len,
):
    tok_count = queries.shape[0]
    feat_width = queries.shape[1]
    head_count = feat_width // HD
    slot_count = cache_keys.shape[0]
    prior_rows = cache_keys.shape[1]
    req_lens = req_lengths[0]
    req_ends = jnp.cumsum(req_lens)
    starts = req_ends - req_lens
    positions = jnp.arange(tok_count, dtype=jnp.int32)
    row_marks = jnp.arange(NEWCAP, dtype=jnp.int32)
    prior_marks = jnp.arange(prior_rows, dtype=jnp.int32)
    req_count = lax.axis_size("req")
    req_index = lax.axis_index("req")
    raw_offset = (cache_owner[0] - req_index + req_count) % req_count
    offset = jnp.where(raw_offset == req_count - 1, -1, raw_offset)

    def request_at(distance):
        pick = offset[0] == distance
        start = jnp.where(pick, starts[0], starts[1])
        length = jnp.where(pick, req_lens[0], req_lens[1])
        slot = jnp.where(pick, cache_slot[0, 0], cache_slot[0, 1])
        prior = jnp.where(pick, prior_len[0, 0], prior_len[0, 1])
        return start, length, jnp.stack([slot, prior, length])

    def rows_of(source, start):
        return lax.dynamic_slice_in_dim(source, start, NEWCAP, 0)

    right_start, right_len, right_tag = request_at(1)
    left_start, left_len, left_tag = request_at(-1)

    from_left_q, from_left_tag = shifted(
        (rows_of(queries, right_start), right_tag), "req", 1
    )
    from_right_q, from_right_tag = shifted(
        (rows_of(queries, left_start), left_tag), "req", -1
    )

    segment = jnp.sum((positions[:, None] >= req_ends[None, :]).astype(jnp.int32), axis=1)
    own_live = (segment[:, None] == segment[None, :]) & (positions[None, :] <= positions[:, None])
    own_numer, own_top, own_total = attend_part(queries, keys_new, values_new, own_live, head_count)

    def serve(query_rows, tag):
        keys = lax.dynamic_index_in_dim(cache_keys, tag[0], 0, keepdims=False)
        values = lax.dynamic_index_in_dim(cache_values, tag[0], 0, keepdims=False)
        live_mask = jnp.broadcast_to(prior_marks[None, :] < tag[1], (NEWCAP, prior_rows))
        return attend_part(query_rows, keys, values, live_mask, head_count)

    got_right = shifted(serve(from_left_q, from_left_tag), "req", -1)
    got_left = shifted(serve(from_right_q, from_right_tag), "req", 1)

    def masked_rows(source, start, length):
        keep = (row_marks < length)[:, None]
        return jnp.where(keep, rows_of(source, start), jnp.zeros((), jnp.bfloat16))

    right_kv = (
        masked_rows(keys_new, right_start, right_len),
        masked_rows(values_new, right_start, right_len),
    )
    left_kv = (
        masked_rows(keys_new, left_start, left_len),
        masked_rows(values_new, left_start, left_len),
    )
    right_kv, left_kv, got_right, got_left = lax.optimization_barrier(
        (right_kv, left_kv, got_right, got_left)
    )
    from_left_kv = shifted(right_kv, "req", 1)
    from_right_kv = shifted(left_kv, "req", -1)

    def place(result, start, length):
        numer, top, total = result
        shift = tok_count - start
        keep = ((positions - start >= 0) & (positions - start < length))[:, None]

        def moved(x):
            padded = jnp.pad(x, ((tok_count, tok_count - NEWCAP), (0, 0)))
            return lax.dynamic_slice_in_dim(padded, shift, tok_count, 0)

        return keep, moved(numer), moved(top), moved(total)

    keep_r, numer_r, top_r, total_r = place(got_right, right_start, right_len)
    keep_l, numer_l, top_l, total_l = place(got_left, left_start, left_len)
    prior_numer = jnp.where(keep_r, numer_r, jnp.where(keep_l, numer_l, 0.0))
    prior_top = jnp.where(keep_r, top_r, jnp.where(keep_l, top_l, floor_value))
    prior_total = jnp.where(keep_r, total_r, jnp.where(keep_l, total_l, 0.0))

    both_top = jnp.maximum(own_top, prior_top)
    own_scale = jnp.exp(own_top - both_top)
    prior_scale = jnp.exp(prior_top - both_top)
    denominator = own_total * own_scale + prior_total * prior_scale
    numerator = (
        own_numer.reshape(tok_count, head_count, HD) * own_scale[:, :, None]
        + prior_numer.reshape(tok_count, head_count, HD) * prior_scale[:, :, None]
    )
    attended = (
        (numerator / denominator[:, :, None]).reshape(tok_count, feat_width).astype(jnp.bfloat16)
    )
    mixed = lax.psum_scatter(
        jnp.dot(attended, out_proj, preferred_element_type=jnp.float32).astype(jnp.bfloat16),
        "tp",
        scatter_dimension=0,
        tiled=True,
    )

    slot_ids = jnp.arange(slot_count, dtype=jnp.int32)

    def stored(from_left_rows, from_right_rows):
        at_left = (slot_ids == from_left_tag[0])[:, None, None]
        at_right = (slot_ids == from_right_tag[0])[:, None, None]
        return jnp.where(
            at_left,
            from_left_rows[None],
            jnp.where(at_right, from_right_rows[None], jnp.zeros((), jnp.bfloat16)),
        )

    new_keys = stored(from_left_kv[0], from_right_kv[0])
    new_values = stored(from_left_kv[1], from_right_kv[1])
    return (mixed, new_keys, new_values)


def solution(mesh):
    in_specs = (
        P("req", "tp"),
        P("req", "tp"),
        P("req", "tp"),
        P("req", None, "tp"),
        P("req", None, "tp"),
        P("tp", None),
        P("req", None),
        P("req", None),
        P("req", None),
        P("req", None),
    )
    out_specs = (P(("req", "tp"), None), P("req", None, "tp"), P("req", None, "tp"))
    return jax.shard_map(body, mesh=mesh, in_specs=in_specs, out_specs=out_specs, check_vma=False)
```

time: 278 us -> 175 us (0.63)
  waiting for transfers between devices: 141 us -> 32.4 us
  starting transfers between devices: 22 us -> 31 us
  other arithmetic: 22 us -> 13.7 us
    ppermute x10 -> x14, waiting for transfers between devices: 131 us -> 8.96 us  [shifted(): return lax.ppermute(value, axis, pairs)]
    dynamic_slice x1 -> x7, local copies, waits for them, and re-layouts: 0.41 us -> 23.7 us  [the longest x3 11.8 us: serve(): values = lax.dynamic_index_in_dim(cache_values, tag[0], 0, keepdims=False)]
    dynamic_update_slice x6 -> x0, local copies, waits for them, and re-layouts: 18.1 us -> none  [the longest x2 17.1 us: body(): lax.dynamic_update_slice_in_dim(full_numer, jnp.where(keep, results[j][0]...]
    reduce_scatter x1, waiting for transfers between devices: 9.78 us -> 23.4 us  [body(): lax.psum_scatter(jnp.dot(attended, out_proj, preferred_element_type=jnp.f...]
    unnamed x33 -> x45, local copies, waits for them, and re-layouts: 16.3 us -> 5.1 us
    select_n x9 -> x3, other arithmetic: 14.9 us -> 4.58 us  [the longest x1 1.81 us: body(): prior_numer = jnp.where(keep_r, numer_r, jnp.where(keep_l, numer_l, 0.0))]
    ppermute x10 -> x14, starting transfers between devices: 22 us -> 30.9 us  [shifted(): return lax.ppermute(value, axis, pairs)]
    reshape x2, local copies, waits for them, and re-layouts: 0.96 us -> 4.94 us  [attend_part(): numerator.reshape(row_count, head_count * HD)]
  transfers between devices with their start and end apart: 11 -> 15, of which waited for: 6 -> 6; matrix products, arithmetic and copies ran while one was open for 11% -> 34% of each run, Pallas kernels for 0% -> 0%
where the time goes in v1:
time: 175 us; the launch traced here: 174 us
  local copies, waits for them, and re-layouts  46.8 us (27%)
  waiting for transfers between devices  32.4 us (19%)
  starting transfers between devices  31 us (18%)
  between operations  28.5 us (16%)
  matrix products  21.6 us (12%)
  other arithmetic  13.7 us (8%)
    ppermute x14, starting transfers between devices, shifted(): return lax.ppermute(value, axis, pairs)  30.9 us
    reduce_scatter x1, waiting for transfers between devices, body(): lax.psum_scatter(jnp.dot(attended, out_proj, preferred_element_type=jnp.f...  23.4 us
    dynamic_slice x3, local copies, waits for them, and re-layouts, serve(): values = lax.dynamic_index_in_dim(cache_values, tag[0], 0, keepdims=False)  11.8 us
    dynamic_slice x3, local copies, waits for them, and re-layouts, serve(): keys = lax.dynamic_index_in_dim(cache_keys, tag[0], 0, keepdims=False)  9.93 us
    ppermute x14, waiting for transfers between devices, shifted(): return lax.ppermute(value, axis, pairs)  8.96 us
    dot_general x1, matrix products, body(): jnp.dot(attended, out_proj, preferred_element_type=jnp.float32)  8.27 us
    dot_general x3, matrix products, attend_part(): jnp.einsum('hts,shd->thd', weights.astype(jnp.bfloat16), value_heads, pre...  7.62 us
    dot_general x3, matrix products, attend_part(): jnp.einsum('thd,shd->hts', query_heads, key_heads, preferred_element_type...  5.75 us
  transfers between devices with their start and end apart: 15, of which 6 were waited for; matrix products, arithmetic and copies ran while one was open for 34% of the time, Pallas kernels for 0%

profile of v1, /device:TPU:8, one launch (start us, length us, event | category | flops | bytes accessed | tf_op | source)
XLA Modules:
  0.0 174.1 jit_solution(17197747115925881364)
XLA Ops:
  26.7 2.0 %constant_dynamic-slice_fusion.1 = (bf16[192,896]{1,0:T(8,128)(2,1)S(1)}, bf16[192,896]{1,0:T(8,128)(2,1)}) fusion(bf16[512,896]{1,0:T(8,128)(2,1)} %param.10, s32[]{:T(128)S(6)} %select_n.144, s32[]{:T(128)S(6)} %select_n.139), kind=kLoop, calls=%fused_computation.76 | loop fusion | bytes 1376264 | tf_op jit(solution)/shard_map/dynamic_slice | solution.py:80
  28.7 6.6 %collective-permute-start.6 = (bf16[192,896]{1,0:T(8,128)(2,1)S(1)}, bf16[192,896]{1,0:T(8,128)(2,1)}, u32[]{:S(2)}, u32[]{:S(2)}) collective-permute-start(bf16[192,896]{1,0:T(8,128)(2,1)S(1)} %get-tuple-element.30), channel_id=1, source_target_pairs={{0,248},{8,0},{16,8},{24,16},{32,24},{40,32},{48,40},{56,48},{64,5... | collective-permute-start | bytes 1032200 | tf_op jit(solution)/shard_map/ppermute | solution.py:18
  46.8 3.6 %constant_dynamic-slice_fusion = (bf16[1,1024,896]{2,1,0:T(8,128)(2,1)}, bf16[1,1024,896]{2,1,0:T(8,128)(2,1)S(1)}) fusion(bf16[2,1024,896]{2,1,0:T(8,128)(2,1)} %param.13, s32[]{:T(128)S(6)} %select_n.154, s32[]{:T(128)S(6)} %select_n.149), kind=kLoop, calls=%fused_computation.75 | loop fusion | bytes 7340040 | tf_op jit(solution)/shard_map/jit(dynamic_index_in_dim)/dynamic_slice | solution.py:97
  50.4 3.8 %copy.43 = bf16[1,1024,896]{1,2,0:T(8,128)(2,1)} copy(bf16[1,1024,896]{2,1,0:T(8,128)(2,1)} %get-tuple-element.26) | data formatting | bytes 3670016 | tf_op jit(solution)/shard_map/jit(dynamic_index_in_dim)/dynamic_slice | solution.py:97
  54.2 4.1 %constant_dynamic-slice_fusion.2 = (bf16[1,1024,896]{2,1,0:T(8,128)(2,1)}, bf16[1,1024,896]{2,1,0:T(8,128)(2,1)}) fusion(bf16[2,1024,896]{2,1,0:T(8,128)(2,1)} %param.14, s32[]{:T(128)S(6)} %select_n.154, s32[]{:T(128)S(6)} %select_n.149), kind=kLoop, calls=%fused_computation.77 | loop fusion | bytes 7340040 | tf_op jit(solution)/shard_map/jit(dynamic_index_in_dim)/dynamic_slice | solution.py:98
  58.4 3.8 %copy.42 = bf16[1,1024,896]{1,2,0:T(8,128)(2,1)} copy(bf16[1,1024,896]{2,1,0:T(8,128)(2,1)} %get-tuple-element.28) | data formatting | bytes 3670016 | tf_op jit(solution)/shard_map/jit(dynamic_index_in_dim)/dynamic_slice | solution.py:98
  62.2 2.5 %copy.39 = bf16[1,1024,896]{1,2,0:T(8,128)(2,1)} copy(bf16[1,1024,896]{2,1,0:T(8,128)(2,1)S(1)} %get-tuple-element.27) | data formatting | bytes 3670016 | tf_op jit(solution)/shard_map/jit(dynamic_index_in_dim)/dynamic_slice | solution.py:97
  64.7 3.8 %copy.38 = bf16[1,1024,896]{1,2,0:T(8,128)(2,1)} copy(bf16[1,1024,896]{2,1,0:T(8,128)(2,1)} %get-tuple-element.29) | data formatting | bytes 3670016 | tf_op jit(solution)/shard_map/jit(dynamic_index_in_dim)/dynamic_slice | solution.py:98
  72.4 2.3 %fusion.4 = (f32[4,192]{1,0:T(4,128)S(1)}, f32[4,192,1024]{2,1,0:T(8,128)S(1)}) fusion(pred[1024]{0:T(1024)(128)(4,1)} %iota_compare_fusion.2, bf16[1024,4,224]{0,2,1:T(8,128)(2,1)} %bitcast.72, bf16[192,4,224]{2,1,0:T(4,128)(2,1)S(1)} %reshape.190), kind=kOutput, calls=%fused_computation.13 | convolution fusion | flops 354680064 | bytes 5328896 | tf_op jit(solution)/shard_map/thd,shd->hts/dot_general | solution.py:27
  74.7 2.4 %fusion.40 = f32[192,4,224]{2,0,1:T(8,128)S(1)} fusion(bf16[1024,4,224]{0,2,1:T(8,128)(2,1)} %bitcast.74, f32[4,192,1024]{2,1,0:T(8,128)S(1)} %get-tuple-element.55, f32[4,192]{1,0:T(4,128)S(1)} %get-tuple-element.54, pred[1024]{0:T(1024)(128)(4,1)S(1)} %copy-done.19), kind=kOutput, calls=%fused_computation.43 | convolution fusion | flops 356253696 | bytes 5672960 | tf_op jit(solution)/shard_map/hts,shd->thd/dot_general | solution.py:34
  78.5 2.5 %reshape.192 = f32[192,896]{1,0:T(8,128)} reshape(f32[192,4,224]{2,1,0:T(4,128)} %copy.45) | data formatting | bytes 1376256 | tf_op jit(solution)/shard_map/reshape | solution.py:40
  82.4 2.5 %fusion.3 = (f32[4,192]{1,0:T(4,128)S(1)}, f32[4,192,1024]{2,1,0:T(8,128)S(1)}) fusion(pred[1024]{0:T(1024)(128)(4,1)} %iota_compare_fusion.3, bf16[1024,4,224]{0,2,1:T(8,128)(2,1)} %bitcast.71, bf16[192,4,224]{2,1,0:T(4,128)(2,1)S(1)} %reshape.186), kind=kOutput, calls=%fused_computation.12 | convolution fusion | flops 354680064 | bytes 5328896 | tf_op jit(solution)/shard_map/thd,shd->hts/dot_general | solution.py:27
  88.0 2.5 %reshape.188 = f32[192,896]{1,0:T(8,128)} reshape(f32[192,4,224]{2,1,0:T(4,128)} %copy.41) | data formatting | bytes 1376256 | tf_op jit(solution)/shard_map/reshape | solution.py:40
  90.4 2.0 %collective-permute-start.2 = (f32[192,896]{1,0:T(8,128)}, f32[192,896]{1,0:T(8,128)}, u32[]{:S(2)}, u32[]{:S(2)}) collective-permute-start(f32[192,896]{1,0:T(8,128)} %reshape.188), channel_id=1, source_target_pairs={{0,248},{8,0},{16,8},{24,16},{32,24},{40,32},{48,40},{56,48},{64,5... | collective-permute-start | bytes 2064392 | tf_op jit(solution)/shard_map/ppermute | solution.py:18
  94.4 5.4 %collective-permute-start.4 = (f32[192,4]{0,1:T(4,128)S(1)}, f32[192,4]{0,1:T(4,128)S(1)}, u32[]{:S(2)}, u32[]{:S(2)}) collective-permute-start(f32[192,4]{0,1:T(4,128)S(1)} %bitcast.81), channel_id=1, source_target_pairs={{0,248},{8,0},{16,8},{24,16},{32,24},{40,32},{48,40},{56,48},{64,5... | collective-permute-start | bytes 9224 | tf_op jit(solution)/shard_map/ppermute | solution.py:18
  99.8 5.3 %collective-permute-start.3 = (f32[192,4]{0,1:T(4,128)S(1)}, f32[192,4]{0,1:T(4,128)S(1)}, u32[]{:S(2)}, u32[]{:S(2)}) collective-permute-start(f32[192,4]{0,1:T(4,128)S(1)} %bitcast.80), channel_id=1, source_target_pairs={{0,248},{8,0},{16,8},{24,16},{32,24},{40,32},{48,40},{56,48},{64,5... | collective-permute-start | bytes 9224 | tf_op jit(solution)/shard_map/ppermute | solution.py:18
  108.7 1.8 %fusion.16 = f32[512,896]{1,0:T(8,128)S(1)} fusion(s32[]{:T(128)S(6)} %select_n.157, f32[192,896]{1,0:T(8,128)} %collective-permute-done.2, s32[]{:T(128)S(6)} %select_n.158, f32[192,896]{1,0:T(8,128)} %collective-permute-done.7, pred[512]{0:T(512)(128)(4,1)S(1)} %get-tuple-element.59, pred[512]{0:T(512)(128)(4,1)S(1)} %get-tuple-element.58), kind=kLoop, calls=%fused_computation.24 | loop fusion | flops 917504 | bytes 3212296 | tf_op jit(solution)/shard_map/jit(_where)/select_n | solution.py:136
  110.5 1.8 %copy.46 = f32[512,896]{0,1:T(8,128)} copy(f32[512,896]{1,0:T(8,128)S(1)} %fusion.16) | data formatting | bytes 3670016 | tf_op jit(solution)/shard_map/jit(_where)/select_n | solution.py:136
  112.4 4.3 %fusion.20 = bf16[512,4,224]{0,2,1:T(8,128)(2,1)S(1)} fusion(f32[512,4,224]{0,2,1:T(8,128)} %bitcast.75, bf16[512,4,224]{0,2,1:T(8,128)(2,1)S(1)} %bitcast.76, f32[4,512,512]{1,2,0:T(8,128)} %copy-done.2, f32[4,512]{1,0:T(4,128)S(1)} %get-tuple-element.56, pred[512,512]{0,1:T(8,128)(4,1)S(1)} %copy-done.8, f32[512,4]{0,1:T(4,128)S(1)} %get-tuple-element.23, ...), kind=kOutput, calls=%fused_computation.29 | convolution fusion | flops 477298688 | bytes 8159232 | tf_op jit(solution)/shard_map/hts,shd->thd/dot_general | solution.py:34
  116.7 8.3 %convolution_convert_fusion = bf16[512,3584]{1,0:T(8,128)(2,1)} fusion(bf16[512,896]{0,1:T(8,128)(2,1)S(1)} %bitcast.85, bf16[896,3584]{1,0:T(8,128)(2,1)} %param.15), kind=kOutput, calls=%fused_computation | convolution fusion | flops 3290169344 | bytes 11010048 | tf_op jit(solution)/shard_map/dot_general | solution.py:152
  126.1 3.9 %collective-permute-start.11 = (bf16[192,896]{1,0:T(8,128)(2,1)S(1)}, bf16[192,896]{1,0:T(8,128)(2,1)S(1)}, u32[]{:S(2)}, u32[]{:S(2)}) collective-permute-start(bf16[192,896]{1,0:T(8,128)(2,1)S(1)} %copy-done.11), channel_id=1, source_target_pairs={{0,248},{8,0},{16,8},{24,16},{32,24},{40,32},{48,40},{56,48},{64,5... | collective-permute-start | bytes 1032200 | tf_op jit(solution)/shard_map/ppermute | solution.py:18
  130.0 5.3 %collective-permute-start.13 = (bf16[192,896]{1,0:T(8,128)(2,1)S(1)}, bf16[192,896]{1,0:T(8,128)(2,1)S(1)}, u32[]{:S(2)}, u32[]{:S(2)}) collective-permute-start(bf16[192,896]{1,0:T(8,128)(2,1)S(1)} %copy-done.9), channel_id=1, source_target_pairs={{0,248},{8,0},{16,8},{24,16},{32,24},{40,32},{48,40},{56,48},{64,5... | collective-permute-start | bytes 1032200 | tf_op jit(solution)/shard_map/ppermute | solution.py:18
  137.0 5.5 %collective-permute-done.12 = bf16[192,896]{1,0:T(8,128)(2,1)S(1)} collective-permute-done((bf16[192,896]{1,0:T(8,128)(2,1)S(1)}, bf16[192,896]{1,0:T(8,128)(2,1)S(1)}, u32[]{:S(2)}, u32[]{:S(2)}) %collective-permute-start.12) | collective-permute-done | bytes 344096 | tf_op jit(solution)/shard_map/ppermute | solution.py:18
  143.8 23.4 %reduce-scatter.2.cloned.1.call-done = bf16[64,3584]{1,0:T(8,128)(2,1)} async-done(((bf16[512,3584]{1,0:T(8,128)(2,1)}), bf16[64,3584]{1,0:T(8,128)(2,1)}) %reduce-scatter.2.cloned.1.call-update) | async-done | bytes 458768 | tf_op jit(solution)/shard_map/reduce_scatter | solution.py:151
  (98 shorter events, 36.1 us)
Async XLA Ops:
  7.2 29.9 %copy-start.3 = (bf16[512,896]{1,0:T(8,128)(2,1)S(1)}, bf16[512,896]{1,0:T(8,128)(2,1)}, u32[]{:S(2)}) copy-start(bf16[512,896]{1,0:T(8,128)(2,1)} %param.11) | copy-start | bytes 2752516
  7.2 160.1 %reduce-scatter.2.cloned.1.call-start = ((), (), s32[]{:S(2)}) async-start(), calls=%async_computation.1 | async-start | bytes 4128768 | tf_op jit(solution)/shard_map/reduce_scatter | solution.py:151
  19.8 22.2 %collective-permute-start = (s32[3]{0:T(128)S(1)}, s32[3]{0:T(128)S(1)}, u32[]{:S(2)}, u32[]{:S(2)}) collective-permute-start(s32[3]{0:T(128)S(1)} %get-tuple-element.60), channel_id=1, source_target_pairs={{0,8},{8,16},{16,24},{24,32},{32,40},{40,48},{48,56},{56,64},{64,7... | collective-permute-start | bytes 44 | tf_op jit(solution)/shard_map/ppermute | solution.py:18
  21.4 22.4 %collective-permute-start.5 = (s32[3]{0:T(128)S(1)}, s32[3]{0:T(128)S(1)}, u32[]{:S(2)}, u32[]{:S(2)}) collective-permute-start(s32[3]{0:T(128)S(1)} %get-tuple-element.61), channel_id=1, source_target_pairs={{0,248},{8,0},{16,8},{24,16},{32,24},{40,32},{48,40},{56,48},{64,5... | collective-permute-start | bytes 44 | tf_op jit(solution)/shard_map/ppermute | solution.py:18
  28.7 42.3 %collective-permute-start.6 = (bf16[192,896]{1,0:T(8,128)(2,1)S(1)}, bf16[192,896]{1,0:T(8,128)(2,1)}, u32[]{:S(2)}, u32[]{:S(2)}) collective-permute-start(bf16[192,896]{1,0:T(8,128)(2,1)S(1)} %get-tuple-element.30), channel_id=1, source_target_pairs={{0,248},{8,0},{16,8},{24,16},{32,24},{40,32},{48,40},{56,48},{64,5... | collective-permute-start | bytes 1032200 | tf_op jit(solution)/shard_map/ppermute | solution.py:18
  35.3 45.7 %collective-permute-start.1 = (bf16[192,896]{1,0:T(8,128)(2,1)}, bf16[192,896]{1,0:T(8,128)(2,1)}, u32[]{:S(2)}, u32[]{:S(2)}) collective-permute-start(bf16[192,896]{1,0:T(8,128)(2,1)} %get-tuple-element.31), channel_id=1, source_target_pairs={{0,8},{8,16},{16,24},{24,32},{32,40},{40,48},{48,56},{56,64},{64,7... | collective-permute-start | bytes 1032200 | tf_op jit(solution)/shard_map/ppermute | solution.py:18
  81.0 27.7 %collective-permute-start.7 = (f32[192,896]{1,0:T(8,128)}, f32[192,896]{1,0:T(8,128)}, u32[]{:S(2)}, u32[]{:S(2)}) collective-permute-start(f32[192,896]{1,0:T(8,128)} %reshape.192), channel_id=1, source_target_pairs={{0,8},{8,16},{16,24},{24,32},{32,40},{40,48},{48,56},{56,64},{64,7... | collective-permute-start | bytes 2064392 | tf_op jit(solution)/shard_map/ppermute | solution.py:18
  84.9 7.6 %copy-start.14 = (f32[4,192]{1,0:T(4,128)S(1)}, f32[4,192]{1,0:T(4,128)}, u32[]{:S(2)}) copy-start(f32[4,192]{1,0:T(4,128)} %copy-done.13) | copy-start | bytes 9220
  84.9 7.6 %copy-start.20 = (pred[1024]{0:T(1024)(128)(4,1)S(1)}, pred[1024]{0:T(1024)(128)(4,1)}, u32[]{:S(2)}) copy-start(pred[1024]{0:T(1024)(128)(4,1)} %iota_compare_fusion.2) | copy-start | bytes 3076
  86.5 6.9 %copy-start.18 = (pred[1024]{0:T(1024)(128)(4,1)S(1)}, pred[1024]{0:T(1024)(128)(4,1)}, u32[]{:S(2)}) copy-start(pred[1024]{0:T(1024)(128)(4,1)} %iota_compare_fusion.3) | copy-start | bytes 3076
  87.9 5.5 %copy-start.16 = (f32[4,192]{1,0:T(4,128)S(1)}, f32[4,192]{1,0:T(4,128)}, u32[]{:S(2)}) copy-start(f32[4,192]{1,0:T(4,128)} %copy-done.15) | copy-start | bytes 9220
  90.4 18.3 %collective-permute-start.2 = (f32[192,896]{1,0:T(8,128)}, f32[192,896]{1,0:T(8,128)}, u32[]{:S(2)}, u32[]{:S(2)}) collective-permute-start(f32[192,896]{1,0:T(8,128)} %reshape.188), channel_id=1, source_target_pairs={{0,248},{8,0},{16,8},{24,16},{32,24},{40,32},{48,40},{56,48},{64,5... | collective-permute-start | bytes 2064392 | tf_op jit(solution)/shard_map/ppermute | solution.py:18
  93.3 11.8 %copy-start.5 = (bf16[512,896]{1,0:T(8,128)(2,1)S(1)}, bf16[512,896]{1,0:T(8,128)(2,1)}, u32[]{:S(2)}) copy-start(bf16[512,896]{1,0:T(8,128)(2,1)} %param.12) | copy-start | bytes 2752516
  93.3 11.7 %collective-permute-start.9 = (f32[192,4]{0,1:T(4,128)S(1)}, f32[192,4]{0,1:T(4,128)S(1)}, u32[]{:S(2)}, u32[]{:S(2)}) collective-permute-start(f32[192,4]{0,1:T(4,128)S(1)} %bitcast.82), channel_id=1, source_target_pairs={{0,8},{8,16},{16,24},{24,32},{32,40},{40,48},{48,56},{56,64},{64,7... | collective-permute-start | bytes 9224 | tf_op jit(solution)/shard_map/ppermute | solution.py:18
  94.4 13.1 %collective-permute-start.4 = (f32[192,4]{0,1:T(4,128)S(1)}, f32[192,4]{0,1:T(4,128)S(1)}, u32[]{:S(2)}, u32[]{:S(2)}) collective-permute-start(f32[192,4]{0,1:T(4,128)S(1)} %bitcast.81), channel_id=1, source_target_pairs={{0,248},{8,0},{16,8},{24,16},{32,24},{40,32},{48,40},{56,48},{64,5... | collective-permute-start | bytes 9224 | tf_op jit(solution)/shard_map/ppermute | solution.py:18
  99.8 7.7 %collective-permute-start.3 = (f32[192,4]{0,1:T(4,128)S(1)}, f32[192,4]{0,1:T(4,128)S(1)}, u32[]{:S(2)}, u32[]{:S(2)}) collective-permute-start(f32[192,4]{0,1:T(4,128)S(1)} %bitcast.80), channel_id=1, source_target_pairs={{0,248},{8,0},{16,8},{24,16},{32,24},{40,32},{48,40},{56,48},{64,5... | collective-permute-start | bytes 9224 | tf_op jit(solution)/shard_map/ppermute | solution.py:18
  105.1 3.6 %collective-permute-start.8 = (f32[192,4]{0,1:T(4,128)S(1)}, f32[192,4]{0,1:T(4,128)S(1)}, u32[]{:S(2)}, u32[]{:S(2)}) collective-permute-start(f32[192,4]{0,1:T(4,128)S(1)} %bitcast.79), channel_id=1, source_target_pairs={{0,8},{8,16},{16,24},{24,32},{32,40},{40,48},{48,56},{56,64},{64,7... | collective-permute-start | bytes 9224 | tf_op jit(solution)/shard_map/ppermute | solution.py:18
  108.7 3.7 %copy-start.8 = (pred[512,512]{0,1:T(8,128)(4,1)S(1)}, pred[512,512]{0,1:T(8,128)(4,1)}, u32[]{:S(2)}) copy-start(pred[512,512]{0,1:T(8,128)(4,1)} %copy-done.7) | copy-start | bytes 786436
  125.0 5.0 %copy-start.10 = (bf16[192,896]{1,0:T(8,128)(2,1)S(1)}, bf16[192,896]{1,0:T(8,128)(2,1)}, u32[]{:S(2)}) copy-start(bf16[192,896]{1,0:T(8,128)(2,1)} %get-tuple-element.21) | copy-start | bytes 1032196
  125.0 5.0 %copy-start.9 = (bf16[192,896]{1,0:T(8,128)(2,1)S(1)}, bf16[192,896]{1,0:T(8,128)(2,1)}, u32[]{:S(2)}) copy-start(bf16[192,896]{1,0:T(8,128)(2,1)} %get-tuple-element.22) | copy-start | bytes 1032196
  126.0 10.8 %collective-permute-start.10 = (bf16[192,896]{1,0:T(8,128)(2,1)S(1)}, bf16[192,896]{1,0:T(8,128)(2,1)S(1)}, u32[]{:S(2)}, u32[]{:S(2)}) collective-permute-start(bf16[192,896]{1,0:T(8,128)(2,1)S(1)} %copy-done.12), channel_id=1, source_target_pairs={{0,8},{8,16},{16,24},{24,32},{32,40},{40,48},{48,56},{56,64},{64,7... | collective-permute-start | bytes 1032200 | tf_op jit(solution)/shard_map/ppermute | solution.py:18
  126.1 10.9 %collective-permute-start.11 = (bf16[192,896]{1,0:T(8,128)(2,1)S(1)}, bf16[192,896]{1,0:T(8,128)(2,1)S(1)}, u32[]{:S(2)}, u32[]{:S(2)}) collective-permute-start(bf16[192,896]{1,0:T(8,128)(2,1)S(1)} %copy-done.11), channel_id=1, source_target_pairs={{0,248},{8,0},{16,8},{24,16},{32,24},{40,32},{48,40},{56,48},{64,5... | collective-permute-start | bytes 1032200 | tf_op jit(solution)/shard_map/ppermute | solution.py:18
  130.0 12.5 %collective-permute-start.12 = (bf16[192,896]{1,0:T(8,128)(2,1)S(1)}, bf16[192,896]{1,0:T(8,128)(2,1)S(1)}, u32[]{:S(2)}, u32[]{:S(2)}) collective-permute-start(bf16[192,896]{1,0:T(8,128)(2,1)S(1)} %copy-done.10), channel_id=1, source_target_pairs={{0,8},{8,16},{16,24},{24,32},{32,40},{40,48},{48,56},{56,64},{64,7... | collective-permute-start | bytes 1032200 | tf_op jit(solution)/shard_map/ppermute | solution.py:18
  130.0 12.5 %collective-permute-start.13 = (bf16[192,896]{1,0:T(8,128)(2,1)S(1)}, bf16[192,896]{1,0:T(8,128)(2,1)S(1)}, u32[]{:S(2)}, u32[]{:S(2)}) collective-permute-start(bf16[192,896]{1,0:T(8,128)(2,1)S(1)} %copy-done.9), channel_id=1, source_target_pairs={{0,248},{8,0},{16,8},{24,16},{32,24},{40,32},{48,40},{56,48},{64,5... | collective-permute-start | bytes 1032200 | tf_op jit(solution)/shard_map/ppermute | solution.py:18
  (12 other events, 25.0 us)
Sparse Core Ops, SparseCore 0:
  125.2 42.0 reduce-scatter.1

commit v2 on v1

--- a/solution.py
+++ b/solution.py
@@ -10,6 +10,8 @@
 
 
 floor_value = -1e30
+TAG_ROWS = 8
+RESULT_WIDTH = 1024
 
 
 def shifted(value, axis, steps):
@@ -74,51 +76,73 @@
         length = jnp.where(pick, req_lens[0], req_lens[1])
         slot = jnp.where(pick, cache_slot[0, 0], cache_slot[0, 1])
         prior = jnp.where(pick, prior_len[0, 0], prior_len[0, 1])
-        return start, length, jnp.stack([slot, prior, length])
+        return start, length, slot, prior
 
     def rows_of(source, start):
         return lax.dynamic_slice_in_dim(source, start, NEWCAP, 0)
 
-    right_start, right_len, right_tag = request_at(1)
-    left_start, left_len, left_tag = request_at(-1)
-
-    from_left_q, from_left_tag = shifted(
-        (rows_of(queries, right_start), right_tag), "req", 1
-    )
-    from_right_q, from_right_tag = shifted(
-        (rows_of(queries, left_start), left_tag), "req", -1
-    )
+    def query_bundle(start, length, slot, prior):
+        tag = jnp.stack([slot, prior // 32, prior % 32, length]).astype(jnp.bfloat16)
+        tag_rows = jnp.zeros((TAG_ROWS, feat_width), jnp.bfloat16).at[0, :4].set(tag)
+        return jnp.concatenate([rows_of(queries, start), tag_rows], axis=0)
+
+    def read_tag(bundle):
+        tag = bundle[NEWCAP, :4].astype(jnp.float32).astype(jnp.int32)
+        return tag[0], tag[1] * 32 + tag[2], tag[3]
+
+    right_start, right_len, right_slot, right_prior = request_at(1)
+    left_start, left_len, left_slot, left_prior = request_at(-1)
+
+    from_left = shifted(query_bundle(right_start, right_len, right_slot, right_prior), "req", 1)
+    from_right = shifted(query_bundle(left_start, left_len, left_slot, left_prior), "req", -1)
 
     segment = jnp.sum((positions[:, None] >= req_ends[None, :]).astype(jnp.int32), axis=1)
     own_live = (segment[:, None] == segment[None, :]) & (positions[None, :] <= positions[:, None])
     own_numer, own_top, own_total = attend_part(queries, keys_new, values_new, own_live, head_count)
 
-    def serve(query_rows, tag):
-        keys = lax.dynamic_index_in_dim(cache_keys, tag[0], 0, keepdims=False)
-        values = lax.dynamic_index_in_dim(cache_values, tag[0], 0, keepdims=False)
-        live_mask = jnp.broadcast_to(prior_marks[None, :] < tag[1], (NEWCAP, prior_rows))
-        return attend_part(query_rows, keys, values, live_mask, head_count)
-
-    got_right = shifted(serve(from_left_q, from_left_tag), "req", -1)
-    got_left = shifted(serve(from_right_q, from_right_tag), "req", 1)
+    left_tag = read_tag(from_left)
+    right_tag = read_tag(from_right)
+    left_is_zero = left_tag[0] == 0
+    served = []
+    for s in range(slot_count):
+        mine = left_is_zero if s == 0 else jnp.logical_not(left_is_zero)
+        query_rows = jnp.where(mine, from_left[:NEWCAP], from_right[:NEWCAP])
+        prior = jnp.where(mine, left_tag[1], right_tag[1])
+        live_mask = jnp.broadcast_to(prior_marks[None, :] < prior, (NEWCAP, prior_rows))
+        numer, top, total = attend_part(
+            query_rows, cache_keys[s], cache_values[s], live_mask, head_count
+        )
+        pad = jnp.zeros((NEWCAP, RESULT_WIDTH - feat_width - 2 * head_count), jnp.float32)
+        served.append(jnp.concatenate([numer, top, total, pad], axis=1))
+    back_left = jnp.where(left_is_zero, served[0], served[1])
+    back_right = jnp.where(left_is_zero, served[1], served[0])
+    got_right = shifted(back_left, "req", -1)
+    got_left = shifted(back_right, "req", 1)
 
     def masked_rows(source, start, length):
         keep = (row_marks < length)[:, None]
         return jnp.where(keep, rows_of(source, start), jnp.zeros((), jnp.bfloat16))
 
-    right_kv = (
-        masked_rows(keys_new, right_start, right_len),
-        masked_rows(values_new, right_start, right_len),
-    )
-    left_kv = (
-        masked_rows(keys_new, left_start, left_len),
-        masked_rows(values_new, left_start, left_len),
+    right_kv = jnp.stack(
+        [masked_rows(keys_new, right_start, right_len), masked_rows(values_new, right_start, right_len)]
+    )
+    left_kv = jnp.stack(
+        [masked_rows(keys_new, left_start, left_len), masked_rows(values_new, left_start, left_len)]
     )
     right_kv, left_kv, got_right, got_left = lax.optimization_barrier(
         (right_kv, left_kv, got_right, got_left)
     )
     from_left_kv = shifted(right_kv, "req", 1)
     from_right_kv = shifted(left_kv, "req", -1)
+
+    def split_result(result):
+        numer = result[:, :feat_width]
+        top = result[:, feat_width : feat_width + head_count]
+        total = result[:, feat_width + head_count : feat_width + 2 * head_count]
+        return numer, top, total
+
+    got_right = split_result(got_right)
+    got_left = split_result(got_left)
 
     def place(result, start, length):
         numer, top, total = result
@@ -158,8 +182,8 @@
     slot_ids = jnp.arange(slot_count, dtype=jnp.int32)
 
     def stored(from_left_rows, from_right_rows):
-        at_left = (slot_ids == from_left_tag[0])[:, None, None]
-        at_right = (slot_ids == from_right_tag[0])[:, None, None]
+        at_left = (slot_ids == left_tag[0])[:, None, None]
+        at_right = (slot_ids == right_tag[0])[:, None, None]
         return jnp.where(
             at_left,
             from_left_rows[None],

time: 175 us -> 167 us (0.954)
  starting transfers between devices: 31 us -> 14.5 us
  waiting for transfers between devices: 32.4 us -> 44 us
  matrix products: 21.6 us -> 18.9 us
    slice x2 -> x12, local copies, waits for them, and re-layouts: 1.17 us -> 23 us  [the longest x3 10.1 us: body(): cache_keys[s]]
    dynamic_slice x6 -> x0, local copies, waits for them, and re-layouts: 21.7 us -> none  [the longest x3 11.8 us: serve(): values = lax.dynamic_index_in_dim(cache_values, tag[0], 0, keepdims=False)]
    ppermute x14 -> x6, waiting for transfers between devices: 8.96 us -> 25.5 us  [shifted(): return lax.ppermute(value, axis, pairs)]
    ppermute x14 -> x6, starting transfers between devices: 30.9 us -> 14.4 us  [shifted(): return lax.ppermute(value, axis, pairs)]
    reduce_scatter x1, waiting for transfers between devices: 23.4 us -> 18.5 us  [body(): lax.psum_scatter(jnp.dot(attended, out_proj, preferred_element_type=jnp.f...]
    reshape x2, local copies, waits for them, and re-layouts: 4.94 us -> 0.97 us  [attend_part(): numerator.reshape(row_count, head_count * HD)]
    unnamed x45 -> x29, local copies, waits for them, and re-layouts: 5.1 us -> 8.9 us
    optimization_barrier x0 -> x2, local copies, waits for them, and re-layouts: none -> 2.65 us  [body(): lax.optimization_barrier((right_kv, left_kv, got_right, got_left))]
  transfers between devices with their start and end apart: 15 -> 7, of which waited for: 6 -> 4; matrix products, arithmetic and copies ran while one was open for 34% -> 22% of each run, Pallas kernels for 0% -> 0%
where the time goes in v2:
time: 167 us
  local copies, waits for them, and re-layouts  46.6 us (28%)
  waiting for transfers between devices  44 us (26%)
  between operations  28 us (17%)
  matrix products  18.9 us (11%)
  other arithmetic  14.6 us (9%)
  starting transfers between devices  14.5 us (9%)
    ppermute x6, waiting for transfers between devices, shifted(): return lax.ppermute(value, axis, pairs)  25.5 us
    reduce_scatter x1, waiting for transfers between devices, body(): lax.psum_scatter(jnp.dot(attended, out_proj, preferred_element_type=jnp.f...  18.5 us
    ppermute x6, starting transfers between devices, shifted(): return lax.ppermute(value, axis, pairs)  14.4 us
    slice x3, local copies, waits for them, and re-layouts, body(): cache_keys[s]  10.1 us
    slice x3, local copies, waits for them, and re-layouts, body(): cache_values[s]  10 us
    unnamed x29, local copies, waits for them, and re-layouts  8.9 us
    dot_general x1, matrix products, body(): jnp.dot(attended, out_proj, preferred_element_type=jnp.float32)  8.28 us
    dot_general x3, matrix products, attend_part(): jnp.einsum('hts,shd->thd', weights.astype(jnp.bfloat16), value_heads, pre...  6.46 us
  transfers between devices with their start and end apart: 7, of which 4 were waited for; matrix products, arithmetic and copies ran while one was open for 22% of the time, Pallas kernels for 0%

profile of v2, /device:TPU:8, one launch (start us, length us, event | category | flops | bytes accessed | tf_op | source)
XLA Modules:
  0.0 166.5 jit_solution(3762542558114150693)
XLA Ops:
  10.5 1.4 fusion.109
  22.0 1.7 collective-permute-start
  28.3 3.7 %fusion.102 = (bf16[1,1024,896]{2,1,0:T(8,128)(2,1)}, bf16[1,1024,896]{2,1,0:T(8,128)(2,1)S(1)}) fusion(bf16[2,1024,896]{2,1,0:T(8,128)(2,1)} %param.17), kind=kLoop, calls=%fused_computation.148 | loop fusion | bytes 7340032 | tf_op jit(solution)/shard_map/slice | solution.py:113
  32.0 2.2 %fusion.101 = (bf16[1,1024,896]{2,1,0:T(8,128)(2,1)}, bf16[1,1024,896]{2,1,0:T(8,128)(2,1)}) fusion(bf16[2,1024,896]{2,1,0:T(8,128)(2,1)S(1)} %copy-done.3), kind=kLoop, calls=%fused_computation.147 | loop fusion | bytes 7340032 | tf_op jit(solution)/shard_map/slice | solution.py:113
  38.3 2.3 %copy.78 = bf16[512,896]{0,1:T(8,128)(2,1)} copy(bf16[512,896]{1,0:T(8,128)(2,1)} %param.15) | data formatting | bytes 1835008 | tf_op args[1]
  40.6 2.3 %copy.79 = bf16[512,896]{0,1:T(8,128)(2,1)} copy(bf16[512,896]{1,0:T(8,128)(2,1)} %param.16) | data formatting | bytes 1835008 | tf_op args[2]
  42.9 3.8 %copy.81 = bf16[1,1024,896]{1,2,0:T(8,128)(2,1)} copy(bf16[1,1024,896]{2,1,0:T(8,128)(2,1)} %get-tuple-element.40) | data formatting | bytes 3670016 | tf_op jit(solution)/shard_map/slice | solution.py:113
  46.7 3.8 %copy.83 = bf16[1,1024,896]{1,2,0:T(8,128)(2,1)} copy(bf16[1,1024,896]{2,1,0:T(8,128)(2,1)} %get-tuple-element.38) | data formatting | bytes 3670016 | tf_op jit(solution)/shard_map/slice | solution.py:113
  50.5 2.5 %copy.87 = bf16[1,1024,896]{1,2,0:T(8,128)(2,1)} copy(bf16[1,1024,896]{2,1,0:T(8,128)(2,1)S(1)} %get-tuple-element.41) | data formatting | bytes 3670016 | tf_op jit(solution)/shard_map/slice | solution.py:113
  53.0 4.0 %copy.89 = bf16[1,1024,896]{1,2,0:T(8,128)(2,1)} copy(bf16[1,1024,896]{2,1,0:T(8,128)(2,1)} %get-tuple-element.39) | data formatting | bytes 3670016 | tf_op jit(solution)/shard_map/slice | solution.py:113
  62.9 1.9 %broadcast_select_fusion.1 = (bf16[192,896]{1,0:T(8,128)(2,1)S(1)}, bf16[192,896]{1,0:T(8,128)(2,1)}) fusion(pred[]{:T(512)S(6)} %eq.72, bf16[200,896]{1,0:T(8,128)(2,1)} %collective-permute-done.1, bf16[200,896]{1,0:T(8,128)(2,1)} %collective-permute-done, pred[]{:T(512)S(6)} %not.3), kind=kLoop, calls=%fused_computation.69 | loop fusion | flops 344064 | bytes 1376258 | tf_op jit(solution)/shard_map/jit(_where)/select_n | solution.py:109
  69.2 1.3 reshape.337
  74.7 6.8 %collective-permute-start.2 = (f32[192,1024]{1,0:T(8,128)S(1)}, f32[192,1024]{1,0:T(8,128)S(1)}, u32[]{:S(2)}, u32[]{:S(2)}) collective-permute-start(f32[192,1024]{1,0:T(8,128)S(1)} %get-tuple-element.43), channel_id=1, source_target_pairs={{0,248},{8,0},{16,8},{24,16},{32,24},{40,32},{48,40},{56,48},{64,5... | collective-permute-start | bytes 2359304 | tf_op jit(solution)/shard_map/ppermute | solution.py:20
  81.6 2.4 %fusion = (f32[4,512]{1,0:T(4,128)S(1)}, f32[4,512,512]{1,2,0:T(8,128)S(1)}) fusion(pred[512,512]{0,1:T(8,128)(4,1)S(1)} %copy-done.9, bf16[512,4,224]{0,2,1:T(8,128)(2,1)} %bitcast.95, bf16[512,4,224]{0,2,1:T(8,128)(2,1)} %bitcast.96), kind=kOutput, calls=%fused_computation.3 | convolution fusion | flops 472905728 | bytes 6299648 | tf_op jit(solution)/shard_map/thd,shd->hts/dot_general | solution.py:29
  84.0 1.9 %copy-done.2 = f32[4,512,512]{1,2,0:T(8,128)} copy-done((f32[4,512,512]{1,2,0:T(8,128)}, f32[4,512,512]{1,2,0:T(8,128)S(1)}, u32[]{:S(2)}) %copy-start.2) | copy-done | bytes 4194328
  87.0 11.1 %collective-permute-done.2 = f32[192,1024]{1,0:T(8,128)S(1)} collective-permute-done((f32[192,1024]{1,0:T(8,128)S(1)}, f32[192,1024]{1,0:T(8,128)S(1)}, u32[]{:S(2)}, u32[]{:S(2)}) %collective-permute-start.2) | collective-permute-done | bytes 786464 | tf_op jit(solution)/shard_map/ppermute | solution.py:20
  98.1 2.2 %collective-permute-done.3 = f32[192,1024]{1,0:T(8,128)S(1)} collective-permute-done((f32[192,1024]{1,0:T(8,128)S(1)}, f32[192,1024]{1,0:T(8,128)S(1)}, u32[]{:S(2)}, u32[]{:S(2)}) %collective-permute-start.3) | collective-permute-done | bytes 786464 | tf_op jit(solution)/shard_map/ppermute | solution.py:20
  101.7 1.3 copy.94
  105.2 1.8 %copy.95 = f32[512,896]{0,1:T(8,128)} copy(f32[512,896]{1,0:T(8,128)S(1)} %fusion.16) | data formatting | bytes 3670016 | tf_op jit(solution)/shard_map/jit(_where)/select_n | solution.py:160
  107.1 4.6 %fusion.20 = bf16[512,4,224]{0,2,1:T(8,128)(2,1)S(1)} fusion(f32[512,4,224]{0,2,1:T(8,128)} %bitcast.93, bf16[512,4,224]{0,2,1:T(8,128)(2,1)} %bitcast.94, f32[4,512,512]{1,2,0:T(8,128)} %copy-done.2, f32[4,512]{1,0:T(4,128)S(1)} %get-tuple-element.82, pred[512,512]{0,1:T(8,128)(4,1)S(1)} %copy-done.10, f32[512,4]{0,1:T(4,128)S(1)} %get-tuple-element.35, ...), kind=kOutput, calls=%fused_computation.29 | convolution fusion | flops 477298688 | bytes 8159232 | tf_op jit(solution)/shard_map/hts,shd->thd/dot_general | solution.py:36
  111.6 8.3 %convolution_convert_fusion = bf16[512,3584]{1,0:T(8,128)(2,1)} fusion(bf16[512,896]{0,1:T(8,128)(2,1)S(1)} %bitcast.103, bf16[896,3584]{1,0:T(8,128)(2,1)} %param.19), kind=kOutput, calls=%fused_computation | convolution fusion | flops 3290169344 | bytes 11010048 | tf_op jit(solution)/shard_map/dot_general | solution.py:176
  121.3 5.0 %collective-permute-start.5 = (bf16[2,192,896]{2,1,0:T(8,128)(2,1)S(1)}, bf16[2,192,896]{2,1,0:T(8,128)(2,1)S(1)}, u32[]{:S(2)}, u32[]{:S(2)}) collective-permute-start(bf16[2,192,896]{2,1,0:T(8,128)(2,1)S(1)} %copy-done.11), channel_id=1, source_target_pairs={{0,248},{8,0},{16,8},{24,16},{32,24},{40,32},{48,40},{56,48},{64,5... | collective-permute-start | bytes 2064392 | tf_op jit(solution)/shard_map/ppermute | solution.py:20
  127.5 12.2 %collective-permute-done.4 = bf16[2,192,896]{2,1,0:T(8,128)(2,1)S(1)} collective-permute-done((bf16[2,192,896]{2,1,0:T(8,128)(2,1)S(1)}, bf16[2,192,896]{2,1,0:T(8,128)(2,1)S(1)}, u32[]{:S(2)}, u32[]{:S(2)}) %collective-permute-start.4) | collective-permute-done | bytes 688160 | tf_op jit(solution)/shard_map/ppermute | solution.py:20
  141.2 18.5 %reduce-scatter.2.cloned.1.call-done = bf16[64,3584]{1,0:T(8,128)(2,1)} async-done(((bf16[512,3584]{1,0:T(8,128)(2,1)}), bf16[64,3584]{1,0:T(8,128)(2,1)}) %reduce-scatter.2.cloned.1.call-update) | async-done | bytes 458768 | tf_op jit(solution)/shard_map/reduce_scatter | solution.py:175
  (88 shorter events, 31.6 us)
Async XLA Ops:
  7.2 152.5 %reduce-scatter.2.cloned.1.call-start = ((), (), s32[]{:S(2)}) async-start(), calls=%async_computation.1 | async-start | bytes 4128768 | tf_op jit(solution)/shard_map/reduce_scatter | solution.py:175
  22.0 35.1 %collective-permute-start = (bf16[200,896]{1,0:T(8,128)(2,1)S(1)}, bf16[200,896]{1,0:T(8,128)(2,1)}, u32[]{:S(2)}, u32[]{:S(2)}) collective-permute-start(bf16[200,896]{1,0:T(8,128)(2,1)S(1)} %pad_maximum_fusion.2), channel_id=1, source_target_pairs={{0,8},{8,16},{16,24},{24,32},{32,40},{40,48},{48,56},{56,64},{64,7... | collective-permute-start | bytes 1075208 | tf_op jit(solution)/shard_map/ppermute | solution.py:20
  27.6 30.8 %collective-permute-start.1 = (bf16[200,896]{1,0:T(8,128)(2,1)S(1)}, bf16[200,896]{1,0:T(8,128)(2,1)}, u32[]{:S(2)}, u32[]{:S(2)}) collective-permute-start(bf16[200,896]{1,0:T(8,128)(2,1)S(1)} %pad_maximum_fusion.3), channel_id=1, source_target_pairs={{0,248},{8,0},{16,8},{24,16},{32,24},{40,32},{48,40},{56,48},{64,5... | collective-permute-start | bytes 1075208 | tf_op jit(solution)/shard_map/ppermute | solution.py:20
  28.3 3.7 %copy-start.3 = (bf16[2,1024,896]{2,1,0:T(8,128)(2,1)S(1)}, bf16[2,1024,896]{2,1,0:T(8,128)(2,1)}, u32[]{:S(2)}) copy-start(bf16[2,1024,896]{2,1,0:T(8,128)(2,1)} %param.18) | copy-start | bytes 11010052
  32.0 2.2 %copy-start.5 = (bf16[512,896]{1,0:T(8,128)(2,1)S(1)}, bf16[512,896]{1,0:T(8,128)(2,1)}, u32[]{:S(2)}) copy-start(bf16[512,896]{1,0:T(8,128)(2,1)} %param.15) | copy-start | bytes 2752516
  32.0 2.2 %copy-start.6 = (bf16[512,896]{1,0:T(8,128)(2,1)S(1)}, bf16[512,896]{1,0:T(8,128)(2,1)}, u32[]{:S(2)}) copy-start(bf16[512,896]{1,0:T(8,128)(2,1)} %param.16) | copy-start | bytes 2752516
  34.3 2.8 %copy-start.4 = (bf16[512,896]{1,0:T(8,128)(2,1)S(1)}, bf16[512,896]{1,0:T(8,128)(2,1)}, u32[]{:S(2)}) copy-start(bf16[512,896]{1,0:T(8,128)(2,1)} %param.14) | copy-start | bytes 2752516
  53.0 12.2 %copy-start.1 = (bf16[1,1024,896]{1,2,0:T(8,128)(2,1)S(1)}, bf16[1,1024,896]{1,2,0:T(8,128)(2,1)}, u32[]{:S(2)}) copy-start(bf16[1,1024,896]{1,2,0:T(8,128)(2,1)} %copy.81) | copy-start | bytes 5505028
  65.2 1.8 %copy-start.8 = (bf16[1,1024,896]{1,2,0:T(8,128)(2,1)S(1)}, bf16[1,1024,896]{1,2,0:T(8,128)(2,1)}, u32[]{:S(2)}) copy-start(bf16[1,1024,896]{1,2,0:T(8,128)(2,1)} %copy.83) | copy-start | bytes 5505028
  67.9 2.6 %copy-start = (bf16[1,1024,896]{1,2,0:T(8,128)(2,1)S(1)}, bf16[1,1024,896]{1,2,0:T(8,128)(2,1)}, u32[]{:S(2)}) copy-start(bf16[1,1024,896]{1,2,0:T(8,128)(2,1)} %copy.87) | copy-start | bytes 5505028
  70.6 1.8 %copy-start.7 = (bf16[1,1024,896]{1,2,0:T(8,128)(2,1)S(1)}, bf16[1,1024,896]{1,2,0:T(8,128)(2,1)}, u32[]{:S(2)}) copy-start(bf16[1,1024,896]{1,2,0:T(8,128)(2,1)} %copy.89) | copy-start | bytes 5505028
  73.3 8.3 %copy-start.9 = (pred[512,512]{0,1:T(8,128)(4,1)S(1)}, pred[512,512]{0,1:T(8,128)(4,1)}, u32[]{:S(2)}) copy-start(pred[512,512]{0,1:T(8,128)(4,1)} %fusion.43) | copy-start | bytes 786436
  74.7 23.3 %collective-permute-start.2 = (f32[192,1024]{1,0:T(8,128)S(1)}, f32[192,1024]{1,0:T(8,128)S(1)}, u32[]{:S(2)}, u32[]{:S(2)}) collective-permute-start(f32[192,1024]{1,0:T(8,128)S(1)} %get-tuple-element.43), channel_id=1, source_target_pairs={{0,248},{8,0},{16,8},{24,16},{32,24},{40,32},{48,40},{56,48},{64,5... | collective-permute-start | bytes 2359304 | tf_op jit(solution)/shard_map/ppermute | solution.py:20
  81.6 18.7 %collective-permute-start.3 = (f32[192,1024]{1,0:T(8,128)S(1)}, f32[192,1024]{1,0:T(8,128)S(1)}, u32[]{:S(2)}, u32[]{:S(2)}) collective-permute-start(f32[192,1024]{1,0:T(8,128)S(1)} %get-tuple-element.42), channel_id=1, source_target_pairs={{0,8},{8,16},{16,24},{24,32},{32,40},{40,48},{48,56},{56,64},{64,7... | collective-permute-start | bytes 2359304 | tf_op jit(solution)/shard_map/ppermute | solution.py:20
  84.0 2.0 %copy-start.2 = (f32[4,512,512]{1,2,0:T(8,128)}, f32[4,512,512]{1,2,0:T(8,128)S(1)}, u32[]{:S(2)}) copy-start(f32[4,512,512]{1,2,0:T(8,128)S(1)} %get-tuple-element.83) | copy-start | bytes 12582916
  104.6 2.4 %copy-start.10 = (pred[512,512]{0,1:T(8,128)(4,1)S(1)}, pred[512,512]{0,1:T(8,128)(4,1)}, u32[]{:S(2)}) copy-start(pred[512,512]{0,1:T(8,128)(4,1)} %fusion.43) | copy-start | bytes 786436
  119.9 1.1 copy-start.12
  119.9 1.4 copy-start.11
  121.0 18.7 %collective-permute-start.4 = (bf16[2,192,896]{2,1,0:T(8,128)(2,1)S(1)}, bf16[2,192,896]{2,1,0:T(8,128)(2,1)S(1)}, u32[]{:S(2)}, u32[]{:S(2)}) collective-permute-start(bf16[2,192,896]{2,1,0:T(8,128)(2,1)S(1)} %copy-done.12), channel_id=1, source_target_pairs={{0,8},{8,16},{16,24},{24,32},{32,40},{40,48},{48,56},{56,64},{64,7... | collective-permute-start | bytes 2064392 | tf_op jit(solution)/shard_map/ppermute | solution.py:20
  121.3 18.5 %collective-permute-start.5 = (bf16[2,192,896]{2,1,0:T(8,128)(2,1)S(1)}, bf16[2,192,896]{2,1,0:T(8,128)(2,1)S(1)}, u32[]{:S(2)}, u32[]{:S(2)}) collective-permute-start(bf16[2,192,896]{2,1,0:T(8,128)(2,1)S(1)} %copy-done.11), channel_id=1, source_target_pairs={{0,248},{8,0},{16,8},{24,16},{32,24},{40,32},{48,40},{56,48},{64,5... | collective-permute-start | bytes 2064392 | tf_op jit(solution)/shard_map/ppermute | solution.py:20
Sparse Core Ops, SparseCore 0:
  120.0 39.5 reduce-scatter.1

commit v3 on v2

--- a/solution.py
+++ b/solution.py
@@ -1,8 +1,11 @@
+import functools
 import math
 
 import jax
 import jax.numpy as jnp
 from jax import lax
+from jax.experimental import pallas as pl
+from jax.experimental.pallas import tpu as pltpu
 from jax.sharding import PartitionSpec as P
 
 HD = 224
@@ -40,6 +43,65 @@
         preferred_element_type=jnp.float32,
     )
     return (numerator.reshape(row_count, head_count * HD), row_top.T, row_total.T)
+
+
+def prior_kernel(head_count, prior_ref, query_ref, key_ref, value_ref, out_ref):
+    slot = pl.program_id(0)
+    prior = prior_ref[slot]
+    query_rows = query_ref[...]
+    key_rows = key_ref[...]
+    value_rows = value_ref[...]
+    row_count, feat_width = query_rows.shape
+    key_count = key_rows.shape[0]
+    lanes = lax.broadcasted_iota(jnp.int32, (1, feat_width), 1)
+    live = lax.broadcasted_iota(jnp.int32, (1, key_count), 1) < prior
+    tail_lanes = lax.broadcasted_iota(jnp.int32, (row_count, out_ref.shape[1] - feat_width), 1)
+    numer = jnp.zeros((row_count, feat_width), jnp.float32)
+    tail = jnp.zeros((row_count, out_ref.shape[1] - feat_width), jnp.float32)
+    for h in range(head_count):
+        in_head = (lanes >= h * HD) & (lanes < (h + 1) * HD)
+        head_query = jnp.where(in_head, query_rows, jnp.zeros((), query_rows.dtype))
+        scores = lax.dot_general(
+            head_query, key_rows, (((1,), (1,)), ((), ())), preferred_element_type=jnp.float32
+        ) * (1.0 / math.sqrt(HD))
+        scores = jnp.where(live, scores, floor_value)
+        row_top = jnp.max(scores, axis=1, keepdims=True)
+        weights = jnp.where(live, jnp.exp(scores - row_top), 0.0)
+        row_total = jnp.sum(weights, axis=1, keepdims=True)
+        head_out = jnp.dot(
+            weights.astype(jnp.bfloat16), value_rows, preferred_element_type=jnp.float32
+        )
+        numer = numer + jnp.where(in_head, head_out, 0.0)
+        tail = jnp.where(tail_lanes == h, row_top, tail)
+        tail = jnp.where(tail_lanes == head_count + h, row_total, tail)
+    out_ref[:, :feat_width] = numer
+    out_ref[:, feat_width:] = tail
+
+
+def serve_slots(priors, query_stack, cache_keys, cache_values, head_count):
+    slot_count, row_count, feat_width = query_stack.shape
+    key_count = cache_keys.shape[1]
+    flops = slot_count * head_count * 4 * row_count * key_count * feat_width
+    moved = 2 * (query_stack.size + cache_keys.size + cache_values.size) + 4 * slot_count * row_count * RESULT_WIDTH
+    return pl.pallas_call(
+        functools.partial(prior_kernel, head_count),
+        out_shape=jax.ShapeDtypeStruct((slot_count, row_count, RESULT_WIDTH), jnp.float32),
+        grid_spec=pltpu.PrefetchScalarGridSpec(
+            num_scalar_prefetch=1,
+            grid=(slot_count,),
+            in_specs=[
+                pl.BlockSpec((None, row_count, feat_width), lambda s, pr: (s, 0, 0)),
+                pl.BlockSpec((None, key_count, feat_width), lambda s, pr: (s, 0, 0)),
+                pl.BlockSpec((None, key_count, feat_width), lambda s, pr: (s, 0, 0)),
+            ],
+            out_specs=pl.BlockSpec((None, row_count, RESULT_WIDTH), lambda s, pr: (s, 0, 0)),
+        ),
+        cost_estimate=pl.CostEstimate(
+            flops=flops,
+            transcendentals=slot_count * head_count * row_count * key_count,
+            bytes_accessed=moved,
+        ),
+    )(priors, query_stack, cache_keys, cache_values)
 
 
 def body(
@@ -103,17 +165,15 @@
     left_tag = read_tag(from_left)
     right_tag = read_tag(from_right)
     left_is_zero = left_tag[0] == 0
-    served = []
-    for s in range(slot_count):
-        mine = left_is_zero if s == 0 else jnp.logical_not(left_is_zero)
-        query_rows = jnp.where(mine, from_left[:NEWCAP], from_right[:NEWCAP])
-        prior = jnp.where(mine, left_tag[1], right_tag[1])
-        live_mask = jnp.broadcast_to(prior_marks[None, :] < prior, (NEWCAP, prior_rows))
-        numer, top, total = attend_part(
-            query_rows, cache_keys[s], cache_values[s], live_mask, head_count
-        )
-        pad = jnp.zeros((NEWCAP, RESULT_WIDTH - feat_width - 2 * head_count), jnp.float32)
-        served.append(jnp.concatenate([numer, top, total, pad], axis=1))
+    left_rows = from_left[:NEWCAP]
+    right_rows = from_right[:NEWCAP]
+    query_stack = jnp.stack(
+        [jnp.where(left_is_zero, left_rows, right_rows), jnp.where(left_is_zero, right_rows, left_rows)]
+    )
+    priors = jnp.stack(
+        [jnp.where(left_is_zero, left_tag[1], right_tag[1]), jnp.where(left_is_zero, right_tag[1], left_tag[1])]
+    )
+    served = serve_slots(priors, query_stack, cache_keys, cache_values, head_count)
     back_left = jnp.where(left_is_zero, served[0], served[1])
     back_right = jnp.where(left_is_zero, served[1], served[0])
     got_right = shifted(back_left, "req", -1)

time: 167 us -> 156 us (0.934)
  local copies, waits for them, and re-layouts: 46.6 us -> 15.5 us
  Pallas kernels: 0 us -> 14 us
  waiting for transfers between devices: 44 us -> 50.9 us
  other arithmetic: 14.6 us -> 18.9 us
  matrix products: 18.9 us -> 15.8 us
  starting transfers between devices: 14.5 us -> 12.5 us
    slice x6 -> x0, local copies, waits for them, and re-layouts: 20.1 us -> none  [the longest x3 10.1 us: body(): cache_keys[s]]
    pallas_call x0 -> x1, Pallas kernels: none -> 14 us  [serve_slots(): pl.pallas_call(functools.partial(prior_kernel, head_count), out_shape=jax...]
    unnamed x29 -> x11, local copies, waits for them, and re-layouts: 8.9 us -> 3.31 us
    ppermute x6, waiting for transfers between devices: 25.5 us -> 30.1 us  [shifted(): return lax.ppermute(value, axis, pairs)]
    another operation x1 -> x4, other arithmetic: 0.83 us -> 3.55 us  [the longest x2 2.07 us: body(): jnp.stack([jnp.where(left_is_zero, left_rows, right_rows), jnp.where(left...]
    select_n x1, other arithmetic: 0.19 us -> 2.87 us  [body(): back_right = jnp.where(left_is_zero, served[1], served[0])]
    optimization_barrier x2 -> x0, local copies, waits for them, and re-layouts: 2.65 us -> none  [body(): lax.optimization_barrier((right_kv, left_kv, got_right, got_left))]
    reshape x4 -> x0, local copies, waits for them, and re-layouts: 2.64 us -> none  [the longest x2 1.68 us: attend_part(): query_heads = query_rows.reshape(row_count, head_count, HD)]
  transfers between devices with their start and end apart: 7 -> 7, of which waited for: 4 -> 5; matrix products, arithmetic and copies ran while one was open for 22% -> 11% of each run, Pallas kernels for 0% -> 0%
where the time goes in v3:
time: 156 us
  waiting for transfers between devices  50.9 us (33%)
  between operations  28 us (18%)
  other arithmetic  18.9 us (12%)
  matrix products  15.8 us (10%)
  local copies, waits for them, and re-layouts  15.5 us (10%)
  Pallas kernels  14 us (9%)
  starting transfers between devices  12.5 us (8%)
    ppermute x6, waiting for transfers between devices, shifted(): return lax.ppermute(value, axis, pairs)  30.1 us
    reduce_scatter x1, waiting for transfers between devices, body(): lax.psum_scatter(jnp.dot(attended, out_proj, preferred_element_type=jnp.f...  20.8 us
    pallas_call x1, Pallas kernels, serve_slots(): pl.pallas_call(functools.partial(prior_kernel, head_count), out_shape=jax...  14 us
    ppermute x6, starting transfers between devices, shifted(): return lax.ppermute(value, axis, pairs)  12.5 us
    dot_general x1, matrix products, body(): jnp.dot(attended, out_proj, preferred_element_type=jnp.float32)  8.37 us
    dot_general x1, matrix products, attend_part(): jnp.einsum('hts,shd->thd', weights.astype(jnp.bfloat16), value_heads, pre...  4.55 us
    unnamed x11, local copies, waits for them, and re-layouts  3.31 us
    reduce_sum x1, other arithmetic, attend_part(): row_total = jnp.sum(weights, axis=2)  3.23 us
  transfers between devices with their start and end apart: 7, of which 5 were waited for; matrix products, arithmetic and copies ran while one was open for 11% of the time, Pallas kernels for 0%

profile of v3, /device:TPU:8, one launch (start us, length us, event | category | flops | bytes accessed | tf_op | source)
XLA Modules:
  0.0 155.6 jit_solution(6836556139770484202)
XLA Ops:
  7.2 1.3 fusion.68
  10.5 1.4 fusion.69
  18.0 1.4 fusion.67
  20.6 1.3 constant_dynamic-slice_fusion
  22.0 1.7 %collective-permute-start = (bf16[200,896]{1,0:T(8,128)(2,1)S(1)}, bf16[200,896]{1,0:T(8,128)(2,1)}, u32[]{:S(2)}, u32[]{:S(2)}) collective-permute-start(bf16[200,896]{1,0:T(8,128)(2,1)S(1)} %pad_maximum_fusion.3), channel_id=1, source_target_pairs={{0,8},{8,16},{16,24},{24,32},{32,40},{40,48},{48,56},{56,64},{64,7... | collective-permute-start | bytes 1075208 | tf_op jit(solution)/shard_map/ppermute | solution.py:23
  29.0 1.5 copy.51
  31.3 2.9 %fusion = (f32[4,512]{1,0:T(4,128)S(1)}, f32[4,512,512]{1,2,0:T(8,128)}) fusion(pred[512,512]{0,1:T(8,128)(4,1)S(1)} %fusion.17, bf16[512,4,224]{0,2,1:T(8,128)(2,1)S(1)} %bitcast.85, bf16[512,4,224]{0,2,1:T(8,128)(2,1)S(1)} %bitcast.86), kind=kOutput, calls=%fused_computation.3 | convolution fusion | flops 472905728 | bytes 6299648 | tf_op jit(solution)/shard_map/thd,shd->hts/dot_general | solution.py:32
  36.2 2.3 %collective-permute-done.1 = bf16[200,896]{1,0:T(8,128)(2,1)} collective-permute-done((bf16[200,896]{1,0:T(8,128)(2,1)}, bf16[200,896]{1,0:T(8,128)(2,1)}, u32[]{:S(2)}, u32[]{:S(2)}) %collective-permute-start.1) | collective-permute-done | bytes 358432 | tf_op jit(solution)/shard_map/ppermute | solution.py:23
  45.2 14.0 %shard_map.121 = f32[2,192,1024]{2,1,0:T(8,128)} custom-call(s32[2]{0:T(128)} %pad_add_fusion.prior_ref, bf16[2,192,896]{2,1,0:T(8,128)(2,1)} %pad_maximum_fusion.2.query_ref, bf16[2,1024,896]{2,1,0:T(8,128)(2,1)} %key_ref.1, bf16[2,1024,896]{2,1,0:T(8,128)(2,1)} %value_ref.1), custom_call_target="tpu_custom_call" | custom-call | flops 5637144576 | bytes 9601024 | tf_op jit(solution)/shard_map/pallas_call | solution.py:86
  59.2 2.9 %select_bitcast_fusion = (f32[192,1024]{1,0:T(8,128)}, f32[192,1024]{1,0:T(8,128)}) fusion(f32[2,192,1024]{2,1,0:T(8,128)} %shard_map.121, pred[]{:T(512)S(6)} %eq.72), kind=kLoop, calls=%fused_computation.22 | loop fusion | flops 393216 | bytes 3145729 | tf_op jit(solution)/shard_map/jit(_where)/select_n | solution.py:178
  62.1 5.0 %collective-permute-start.2 = (f32[192,1024]{1,0:T(8,128)}, f32[192,1024]{1,0:T(8,128)S(1)}, u32[]{:S(2)}, u32[]{:S(2)}) collective-permute-start(f32[192,1024]{1,0:T(8,128)} %get-tuple-element.39), channel_id=1, source_target_pairs={{0,248},{8,0},{16,8},{24,16},{32,24},{40,32},{48,40},{56,48},{64,5... | collective-permute-start | bytes 2359304 | tf_op jit(solution)/shard_map/ppermute | solution.py:23
  67.1 3.2 %fusion.1 = f32[4,512]{1,0:T(4,128)S(1)} fusion(f32[4,512,512]{1,2,0:T(8,128)} %get-tuple-element.75, f32[4,512]{1,0:T(4,128)S(1)} %get-tuple-element.74, pred[512,512]{0,1:T(8,128)(4,1)S(1)} %fusion.17), kind=kLoop, calls=%fused_computation.6 | loop fusion | flops 5240832 | bytes 4472832 | tf_op jit(solution)/shard_map/reduce_sum | solution.py:38
  70.6 1.3 copy.53
  72.5 1.2 pad_maximum_fusion
  73.7 9.6 %collective-permute-done.2 = f32[192,1024]{1,0:T(8,128)S(1)} collective-permute-done((f32[192,1024]{1,0:T(8,128)}, f32[192,1024]{1,0:T(8,128)S(1)}, u32[]{:S(2)}, u32[]{:S(2)}) %collective-permute-start.2) | collective-permute-done | bytes 786464 | tf_op jit(solution)/shard_map/ppermute | solution.py:23
  83.3 6.3 %collective-permute-done.3 = f32[192,1024]{1,0:T(8,128)} collective-permute-done((f32[192,1024]{1,0:T(8,128)}, f32[192,1024]{1,0:T(8,128)}, u32[]{:S(2)}, u32[]{:S(2)}) %collective-permute-start.3) | collective-permute-done | bytes 786464 | tf_op jit(solution)/shard_map/ppermute | solution.py:23
  93.2 1.8 %copy.57 = f32[512,896]{0,1:T(8,128)} copy(f32[512,896]{1,0:T(8,128)S(1)} %fusion.10) | data formatting | bytes 3670016 | tf_op jit(solution)/shard_map/jit(_where)/select_n | solution.py:220
  95.0 4.5 %fusion.14 = bf16[512,4,224]{0,2,1:T(8,128)(2,1)S(1)} fusion(f32[512,4,224]{0,2,1:T(8,128)} %bitcast.83, bf16[512,4,224]{0,2,1:T(8,128)(2,1)} %bitcast.84, f32[4,512,512]{1,2,0:T(8,128)} %get-tuple-element.75, f32[4,512]{1,0:T(4,128)S(1)} %get-tuple-element.74, pred[512,512]{0,1:T(8,128)(4,1)S(1)} %fusion.17, f32[512,4]{0,1:T(4,128)S(1)} %copy.60, ...), kind=kOutput, calls=%fused_computation.19 | convolution fusion | flops 477298688 | bytes 8159232 | tf_op jit(solution)/shard_map/hts,shd->thd/dot_general | solution.py:39
  99.6 8.4 %convolution_convert_fusion = bf16[512,3584]{1,0:T(8,128)(2,1)} fusion(bf16[512,896]{0,1:T(8,128)(2,1)S(1)} %bitcast.89, bf16[896,3584]{1,0:T(8,128)(2,1)} %param.19), kind=kOutput, calls=%fused_computation | convolution fusion | flops 3290169344 | bytes 11010048 | tf_op jit(solution)/shard_map/dot_general | solution.py:236
  108.1 5.1 %collective-permute-start.5 = (bf16[2,192,896]{2,1,0:T(8,128)(2,1)S(1)}, bf16[2,192,896]{2,1,0:T(8,128)(2,1)S(1)}, u32[]{:S(2)}, u32[]{:S(2)}) collective-permute-start(bf16[2,192,896]{2,1,0:T(8,128)(2,1)S(1)} %copy-done.2), channel_id=1, source_target_pairs={{0,248},{8,0},{16,8},{24,16},{32,24},{40,32},{48,40},{56,48},{64,5... | collective-permute-start | bytes 2064392 | tf_op jit(solution)/shard_map/ppermute | solution.py:23
  113.2 1.4 iota_compare_fusion.6
  114.6 11.9 %collective-permute-done.4 = bf16[2,192,896]{2,1,0:T(8,128)(2,1)S(1)} collective-permute-done((bf16[2,192,896]{2,1,0:T(8,128)(2,1)S(1)}, bf16[2,192,896]{2,1,0:T(8,128)(2,1)S(1)}, u32[]{:S(2)}, u32[]{:S(2)}) %collective-permute-start.4) | collective-permute-done | bytes 688160 | tf_op jit(solution)/shard_map/ppermute | solution.py:23
  126.6 1.3 select_select_fusion
  127.9 20.8 %reduce-scatter.2.cloned.1.call-done = bf16[64,3584]{1,0:T(8,128)(2,1)} async-done(((bf16[512,3584]{1,0:T(8,128)(2,1)}), bf16[64,3584]{1,0:T(8,128)(2,1)}) %reduce-scatter.2.cloned.1.call-update) | async-done | bytes 458768 | tf_op jit(solution)/shard_map/reduce_scatter | solution.py:235
  (50 shorter events, 15.2 us)
Async XLA Ops:
  7.2 23.6 %copy-start.1 = (bf16[512,896]{1,0:T(8,128)(2,1)S(1)}, bf16[512,896]{1,0:T(8,128)(2,1)}, u32[]{:S(2)}) copy-start(bf16[512,896]{1,0:T(8,128)(2,1)} %param.15) | copy-start | bytes 2752516
  7.2 141.6 %reduce-scatter.2.cloned.1.call-start = ((), (), s32[]{:S(2)}) async-start(), calls=%async_computation.1 | async-start | bytes 4128768 | tf_op jit(solution)/shard_map/reduce_scatter | solution.py:235
  22.0 12.2 %collective-permute-start = (bf16[200,896]{1,0:T(8,128)(2,1)S(1)}, bf16[200,896]{1,0:T(8,128)(2,1)}, u32[]{:S(2)}, u32[]{:S(2)}) collective-permute-start(bf16[200,896]{1,0:T(8,128)(2,1)S(1)} %pad_maximum_fusion.3), channel_id=1, source_target_pairs={{0,8},{8,16},{16,24},{24,32},{32,40},{40,48},{48,56},{56,64},{64,7... | collective-permute-start | bytes 1075208 | tf_op jit(solution)/shard_map/ppermute | solution.py:23
  28.4 10.1 %collective-permute-start.1 = (bf16[200,896]{1,0:T(8,128)(2,1)}, bf16[200,896]{1,0:T(8,128)(2,1)}, u32[]{:S(2)}, u32[]{:S(2)}) collective-permute-start(bf16[200,896]{1,0:T(8,128)(2,1)} %pad_maximum_fusion.4), channel_id=1, source_target_pairs={{0,248},{8,0},{16,8},{24,16},{32,24},{40,32},{48,40},{56,48},{64,5... | collective-permute-start | bytes 1075208 | tf_op jit(solution)/shard_map/ppermute | solution.py:23
  59.2 11.4 %copy-start = (bf16[512,896]{1,0:T(8,128)(2,1)S(1)}, bf16[512,896]{1,0:T(8,128)(2,1)}, u32[]{:S(2)}) copy-start(bf16[512,896]{1,0:T(8,128)(2,1)} %param.16) | copy-start | bytes 2752516
  62.1 21.2 %collective-permute-start.2 = (f32[192,1024]{1,0:T(8,128)}, f32[192,1024]{1,0:T(8,128)S(1)}, u32[]{:S(2)}, u32[]{:S(2)}) collective-permute-start(f32[192,1024]{1,0:T(8,128)} %get-tuple-element.39), channel_id=1, source_target_pairs={{0,248},{8,0},{16,8},{24,16},{32,24},{40,32},{48,40},{56,48},{64,5... | collective-permute-start | bytes 2359304 | tf_op jit(solution)/shard_map/ppermute | solution.py:23
  67.1 22.5 %collective-permute-start.3 = (f32[192,1024]{1,0:T(8,128)}, f32[192,1024]{1,0:T(8,128)}, u32[]{:S(2)}, u32[]{:S(2)}) collective-permute-start(f32[192,1024]{1,0:T(8,128)} %get-tuple-element.38), channel_id=1, source_target_pairs={{0,8},{8,16},{16,24},{24,32},{32,40},{40,48},{48,56},{56,64},{64,7... | collective-permute-start | bytes 2359304 | tf_op jit(solution)/shard_map/ppermute | solution.py:23
  99.6 8.4 %copy-start.3 = (bf16[2,192,896]{2,1,0:T(8,128)(2,1)S(1)}, bf16[2,192,896]{2,1,0:T(8,128)(2,1)}, u32[]{:S(2)}) copy-start(bf16[2,192,896]{2,1,0:T(8,128)(2,1)} %get-tuple-element.33) | copy-start | bytes 2064388
  99.6 8.5 %copy-start.2 = (bf16[2,192,896]{2,1,0:T(8,128)(2,1)S(1)}, bf16[2,192,896]{2,1,0:T(8,128)(2,1)}, u32[]{:S(2)}) copy-start(bf16[2,192,896]{2,1,0:T(8,128)(2,1)} %get-tuple-element.34) | copy-start | bytes 2064388
  108.0 18.5 %collective-permute-start.4 = (bf16[2,192,896]{2,1,0:T(8,128)(2,1)S(1)}, bf16[2,192,896]{2,1,0:T(8,128)(2,1)S(1)}, u32[]{:S(2)}, u32[]{:S(2)}) collective-permute-start(bf16[2,192,896]{2,1,0:T(8,128)(2,1)S(1)} %copy-done.3), channel_id=1, source_target_pairs={{0,8},{8,16},{16,24},{24,32},{32,40},{40,48},{48,56},{56,64},{64,7... | collective-permute-start | bytes 2064392 | tf_op jit(solution)/shard_map/ppermute | solution.py:23
  108.1 18.5 %collective-permute-start.5 = (bf16[2,192,896]{2,1,0:T(8,128)(2,1)S(1)}, bf16[2,192,896]{2,1,0:T(8,128)(2,1)S(1)}, u32[]{:S(2)}, u32[]{:S(2)}) collective-permute-start(bf16[2,192,896]{2,1,0:T(8,128)(2,1)S(1)} %copy-done.2), channel_id=1, source_target_pairs={{0,248},{8,0},{16,8},{24,16},{32,24},{40,32},{48,40},{56,48},{64,5... | collective-permute-start | bytes 2064392 | tf_op jit(solution)/shard_map/ppermute | solution.py:23
Sparse Core Ops, SparseCore 0:
  108.1 40.6 reduce-scatter.1

commit v4 on v3

--- a/solution.py
+++ b/solution.py
@@ -232,13 +232,19 @@
     attended = (
         (numerator / denominator[:, :, None]).reshape(tok_count, feat_width).astype(jnp.bfloat16)
     )
-    mixed = lax.psum_scatter(
-        jnp.dot(attended, out_proj, preferred_element_type=jnp.float32).astype(jnp.bfloat16),
-        "tp",
-        scatter_dimension=0,
-        tiled=True,
-    )
-
+    chip_count = lax.axis_size("x")
+    core_count = lax.axis_size("core")
+    block_rows = tok_count // (chip_count * core_count)
+    reordered = (
+        attended.reshape(chip_count, core_count, block_rows, feat_width)
+        .transpose(1, 0, 2, 3)
+        .reshape(tok_count, feat_width)
+    )
+    partial = jnp.dot(reordered, out_proj, preferred_element_type=jnp.float32).astype(jnp.bfloat16)
+    partial = partial.reshape(core_count, chip_count * block_rows, partial.shape[1])
+    partial = lax.psum_scatter(partial, "core", scatter_dimension=0, tiled=False)
+    partial = partial.reshape(chip_count, block_rows, partial.shape[1])
+    mixed = lax.psum_scatter(partial, "x", scatter_dimension=0, tiled=False)
     slot_ids = jnp.arange(slot_count, dtype=jnp.int32)
 
     def stored(from_left_rows, from_right_rows):
@@ -256,17 +262,25 @@
 
 
 def solution(mesh):
+    req_count, tp_count = mesh.devices.shape
+    core_count = 2
+    split_mesh = jax.sharding.Mesh(
+        mesh.devices.reshape(req_count, tp_count // core_count, core_count), ("req", "x", "core")
+    )
+    tp = ("x", "core")
     in_specs = (
-        P("req", "tp"),
-        P("req", "tp"),
-        P("req", "tp"),
-        P("req", None, "tp"),
-        P("req", None, "tp"),
-        P("tp", None),
-        P("req", None),
-        P("req", None),
-        P("req", None),
-        P("req", None),
-    )
-    out_specs = (P(("req", "tp"), None), P("req", None, "tp"), P("req", None, "tp"))
-    return jax.shard_map(body, mesh=mesh, in_specs=in_specs, out_specs=out_specs, check_vma=False)
+        P("req", tp),
+        P("req", tp),
+        P("req", tp),
+        P("req", None, tp),
+        P("req", None, tp),
+        P(tp, None),
+        P("req", None),
+        P("req", None),
+        P("req", None),
+        P("req", None),
+    )
+    out_specs = (P(("req", "x", "core"), None), P("req", None, tp), P("req", None, tp))
+    return jax.shard_map(
+        body, mesh=split_mesh, in_specs=in_specs, out_specs=out_specs, check_vma=False
+    )

time: 156 us -> 171 us (1.096)
  waiting for transfers between devices: 50.9 us -> 66.3 us
  starting transfers between devices: 12.5 us -> 9.44 us
    reduce_scatter x1 -> x2, waiting for transfers between devices: 20.8 us -> 32.6 us  [the longest x1 18.3 us: body(): lax.psum_scatter(partial, 'core', scatter_dimension=0, tiled=False)]
    ppermute x6, waiting for transfers between devices: 30.1 us -> 33.7 us  [shifted(): return lax.ppermute(value, axis, pairs)]
    ppermute x6, starting transfers between devices: 12.5 us -> 9.36 us  [shifted(): return lax.ppermute(value, axis, pairs)]
  transfers between devices with their start and end apart: 7 -> 8, of which waited for: 5 -> 7; matrix products, arithmetic and copies ran while one was open for 11% -> 10% of each run, Pallas kernels for 0% -> 0%
where the time goes in v4:
time: 171 us; the launch traced here: 169 us
  waiting for transfers between devices  66.3 us (39%)
  between operations  28 us (16%)
  other arithmetic  18.8 us (11%)
  local copies, waits for them, and re-layouts  16.9 us (10%)
  matrix products  15.9 us (9%)
  Pallas kernels  14.1 us (8%)
  starting transfers between devices  9.44 us (6%)
    ppermute x6, waiting for transfers between devices, shifted(): return lax.ppermute(value, axis, pairs)  33.7 us
    reduce_scatter x1, waiting for transfers between devices, body(): lax.psum_scatter(partial, 'core', scatter_dimension=0, tiled=False)  18.3 us
    reduce_scatter x1, waiting for transfers between devices, body(): mixed = lax.psum_scatter(partial, 'x', scatter_dimension=0, tiled=False)  14.3 us
    pallas_call x1, Pallas kernels, serve_slots(): pl.pallas_call(functools.partial(prior_kernel, head_count), out_shape=jax...  14.1 us
    ppermute x6, starting transfers between devices, shifted(): return lax.ppermute(value, axis, pairs)  9.36 us
    dot_general x1, matrix products, body(): jnp.dot(reordered, out_proj, preferred_element_type=jnp.float32)  8.38 us
    dot_general x1, matrix products, attend_part(): jnp.einsum('hts,shd->thd', weights.astype(jnp.bfloat16), value_heads, pre...  4.62 us
  transfers between devices with their start and end apart: 8, of which 7 were waited for; matrix products, arithmetic and copies ran while one was open for 10% of the time, Pallas kernels for 0%

profile of v4, /device:TPU:8, one launch (start us, length us, event | category | flops | bytes accessed | tf_op | source)
XLA Modules:
  0.0 169.4 jit_solution(2422194124812867585)
XLA Ops:
  7.2 1.3 fusion.68
  10.5 1.4 fusion.69
  17.9 1.3 fusion.67
  20.6 1.3 constant_dynamic-slice_fusion
  22.0 1.7 collective-permute-start
  29.0 1.5 copy.57
  31.3 2.9 %fusion = (f32[4,512]{1,0:T(4,128)S(1)}, f32[4,512,512]{1,2,0:T(8,128)}) fusion(pred[512,512]{0,1:T(8,128)(4,1)S(1)} %fusion.17, bf16[512,4,224]{0,2,1:T(8,128)(2,1)S(1)} %bitcast.92, bf16[512,4,224]{0,2,1:T(8,128)(2,1)S(1)} %bitcast.93), kind=kOutput, calls=%fused_computation.3 | convolution fusion | flops 472905728 | bytes 6299648 | tf_op jit(solution)/shard_map/thd,shd->hts/dot_general | solution.py:32
  36.2 2.3 %collective-permute-done.1 = bf16[200,896]{1,0:T(8,128)(2,1)} collective-permute-done((bf16[200,896]{1,0:T(8,128)(2,1)}, bf16[200,896]{1,0:T(8,128)(2,1)}, u32[]{:S(2)}, u32[]{:S(2)}) %collective-permute-start.1) | collective-permute-done | bytes 358432 | tf_op jit(solution)/shard_map/ppermute | solution.py:23
  45.0 14.1 %shard_map.121 = f32[2,192,1024]{2,1,0:T(8,128)} custom-call(s32[2]{0:T(128)} %pad_add_fusion.prior_ref, bf16[2,192,896]{2,1,0:T(8,128)(2,1)} %pad_maximum_fusion.2.query_ref, bf16[2,1024,896]{2,1,0:T(8,128)(2,1)} %key_ref.1, bf16[2,1024,896]{2,1,0:T(8,128)(2,1)} %value_ref.1), custom_call_target="tpu_custom_call" | custom-call | flops 5637144576 | bytes 9601024 | tf_op jit(solution)/shard_map/pallas_call | solution.py:86
  59.1 2.8 %select_bitcast_fusion = (f32[192,1024]{1,0:T(8,128)}, f32[192,1024]{1,0:T(8,128)}) fusion(f32[2,192,1024]{2,1,0:T(8,128)} %shard_map.121, pred[]{:T(512)S(6)} %eq.72), kind=kLoop, calls=%fused_computation.22 | loop fusion | flops 393216 | bytes 3145729 | tf_op jit(solution)/shard_map/jit(_where)/select_n | solution.py:178
  62.0 5.0 %collective-permute-start.2 = (f32[192,1024]{1,0:T(8,128)}, f32[192,1024]{1,0:T(8,128)S(1)}, u32[]{:S(2)}, u32[]{:S(2)}) collective-permute-start(f32[192,1024]{1,0:T(8,128)} %get-tuple-element.39), channel_id=1, source_target_pairs={{0,248},{8,0},{16,8},{24,16},{32,24},{40,32},{48,40},{56,48},{64,5... | collective-permute-start | bytes 2359304 | tf_op jit(solution)/shard_map/ppermute | solution.py:23
  67.0 3.2 %fusion.1 = f32[4,512]{1,0:T(4,128)S(1)} fusion(f32[4,512,512]{1,2,0:T(8,128)} %get-tuple-element.75, f32[4,512]{1,0:T(4,128)S(1)} %get-tuple-element.74, pred[512,512]{0,1:T(8,128)(4,1)S(1)} %fusion.17), kind=kLoop, calls=%fused_computation.6 | loop fusion | flops 5240832 | bytes 4472832 | tf_op jit(solution)/shard_map/reduce_sum | solution.py:38
  70.5 1.3 copy.59
  73.6 9.6 %collective-permute-done.2 = f32[192,1024]{1,0:T(8,128)S(1)} collective-permute-done((f32[192,1024]{1,0:T(8,128)}, f32[192,1024]{1,0:T(8,128)S(1)}, u32[]{:S(2)}, u32[]{:S(2)}) %collective-permute-start.2) | collective-permute-done | bytes 786464 | tf_op jit(solution)/shard_map/ppermute | solution.py:23
  83.2 6.3 %collective-permute-done.3 = f32[192,1024]{1,0:T(8,128)} collective-permute-done((f32[192,1024]{1,0:T(8,128)}, f32[192,1024]{1,0:T(8,128)}, u32[]{:S(2)}, u32[]{:S(2)}) %collective-permute-start.3) | collective-permute-done | bytes 786464 | tf_op jit(solution)/shard_map/ppermute | solution.py:23
  93.1 1.8 %copy.63 = f32[512,896]{0,1:T(8,128)} copy(f32[512,896]{1,0:T(8,128)S(1)} %fusion.10) | data formatting | bytes 3670016 | tf_op jit(solution)/shard_map/jit(_where)/select_n | solution.py:220
  94.9 4.6 %fusion.14 = bf16[512,4,224]{0,2,1:T(8,128)(2,1)S(1)} fusion(f32[512,4,224]{0,2,1:T(8,128)} %bitcast.90, bf16[512,4,224]{0,2,1:T(8,128)(2,1)} %bitcast.91, f32[4,512,512]{1,2,0:T(8,128)} %get-tuple-element.75, f32[4,512]{1,0:T(4,128)S(1)} %get-tuple-element.74, pred[512,512]{0,1:T(8,128)(4,1)} %copy-done.2, f32[512,4]{0,1:T(4,128)S(1)} %copy.66, ...), kind=kOutput, calls=%fused_computation.19 | convolution fusion | flops 477298688 | bytes 8159232 | tf_op jit(solution)/shard_map/hts,shd->thd/dot_general | solution.py:39
  101.1 8.4 %convolution_convert_fusion = bf16[512,3584]{1,0:T(8,128)(2,1)} fusion(bf16[512,896]{1,0:T(8,128)(2,1)S(1)} %bitcast.94, bf16[896,3584]{1,0:T(8,128)(2,1)} %param.19), kind=kOutput, calls=%fused_computation | convolution fusion | flops 3290169344 | bytes 11010048 | tf_op jit(solution)/shard_map/dot_general | solution.py:243
  109.6 18.3 %reduce-scatter.3.cloned.1.call-done = bf16[1,256,3584]{2,1,0:T(8,128)(2,1)} async-done(((bf16[2,256,3584]{2,1,0:T(8,128)(2,1)}), bf16[1,256,3584]{2,1,0:T(8,128)(2,1)}) %reduce-scatter.3.cloned.1.call-update) | async-done | bytes 1835024 | tf_op jit(solution)/shard_map/reduce_scatter | solution.py:245
  127.9 1.6 collective-permute-start.4
  130.0 1.3 iota_compare_fusion.6
  131.2 14.4 %collective-permute-done.4 = bf16[2,192,896]{2,1,0:T(8,128)(2,1)S(1)} collective-permute-done((bf16[2,192,896]{2,1,0:T(8,128)(2,1)S(1)}, bf16[2,192,896]{2,1,0:T(8,128)(2,1)S(1)}, u32[]{:S(2)}, u32[]{:S(2)}) %collective-permute-start.4) | collective-permute-done | bytes 688160 | tf_op jit(solution)/shard_map/ppermute | solution.py:23
  146.9 1.4 select_select_fusion
  148.2 14.3 %reduce-scatter.5.cloned.1.call-done = bf16[1,64,3584]{2,1,0:T(8,128)(2,1)} async-done(((bf16[4,64,3584]{2,1,0:T(8,128)(2,1)}), bf16[1,64,3584]{2,1,0:T(8,128)(2,1)}) %reduce-scatter.5.cloned.1.call-update) | async-done | bytes 458768 | tf_op jit(solution)/shard_map/reduce_scatter | solution.py:247
  (58 shorter events, 19.5 us)
Async XLA Ops:
  7.2 23.6 %copy-start.1 = (bf16[512,896]{1,0:T(8,128)(2,1)S(1)}, bf16[512,896]{1,0:T(8,128)(2,1)}, u32[]{:S(2)}) copy-start(bf16[512,896]{1,0:T(8,128)(2,1)} %param.15) | copy-start | bytes 2752516
  7.2 120.7 %reduce-scatter.3.cloned.1.call-start = ((), (), s32[]{:S(2)}) async-start(), calls=%async_computation.2 | async-start | bytes 5505024 | tf_op jit(solution)/shard_map/reduce_scatter | solution.py:245
  22.0 12.2 %collective-permute-start = (bf16[200,896]{1,0:T(8,128)(2,1)S(1)}, bf16[200,896]{1,0:T(8,128)(2,1)}, u32[]{:S(2)}, u32[]{:S(2)}) collective-permute-start(bf16[200,896]{1,0:T(8,128)(2,1)S(1)} %pad_maximum_fusion.3), channel_id=1, source_target_pairs={{0,8},{8,16},{16,24},{24,32},{32,40},{40,48},{48,56},{56,64},{64,7... | collective-permute-start | bytes 1075208 | tf_op jit(solution)/shard_map/ppermute | solution.py:23
  28.4 10.1 %collective-permute-start.1 = (bf16[200,896]{1,0:T(8,128)(2,1)}, bf16[200,896]{1,0:T(8,128)(2,1)}, u32[]{:S(2)}, u32[]{:S(2)}) collective-permute-start(bf16[200,896]{1,0:T(8,128)(2,1)} %pad_maximum_fusion.4), channel_id=1, source_target_pairs={{0,248},{8,0},{16,8},{24,16},{32,24},{40,32},{48,40},{56,48},{64,5... | collective-permute-start | bytes 1075208 | tf_op jit(solution)/shard_map/ppermute | solution.py:23
  30.7 36.2 %copy-start.2 = (pred[512,512]{0,1:T(8,128)(4,1)}, pred[512,512]{0,1:T(8,128)(4,1)S(1)}, u32[]{:S(2)}) copy-start(pred[512,512]{0,1:T(8,128)(4,1)S(1)} %fusion.17) | copy-start | bytes 786436
  59.1 11.4 %copy-start = (bf16[512,896]{1,0:T(8,128)(2,1)S(1)}, bf16[512,896]{1,0:T(8,128)(2,1)}, u32[]{:S(2)}) copy-start(bf16[512,896]{1,0:T(8,128)(2,1)} %param.16) | copy-start | bytes 2752516
  62.0 21.2 %collective-permute-start.2 = (f32[192,1024]{1,0:T(8,128)}, f32[192,1024]{1,0:T(8,128)S(1)}, u32[]{:S(2)}, u32[]{:S(2)}) collective-permute-start(f32[192,1024]{1,0:T(8,128)} %get-tuple-element.39), channel_id=1, source_target_pairs={{0,248},{8,0},{16,8},{24,16},{32,24},{40,32},{48,40},{56,48},{64,5... | collective-permute-start | bytes 2359304 | tf_op jit(solution)/shard_map/ppermute | solution.py:23
  67.0 22.5 %collective-permute-start.3 = (f32[192,1024]{1,0:T(8,128)}, f32[192,1024]{1,0:T(8,128)}, u32[]{:S(2)}, u32[]{:S(2)}) collective-permute-start(f32[192,1024]{1,0:T(8,128)} %get-tuple-element.38), channel_id=1, source_target_pairs={{0,8},{8,16},{16,24},{24,32},{32,40},{40,48},{48,56},{56,64},{64,7... | collective-permute-start | bytes 2359304 | tf_op jit(solution)/shard_map/ppermute | solution.py:23
  109.5 18.4 %copy-start.4 = (bf16[2,192,896]{2,1,0:T(8,128)(2,1)S(1)}, bf16[2,192,896]{2,1,0:T(8,128)(2,1)}, u32[]{:S(2)}) copy-start(bf16[2,192,896]{2,1,0:T(8,128)(2,1)} %get-tuple-element.33) | copy-start | bytes 2064388
  109.5 19.9 %copy-start.3 = (bf16[2,192,896]{2,1,0:T(8,128)(2,1)S(1)}, bf16[2,192,896]{2,1,0:T(8,128)(2,1)}, u32[]{:S(2)}) copy-start(bf16[2,192,896]{2,1,0:T(8,128)(2,1)} %get-tuple-element.34) | copy-start | bytes 2064388
  109.5 53.0 %reduce-scatter.5.cloned.1.call-start = ((), (), s32[]{:S(2)}) async-start(), calls=%async_computation.3 | async-start | bytes 2293760 | tf_op jit(solution)/shard_map/reduce_scatter | solution.py:247
  127.9 17.8 %collective-permute-start.4 = (bf16[2,192,896]{2,1,0:T(8,128)(2,1)S(1)}, bf16[2,192,896]{2,1,0:T(8,128)(2,1)S(1)}, u32[]{:S(2)}, u32[]{:S(2)}) collective-permute-start(bf16[2,192,896]{2,1,0:T(8,128)(2,1)S(1)} %copy-done.4), channel_id=1, source_target_pairs={{0,8},{8,16},{16,24},{24,32},{32,40},{40,48},{48,56},{56,64},{64,7... | collective-permute-start | bytes 2064392 | tf_op jit(solution)/shard_map/ppermute | solution.py:23
  129.4 17.4 %collective-permute-start.5 = (bf16[2,192,896]{2,1,0:T(8,128)(2,1)S(1)}, bf16[2,192,896]{2,1,0:T(8,128)(2,1)S(1)}, u32[]{:S(2)}, u32[]{:S(2)}) collective-permute-start(bf16[2,192,896]{2,1,0:T(8,128)(2,1)S(1)} %copy-done.3), channel_id=1, source_target_pairs={{0,248},{8,0},{16,8},{24,16},{32,24},{40,32},{48,40},{56,48},{64,5... | collective-permute-start | bytes 2064392 | tf_op jit(solution)/shard_map/ppermute | solution.py:23
Sparse Core Ops, SparseCore 0:
  109.7 18.1 reduce-scatter.2
  131.1 31.3 reduce-scatter.4

commit v5 on v3

--- a/solution.py
+++ b/solution.py
@@ -48,40 +48,43 @@
 def prior_kernel(head_count, prior_ref, query_ref, key_ref, value_ref, out_ref):
     slot = pl.program_id(0)
     prior = prior_ref[slot]
-    query_rows = query_ref[...]
-    key_rows = key_ref[...]
-    value_rows = value_ref[...]
-    row_count, feat_width = query_rows.shape
-    key_count = key_rows.shape[0]
-    lanes = lax.broadcasted_iota(jnp.int32, (1, feat_width), 1)
+    row_count, feat_width = query_ref.shape
+    key_count = key_ref.shape[0]
     live = lax.broadcasted_iota(jnp.int32, (1, key_count), 1) < prior
     tail_lanes = lax.broadcasted_iota(jnp.int32, (row_count, out_ref.shape[1] - feat_width), 1)
-    numer = jnp.zeros((row_count, feat_width), jnp.float32)
     tail = jnp.zeros((row_count, out_ref.shape[1] - feat_width), jnp.float32)
+    out_ref[:, :feat_width] = jnp.zeros((row_count, feat_width), jnp.float32)
     for h in range(head_count):
+        low = (h * HD) // 128 * 128
+        high = min(feat_width, -(-((h + 1) * HD) // 128) * 128)
+        lanes = low + lax.broadcasted_iota(jnp.int32, (1, high - low), 1)
         in_head = (lanes >= h * HD) & (lanes < (h + 1) * HD)
-        head_query = jnp.where(in_head, query_rows, jnp.zeros((), query_rows.dtype))
+        head_query = jnp.where(in_head, query_ref[:, low:high], jnp.zeros((), query_ref.dtype))
         scores = lax.dot_general(
-            head_query, key_rows, (((1,), (1,)), ((), ())), preferred_element_type=jnp.float32
+            head_query, key_ref[:, low:high], (((1,), (1,)), ((), ())),
+            preferred_element_type=jnp.float32,
         ) * (1.0 / math.sqrt(HD))
         scores = jnp.where(live, scores, floor_value)
         row_top = jnp.max(scores, axis=1, keepdims=True)
         weights = jnp.where(live, jnp.exp(scores - row_top), 0.0)
         row_total = jnp.sum(weights, axis=1, keepdims=True)
         head_out = jnp.dot(
-            weights.astype(jnp.bfloat16), value_rows, preferred_element_type=jnp.float32
+            weights.astype(jnp.bfloat16), value_ref[:, low:high], preferred_element_type=jnp.float32
         )
-        numer = numer + jnp.where(in_head, head_out, 0.0)
+        out_ref[:, low:high] = out_ref[:, low:high] + jnp.where(in_head, head_out, 0.0)
         tail = jnp.where(tail_lanes == h, row_top, tail)
         tail = jnp.where(tail_lanes == head_count + h, row_total, tail)
-    out_ref[:, :feat_width] = numer
     out_ref[:, feat_width:] = tail
 
 
 def serve_slots(priors, query_stack, cache_keys, cache_values, head_count):
     slot_count, row_count, feat_width = query_stack.shape
     key_count = cache_keys.shape[1]
-    flops = slot_count * head_count * 4 * row_count * key_count * feat_width
+    window_lanes = sum(
+        min(feat_width, -(-((h + 1) * HD) // 128) * 128) - (h * HD) // 128 * 128
+        for h in range(head_count)
+    )
+    flops = slot_count * 4 * row_count * key_count * window_lanes
     moved = 2 * (query_stack.size + cache_keys.size + cache_values.size) + 4 * slot_count * row_count * RESULT_WIDTH
     return pl.pallas_call(
         functools.partial(prior_kernel, head_count),
@@ -123,18 +126,17 @@
     prior_rows = cache_keys.shape[1]
     req_lens = req_lengths[0]
     req_ends = jnp.cumsum(req_lens)
-    starts = req_ends - req_lens
     positions = jnp.arange(tok_count, dtype=jnp.int32)
     row_marks = jnp.arange(NEWCAP, dtype=jnp.int32)
     prior_marks = jnp.arange(prior_rows, dtype=jnp.int32)
     req_count = lax.axis_size("req")
     req_index = lax.axis_index("req")
-    raw_offset = (cache_owner[0] - req_index + req_count) % req_count
-    offset = jnp.where(raw_offset == req_count - 1, -1, raw_offset)
+
+    first_right = cache_owner[0, 0] == (req_index + 1) % req_count
 
     def request_at(distance):
-        pick = offset[0] == distance
-        start = jnp.where(pick, starts[0], starts[1])
+        pick = first_right if distance == 1 else jnp.logical_not(first_right)
+        start = jnp.where(pick, 0, req_lens[0])
         length = jnp.where(pick, req_lens[0], req_lens[1])
         slot = jnp.where(pick, cache_slot[0, 0], cache_slot[0, 1])
         prior = jnp.where(pick, prior_len[0, 0], prior_len[0, 1])

time: 156 us -> 148 us (0.949)
  Pallas kernels: 14 us -> 9.01 us
  other arithmetic: 18.9 us -> 16.9 us
    pallas_call x1, Pallas kernels: 14 us -> 9.01 us  [serve_slots(): pl.pallas_call(functools.partial(prior_kernel, head_count), out_shape=jax...]
    unnamed x11 -> x13, local copies, waits for them, and re-layouts: 3.31 us -> 3.31 us
where the time goes in v5:
time: 148 us; the launch traced here: 147 us
  waiting for transfers between devices  50.7 us (34%)
  between operations  27.3 us (18%)
  other arithmetic  16.9 us (11%)
  matrix products  15.8 us (11%)
  local copies, waits for them, and re-layouts  14.8 us (10%)
  starting transfers between devices  12.5 us (8%)
  Pallas kernels  9.01 us (6%)
    ppermute x6, waiting for transfers between devices, shifted(): return lax.ppermute(value, axis, pairs)  29.9 us
    reduce_scatter x1, waiting for transfers between devices, body(): lax.psum_scatter(jnp.dot(attended, out_proj, preferred_element_type=jnp.f...  20.8 us
    ppermute x6, starting transfers between devices, shifted(): return lax.ppermute(value, axis, pairs)  12.5 us
    pallas_call x1, Pallas kernels, serve_slots(): pl.pallas_call(functools.partial(prior_kernel, head_count), out_shape=jax...  9.01 us
    dot_general x1, matrix products, body(): jnp.dot(attended, out_proj, preferred_element_type=jnp.float32)  8.37 us
    dot_general x1, matrix products, attend_part(): jnp.einsum('hts,shd->thd', weights.astype(jnp.bfloat16), value_heads, pre...  4.55 us
    unnamed x13, local copies, waits for them, and re-layouts  3.31 us
    reduce_sum x1, other arithmetic, attend_part(): row_total = jnp.sum(weights, axis=2)  3.23 us
  transfers between devices with their start and end apart: 7, of which 5 were waited for; matrix products, arithmetic and copies ran while one was open for 11% of the time, Pallas kernels for 0%

profile of v5, /device:TPU:8, one launch (start us, length us, event | category | flops | bytes accessed | tf_op | source)
XLA Modules:
  0.0 147.2 jit_solution(1639648767179159108)
XLA Ops:
  7.2 1.3 fusion.68
  10.5 1.4 fusion.67
  14.6 1.3 fusion.66
  17.2 1.3 constant_dynamic-slice_fusion
  18.5 1.7 %collective-permute-start = (bf16[200,896]{1,0:T(8,128)(2,1)S(1)}, bf16[200,896]{1,0:T(8,128)(2,1)}, u32[]{:S(2)}, u32[]{:S(2)}) collective-permute-start(bf16[200,896]{1,0:T(8,128)(2,1)S(1)} %pad_maximum_fusion.3), channel_id=1, source_target_pairs={{0,8},{8,16},{16,24},{24,32},{32,40},{40,48},{48,56},{56,64},{64,7... | collective-permute-start | bytes 1075208 | tf_op jit(solution)/shard_map/ppermute | solution.py:23
  25.6 1.5 copy.51
  28.1 2.9 %fusion = (f32[4,512]{1,0:T(4,128)S(1)}, f32[4,512,512]{1,2,0:T(8,128)}) fusion(pred[512,512]{0,1:T(8,128)(4,1)S(1)} %fusion.17, bf16[512,4,224]{0,2,1:T(8,128)(2,1)S(1)} %bitcast.77, bf16[512,4,224]{0,2,1:T(8,128)(2,1)S(1)} %bitcast.78), kind=kOutput, calls=%fused_computation.3 | convolution fusion | flops 472905728 | bytes 6299648 | tf_op jit(solution)/shard_map/thd,shd->hts/dot_general | solution.py:32
  33.0 2.1 %collective-permute-done.1 = bf16[200,896]{1,0:T(8,128)(2,1)} collective-permute-done((bf16[200,896]{1,0:T(8,128)(2,1)}, bf16[200,896]{1,0:T(8,128)(2,1)}, u32[]{:S(2)}, u32[]{:S(2)}) %collective-permute-start.1) | collective-permute-done | bytes 358432 | tf_op jit(solution)/shard_map/ppermute | solution.py:23
  41.7 9.0 %shard_map.121 = f32[2,192,1024]{2,1,0:T(8,128)} custom-call(s32[2]{0:T(128)} %pad_add_fusion.prior_ref, bf16[2,192,896]{2,1,0:T(8,128)(2,1)} %pad_maximum_fusion.2.query_ref, bf16[2,1024,896]{2,1,0:T(8,128)(2,1)} %key_ref.1, bf16[2,1024,896]{2,1,0:T(8,128)(2,1)} %value_ref.1), custom_call_target="tpu_custom_call" | custom-call | flops 2013265920 | bytes 9601024 | tf_op jit(solution)/shard_map/pallas_call | solution.py:89
  50.8 2.9 %select_bitcast_fusion = (f32[192,1024]{1,0:T(8,128)}, f32[192,1024]{1,0:T(8,128)}) fusion(f32[2,192,1024]{2,1,0:T(8,128)} %shard_map.121, pred[]{:T(512)S(6)} %eq.55), kind=kLoop, calls=%fused_computation.22 | loop fusion | flops 393216 | bytes 3145729 | tf_op jit(solution)/shard_map/jit(_where)/select_n | solution.py:180
  53.6 5.0 %collective-permute-start.2 = (f32[192,1024]{1,0:T(8,128)}, f32[192,1024]{1,0:T(8,128)S(1)}, u32[]{:S(2)}, u32[]{:S(2)}) collective-permute-start(f32[192,1024]{1,0:T(8,128)} %get-tuple-element.39), channel_id=1, source_target_pairs={{0,248},{8,0},{16,8},{24,16},{32,24},{40,32},{48,40},{56,48},{64,5... | collective-permute-start | bytes 2359304 | tf_op jit(solution)/shard_map/ppermute | solution.py:23
  58.6 3.2 %fusion.1 = f32[4,512]{1,0:T(4,128)S(1)} fusion(f32[4,512,512]{1,2,0:T(8,128)} %get-tuple-element.73, f32[4,512]{1,0:T(4,128)S(1)} %get-tuple-element.72, pred[512,512]{0,1:T(8,128)(4,1)S(1)} %fusion.17), kind=kLoop, calls=%fused_computation.6 | loop fusion | flops 5240832 | bytes 4472832 | tf_op jit(solution)/shard_map/reduce_sum | solution.py:38
  62.2 1.3 copy.53
  64.0 1.2 pad_maximum_fusion
  65.2 9.7 %collective-permute-done.2 = f32[192,1024]{1,0:T(8,128)S(1)} collective-permute-done((f32[192,1024]{1,0:T(8,128)}, f32[192,1024]{1,0:T(8,128)S(1)}, u32[]{:S(2)}, u32[]{:S(2)}) %collective-permute-start.2) | collective-permute-done | bytes 786464 | tf_op jit(solution)/shard_map/ppermute | solution.py:23
  74.9 6.2 %collective-permute-done.3 = f32[192,1024]{1,0:T(8,128)} collective-permute-done((f32[192,1024]{1,0:T(8,128)}, f32[192,1024]{1,0:T(8,128)}, u32[]{:S(2)}, u32[]{:S(2)}) %collective-permute-start.3) | collective-permute-done | bytes 786464 | tf_op jit(solution)/shard_map/ppermute | solution.py:23
  84.8 1.8 %copy.57 = f32[512,896]{0,1:T(8,128)} copy(f32[512,896]{1,0:T(8,128)S(1)} %fusion.10) | data formatting | bytes 3670016 | tf_op jit(solution)/shard_map/jit(_where)/select_n | solution.py:222
  86.5 4.5 %fusion.14 = bf16[512,4,224]{0,2,1:T(8,128)(2,1)S(1)} fusion(f32[512,4,224]{0,2,1:T(8,128)} %bitcast.75, bf16[512,4,224]{0,2,1:T(8,128)(2,1)} %bitcast.76, f32[4,512,512]{1,2,0:T(8,128)} %get-tuple-element.73, f32[4,512]{1,0:T(4,128)S(1)} %get-tuple-element.72, pred[512,512]{0,1:T(8,128)(4,1)S(1)} %fusion.17, f32[512,4]{0,1:T(4,128)S(1)} %copy.60, ...), kind=kOutput, calls=%fused_computation.19 | convolution fusion | flops 477298688 | bytes 8159232 | tf_op jit(solution)/shard_map/hts,shd->thd/dot_general | solution.py:39
  91.1 8.4 %convolution_convert_fusion = bf16[512,3584]{1,0:T(8,128)(2,1)} fusion(bf16[512,896]{0,1:T(8,128)(2,1)S(1)} %bitcast.82, bf16[896,3584]{1,0:T(8,128)(2,1)} %param.19), kind=kOutput, calls=%fused_computation | convolution fusion | flops 3290169344 | bytes 11010048 | tf_op jit(solution)/shard_map/dot_general | solution.py:238
  99.6 5.1 %collective-permute-start.5 = (bf16[2,192,896]{2,1,0:T(8,128)(2,1)S(1)}, bf16[2,192,896]{2,1,0:T(8,128)(2,1)S(1)}, u32[]{:S(2)}, u32[]{:S(2)}) collective-permute-start(bf16[2,192,896]{2,1,0:T(8,128)(2,1)S(1)} %copy-done.2), channel_id=1, source_target_pairs={{0,248},{8,0},{16,8},{24,16},{32,24},{40,32},{48,40},{56,48},{64,5... | collective-permute-start | bytes 2064392 | tf_op jit(solution)/shard_map/ppermute | solution.py:23
  104.8 1.4 iota_compare_fusion.6
  106.2 11.9 %collective-permute-done.4 = bf16[2,192,896]{2,1,0:T(8,128)(2,1)S(1)} collective-permute-done((bf16[2,192,896]{2,1,0:T(8,128)(2,1)S(1)}, bf16[2,192,896]{2,1,0:T(8,128)(2,1)S(1)}, u32[]{:S(2)}, u32[]{:S(2)}) %collective-permute-start.4) | collective-permute-done | bytes 688160 | tf_op jit(solution)/shard_map/ppermute | solution.py:23
  118.2 1.3 select_select_fusion
  119.5 20.8 %reduce-scatter.2.cloned.1.call-done = bf16[64,3584]{1,0:T(8,128)(2,1)} async-done(((bf16[512,3584]{1,0:T(8,128)(2,1)}), bf16[64,3584]{1,0:T(8,128)(2,1)}) %reduce-scatter.2.cloned.1.call-update) | async-done | bytes 458768 | tf_op jit(solution)/shard_map/reduce_scatter | solution.py:237
  (49 shorter events, 12.7 us)
Async XLA Ops:
  7.2 19.9 %copy-start.4 = (s32[1,4]{1,0:T(1,128)S(1)}, s32[1,4]{1,0:T(1,128)}, u32[]{:S(2)}) copy-start(s32[1,4]{1,0:T(1,128)} %param.20) | copy-start | bytes 52
  7.2 20.3 %copy-start.1 = (bf16[512,896]{1,0:T(8,128)(2,1)S(1)}, bf16[512,896]{1,0:T(8,128)(2,1)}, u32[]{:S(2)}) copy-start(bf16[512,896]{1,0:T(8,128)(2,1)} %param.15) | copy-start | bytes 2752516
  7.2 133.1 %reduce-scatter.2.cloned.1.call-start = ((), (), s32[]{:S(2)}) async-start(), calls=%async_computation.1 | async-start | bytes 4128768 | tf_op jit(solution)/shard_map/reduce_scatter | solution.py:237
  18.5 12.4 %collective-permute-start = (bf16[200,896]{1,0:T(8,128)(2,1)S(1)}, bf16[200,896]{1,0:T(8,128)(2,1)}, u32[]{:S(2)}, u32[]{:S(2)}) collective-permute-start(bf16[200,896]{1,0:T(8,128)(2,1)S(1)} %pad_maximum_fusion.3), channel_id=1, source_target_pairs={{0,8},{8,16},{16,24},{24,32},{32,40},{40,48},{48,56},{56,64},{64,7... | collective-permute-start | bytes 1075208 | tf_op jit(solution)/shard_map/ppermute | solution.py:23
  24.9 10.1 %collective-permute-start.1 = (bf16[200,896]{1,0:T(8,128)(2,1)}, bf16[200,896]{1,0:T(8,128)(2,1)}, u32[]{:S(2)}, u32[]{:S(2)}) collective-permute-start(bf16[200,896]{1,0:T(8,128)(2,1)} %pad_maximum_fusion.4), channel_id=1, source_target_pairs={{0,248},{8,0},{16,8},{24,16},{32,24},{40,32},{48,40},{56,48},{64,5... | collective-permute-start | bytes 1075208 | tf_op jit(solution)/shard_map/ppermute | solution.py:23
  50.7 11.4 %copy-start = (bf16[512,896]{1,0:T(8,128)(2,1)S(1)}, bf16[512,896]{1,0:T(8,128)(2,1)}, u32[]{:S(2)}) copy-start(bf16[512,896]{1,0:T(8,128)(2,1)} %param.16) | copy-start | bytes 2752516
  53.6 21.3 %collective-permute-start.2 = (f32[192,1024]{1,0:T(8,128)}, f32[192,1024]{1,0:T(8,128)S(1)}, u32[]{:S(2)}, u32[]{:S(2)}) collective-permute-start(f32[192,1024]{1,0:T(8,128)} %get-tuple-element.39), channel_id=1, source_target_pairs={{0,248},{8,0},{16,8},{24,16},{32,24},{40,32},{48,40},{56,48},{64,5... | collective-permute-start | bytes 2359304 | tf_op jit(solution)/shard_map/ppermute | solution.py:23
  58.6 22.5 %collective-permute-start.3 = (f32[192,1024]{1,0:T(8,128)}, f32[192,1024]{1,0:T(8,128)}, u32[]{:S(2)}, u32[]{:S(2)}) collective-permute-start(f32[192,1024]{1,0:T(8,128)} %get-tuple-element.38), channel_id=1, source_target_pairs={{0,8},{8,16},{16,24},{24,32},{32,40},{40,48},{48,56},{56,64},{64,7... | collective-permute-start | bytes 2359304 | tf_op jit(solution)/shard_map/ppermute | solution.py:23
  91.1 8.4 %copy-start.3 = (bf16[2,192,896]{2,1,0:T(8,128)(2,1)S(1)}, bf16[2,192,896]{2,1,0:T(8,128)(2,1)}, u32[]{:S(2)}) copy-start(bf16[2,192,896]{2,1,0:T(8,128)(2,1)} %get-tuple-element.33) | copy-start | bytes 2064388
  91.1 8.5 %copy-start.2 = (bf16[2,192,896]{2,1,0:T(8,128)(2,1)S(1)}, bf16[2,192,896]{2,1,0:T(8,128)(2,1)}, u32[]{:S(2)}) copy-start(bf16[2,192,896]{2,1,0:T(8,128)(2,1)} %get-tuple-element.34) | copy-start | bytes 2064388
  99.5 18.5 %collective-permute-start.4 = (bf16[2,192,896]{2,1,0:T(8,128)(2,1)S(1)}, bf16[2,192,896]{2,1,0:T(8,128)(2,1)S(1)}, u32[]{:S(2)}, u32[]{:S(2)}) collective-permute-start(bf16[2,192,896]{2,1,0:T(8,128)(2,1)S(1)} %copy-done.3), channel_id=1, source_target_pairs={{0,8},{8,16},{16,24},{24,32},{32,40},{40,48},{48,56},{56,64},{64,7... | collective-permute-start | bytes 2064392 | tf_op jit(solution)/shard_map/ppermute | solution.py:23
  99.6 18.5 %collective-permute-start.5 = (bf16[2,192,896]{2,1,0:T(8,128)(2,1)S(1)}, bf16[2,192,896]{2,1,0:T(8,128)(2,1)S(1)}, u32[]{:S(2)}, u32[]{:S(2)}) collective-permute-start(bf16[2,192,896]{2,1,0:T(8,128)(2,1)S(1)} %copy-done.2), channel_id=1, source_target_pairs={{0,248},{8,0},{16,8},{24,16},{32,24},{40,32},{48,40},{56,48},{64,5... | collective-permute-start | bytes 2064392 | tf_op jit(solution)/shard_map/ppermute | solution.py:23
Sparse Core Ops, SparseCore 0:
  99.6 40.6 reduce-scatter.1

commit v6 on v5

--- a/solution.py
+++ b/solution.py
@@ -45,7 +45,7 @@
     return (numerator.reshape(row_count, head_count * HD), row_top.T, row_total.T)
 
 
-def prior_kernel(head_count, prior_ref, query_ref, key_ref, value_ref, out_ref):
+def prior_kernel(head_count, prior_ref, query_ref, key_ref, value_ref, out_ref, numer_ref):
     slot = pl.program_id(0)
     prior = prior_ref[slot]
     row_count, feat_width = query_ref.shape
@@ -53,7 +53,7 @@
     live = lax.broadcasted_iota(jnp.int32, (1, key_count), 1) < prior
     tail_lanes = lax.broadcasted_iota(jnp.int32, (row_count, out_ref.shape[1] - feat_width), 1)
     tail = jnp.zeros((row_count, out_ref.shape[1] - feat_width), jnp.float32)
-    out_ref[:, :feat_width] = jnp.zeros((row_count, feat_width), jnp.float32)
+    numer_ref[...] = jnp.zeros((row_count, feat_width), jnp.float32)
     for h in range(head_count):
         low = (h * HD) // 128 * 128
         high = min(feat_width, -(-((h + 1) * HD) // 128) * 128)
@@ -71,10 +71,14 @@
         head_out = jnp.dot(
             weights.astype(jnp.bfloat16), value_ref[:, low:high], preferred_element_type=jnp.float32
         )
-        out_ref[:, low:high] = out_ref[:, low:high] + jnp.where(in_head, head_out, 0.0)
-        tail = jnp.where(tail_lanes == h, row_top, tail)
-        tail = jnp.where(tail_lanes == head_count + h, row_total, tail)
-    out_ref[:, feat_width:] = tail
+        numer_ref[:, low:high] = numer_ref[:, low:high] + jnp.where(in_head, head_out / row_total, 0.0)
+        log_total = row_top + jnp.log(row_total)
+        for part in range(3):
+            piece = log_total.astype(jnp.bfloat16).astype(jnp.float32)
+            tail = jnp.where(tail_lanes == part * head_count + h, piece, tail)
+            log_total = log_total - piece
+    out_ref[:, :feat_width] = numer_ref[...].astype(out_ref.dtype)
+    out_ref[:, feat_width:] = tail.astype(out_ref.dtype)
 
 
 def serve_slots(priors, query_stack, cache_keys, cache_values, head_count):
@@ -85,10 +89,10 @@
         for h in range(head_count)
     )
     flops = slot_count * 4 * row_count * key_count * window_lanes
-    moved = 2 * (query_stack.size + cache_keys.size + cache_values.size) + 4 * slot_count * row_count * RESULT_WIDTH
+    moved = 2 * (query_stack.size + cache_keys.size + cache_values.size) + 2 * slot_count * row_count * RESULT_WIDTH
     return pl.pallas_call(
         functools.partial(prior_kernel, head_count),
-        out_shape=jax.ShapeDtypeStruct((slot_count, row_count, RESULT_WIDTH), jnp.float32),
+        out_shape=jax.ShapeDtypeStruct((slot_count, row_count, RESULT_WIDTH), jnp.bfloat16),
         grid_spec=pltpu.PrefetchScalarGridSpec(
             num_scalar_prefetch=1,
             grid=(slot_count,),
@@ -98,6 +102,7 @@
                 pl.BlockSpec((None, key_count, feat_width), lambda s, pr: (s, 0, 0)),
             ],
             out_specs=pl.BlockSpec((None, row_count, RESULT_WIDTH), lambda s, pr: (s, 0, 0)),
+            scratch_shapes=[pltpu.VMEM((row_count, feat_width), jnp.float32)],
         ),
         cost_estimate=pl.CostEstimate(
             flops=flops,
@@ -198,16 +203,20 @@
     from_right_kv = shifted(left_kv, "req", -1)
 
     def split_result(result):
-        numer = result[:, :feat_width]
-        top = result[:, feat_width : feat_width + head_count]
-        total = result[:, feat_width + head_count : feat_width + 2 * head_count]
-        return numer, top, total
+        scaled = result[:, :feat_width]
+        parts = result[:, feat_width : feat_width + 3 * head_count].astype(jnp.float32)
+        log_total = (
+            parts[:, :head_count]
+            + parts[:, head_count : 2 * head_count]
+            + parts[:, 2 * head_count : 3 * head_count]
+        )
+        return scaled, log_total
 
     got_right = split_result(got_right)
     got_left = split_result(got_left)
 
     def place(result, start, length):
-        numer, top, total = result
+        scaled, log_total = result
         shift = tok_count - start
         keep = ((positions - start >= 0) & (positions - start < length))[:, None]
 
@@ -215,13 +224,15 @@
             padded = jnp.pad(x, ((tok_count, tok_count - NEWCAP), (0, 0)))
             return lax.dynamic_slice_in_dim(padded, shift, tok_count, 0)
 
-        return keep, moved(numer), moved(top), moved(total)
-
-    keep_r, numer_r, top_r, total_r = place(got_right, right_start, right_len)
-    keep_l, numer_l, top_l, total_l = place(got_left, left_start, left_len)
-    prior_numer = jnp.where(keep_r, numer_r, jnp.where(keep_l, numer_l, 0.0))
-    prior_top = jnp.where(keep_r, top_r, jnp.where(keep_l, top_l, floor_value))
-    prior_total = jnp.where(keep_r, total_r, jnp.where(keep_l, total_l, 0.0))
+        return keep, moved(scaled), moved(log_total)
+
+    keep_r, scaled_r, log_r = place(got_right, right_start, right_len)
+    keep_l, scaled_l, log_l = place(got_left, left_start, left_len)
+    prior_scaled = jnp.where(
+        keep_r, scaled_r, jnp.where(keep_l, scaled_l, jnp.zeros((), jnp.bfloat16))
+    ).astype(jnp.float32)
+    prior_top = jnp.where(keep_r, log_r, jnp.where(keep_l, log_l, floor_value))
+    prior_total = jnp.where(keep_r | keep_l, 1.0, 0.0)
 
     both_top = jnp.maximum(own_top, prior_top)
     own_scale = jnp.exp(own_top - both_top)
@@ -229,7 +240,7 @@
     denominator = own_total * own_scale + prior_total * prior_scale
     numerator = (
         own_numer.reshape(tok_count, head_count, HD) * own_scale[:, :, None]
-        + prior_numer.reshape(tok_count, head_count, HD) * prior_scale[:, :, None]
+        + prior_scaled.reshape(tok_count, head_count, HD) * prior_scale[:, :, None]
     )
     attended = (
         (numerator / denominator[:, :, None]).reshape(tok_count, feat_width).astype(jnp.bfloat16)

time: 148 us -> 136 us (0.919)
  waiting for transfers between devices: 50.7 us -> 40.8 us
  other arithmetic: 16.9 us -> 14 us
  starting transfers between devices: 12.5 us -> 14.1 us
    ppermute x6, waiting for transfers between devices: 29.9 us -> 20.9 us  [shifted(): return lax.ppermute(value, axis, pairs)]
    unnamed x13 -> x15, local copies, waits for them, and re-layouts: 3.31 us -> 6.07 us
    slice x4 -> x2, local copies, waits for them, and re-layouts: 2.35 us -> 0.05 us  [split_result(): scaled = result[:, :feat_width]]
    reduce_sum x1, other arithmetic: 3.23 us -> 1.05 us  [attend_part(): row_total = jnp.sum(weights, axis=2)]
    select_n x1 -> x0, local copies, waits for them, and re-layouts: 1.79 us -> none  [body(): prior_numer = jnp.where(keep_r, numer_r, jnp.where(keep_l, numer_l, 0.0))]
    reshape x0 -> x1, local copies, waits for them, and re-layouts: none -> 1.78 us  [body(): prior_scaled.reshape(tok_count, head_count, HD) * prior_scale[:, :, None]]
    select_n x1, other arithmetic: 2.87 us -> 1.17 us  [body(): back_right = jnp.where(left_is_zero, served[1], served[0])]
    ppermute x6, starting transfers between devices: 12.5 us -> 14.1 us  [shifted(): return lax.ppermute(value, axis, pairs)]
  transfers between devices with their start and end apart: 7 -> 7, of which waited for: 5 -> 4; matrix products, arithmetic and copies ran while one was open for 11% -> 11% of each run, Pallas kernels for 0% -> 0%
where the time goes in v6:
time: 136 us; the launch traced here: 135 us
  waiting for transfers between devices  40.8 us (30%)
  between operations  27.1 us (20%)
  local copies, waits for them, and re-layouts  15.2 us (11%)
  matrix products  15.1 us (11%)
  starting transfers between devices  14.1 us (10%)
  other arithmetic  14 us (10%)
  Pallas kernels  9.05 us (7%)
    ppermute x6, waiting for transfers between devices, shifted(): return lax.ppermute(value, axis, pairs)  20.9 us
    reduce_scatter x1, waiting for transfers between devices, body(): lax.psum_scatter(jnp.dot(attended, out_proj, preferred_element_type=jnp.f...  19.9 us
    ppermute x6, starting transfers between devices, shifted(): return lax.ppermute(value, axis, pairs)  14.1 us
    pallas_call x1, Pallas kernels, serve_slots(): pl.pallas_call(functools.partial(prior_kernel, head_count), out_shape=jax...  9.05 us
    dot_general x1, matrix products, body(): jnp.dot(attended, out_proj, preferred_element_type=jnp.float32)  8.39 us
    unnamed x15, local copies, waits for them, and re-layouts  6.07 us
    dot_general x1, matrix products, attend_part(): jnp.einsum('hts,shd->thd', weights.astype(jnp.bfloat16), value_heads, pre...  4.54 us
  transfers between devices with their start and end apart: 7, of which 4 were waited for; matrix products, arithmetic and copies ran while one was open for 11% of the time, Pallas kernels for 0%

profile of v6, /device:TPU:8, one launch (start us, length us, event | category | flops | bytes accessed | tf_op | source)
XLA Modules:
  0.0 135.5 jit_solution(72272440619310924)
XLA Ops:
  7.2 1.3 fusion.66
  10.5 1.3 fusion.65
  14.4 1.4 %fusion.64 = (s32[1,1]{1,0:T(1,128)}, s32[1,1]{1,0:T(1,128)}) fusion(s32[1,2]{1,0:T(1,128)} %param.22), kind=kLoop, calls=%fused_computation.110 | loop fusion | bytes 16 | tf_op jit(solution)/shard_map/slice | solution.py:146
  17.1 1.3 constant_dynamic-slice_fusion
  19.2 1.6 %collective-permute-start = (bf16[200,896]{1,0:T(8,128)(2,1)}, bf16[200,896]{1,0:T(8,128)(2,1)}, u32[]{:S(2)}, u32[]{:S(2)}) collective-permute-start(bf16[200,896]{1,0:T(8,128)(2,1)} %pad_maximum_fusion.3), channel_id=1, source_target_pairs={{0,8},{8,16},{16,24},{24,32},{32,40},{40,48},{48,56},{56,64},{64,7... | collective-permute-start | bytes 1075208 | tf_op jit(solution)/shard_map/ppermute | solution.py:23
  26.1 1.5 %copy.51 = bf16[512,896]{0,1:T(8,128)(2,1)S(1)} copy(bf16[512,896]{1,0:T(8,128)(2,1)} %param.14) | data formatting | bytes 1835008 | tf_op args[0]
  28.0 1.3 copy.52
  29.4 2.2 %fusion = (f32[4,512]{1,0:T(4,128)S(1)}, f32[4,512,512]{1,2,0:T(8,128)S(1)}) fusion(pred[512,512]{0,1:T(8,128)(4,1)S(1)} %fusion.15, bf16[512,4,224]{0,2,1:T(8,128)(2,1)S(1)} %bitcast.77, bf16[512,4,224]{0,2,1:T(8,128)(2,1)} %bitcast.78), kind=kOutput, calls=%fused_computation.3 | convolution fusion | flops 472905728 | bytes 6299648 | tf_op jit(solution)/shard_map/thd,shd->hts/dot_general | solution.py:32
  31.6 2.0 %copy-done = f32[4,512,512]{1,2,0:T(8,128)} copy-done((f32[4,512,512]{1,2,0:T(8,128)}, f32[4,512,512]{1,2,0:T(8,128)S(1)}, u32[]{:S(2)}) %copy-start) | copy-done | bytes 4194328
  34.9 1.3 copy.53
  44.8 9.0 %shard_map.121 = bf16[2,192,1024]{2,1,0:T(8,128)(2,1)} custom-call(s32[2]{0:T(128)} %pad_add_fusion.prior_ref, bf16[2,192,896]{2,1,0:T(8,128)(2,1)} %pad_maximum_fusion.2.query_ref, bf16[2,1024,896]{2,1,0:T(8,128)(2,1)} %key_ref.1, bf16[2,1024,896]{2,1,0:T(8,128)(2,1)} %value_ref.1), custom_call_target="tpu_custom_call" | custom-call | flops 2013265920 | bytes 8814592 | tf_op jit(solution)/shard_map/pallas_call | solution.py:93
  53.9 1.2 select_bitcast_fusion
  55.0 6.7 %collective-permute-start.2 = (bf16[192,1024]{1,0:T(8,128)(2,1)S(1)}, bf16[192,1024]{1,0:T(8,128)(2,1)S(1)}, u32[]{:S(2)}, u32[]{:S(2)}) collective-permute-start(bf16[192,1024]{1,0:T(8,128)(2,1)S(1)} %get-tuple-element.48), channel_id=1, source_target_pairs={{0,248},{8,0},{16,8},{24,16},{32,24},{40,32},{48,40},{56,48},{64,5... | collective-permute-start | bytes 1179656 | tf_op jit(solution)/shard_map/ppermute | solution.py:23
  62.2 1.2 pad_maximum_fusion
  63.4 6.4 %collective-permute-done.2 = bf16[192,1024]{1,0:T(8,128)(2,1)S(1)} collective-permute-done((bf16[192,1024]{1,0:T(8,128)(2,1)S(1)}, bf16[192,1024]{1,0:T(8,128)(2,1)S(1)}, u32[]{:S(2)}, u32[]{:S(2)}) %collective-permute-start.2) | collective-permute-done | bytes 393248 | tf_op jit(solution)/shard_map/ppermute | solution.py:23
  69.8 2.2 %collective-permute-done.3 = bf16[192,1024]{1,0:T(8,128)(2,1)S(1)} collective-permute-done((bf16[192,1024]{1,0:T(8,128)(2,1)S(1)}, bf16[192,1024]{1,0:T(8,128)(2,1)S(1)}, u32[]{:S(2)}, u32[]{:S(2)}) %collective-permute-start.3) | collective-permute-done | bytes 393248 | tf_op jit(solution)/shard_map/ppermute | solution.py:23
  73.7 1.8 %copy.57 = f32[512,896]{0,1:T(8,128)} copy(f32[512,896]{1,0:T(8,128)S(1)} %fusion.17) | data formatting | bytes 3670016 | tf_op jit(solution)/shard_map/reshape | solution.py:243
  75.5 4.5 %fusion.12 = bf16[512,4,224]{0,2,1:T(8,128)(2,1)S(1)} fusion(f32[512,4,224]{0,2,1:T(8,128)} %bitcast.75, bf16[512,4,224]{0,2,1:T(8,128)(2,1)} %bitcast.76, f32[4,512,512]{1,2,0:T(8,128)} %copy-done, f32[4,512]{1,0:T(4,128)S(1)} %get-tuple-element.71, pred[512,512]{0,1:T(8,128)(4,1)S(1)} %fusion.15, f32[512,4]{0,1:T(4,128)S(1)} %copy.60, ...), kind=kOutput, calls=%fused_computation.15 | convolution fusion | flops 477298688 | bytes 8159232 | tf_op jit(solution)/shard_map/hts,shd->thd/dot_general | solution.py:39
  80.0 8.4 %convolution_convert_fusion = bf16[512,3584]{1,0:T(8,128)(2,1)} fusion(bf16[512,896]{0,1:T(8,128)(2,1)S(1)} %bitcast.82, bf16[896,3584]{1,0:T(8,128)(2,1)} %param.19), kind=kOutput, calls=%fused_computation | convolution fusion | flops 3290169344 | bytes 11010048 | tf_op jit(solution)/shard_map/dot_general | solution.py:249
  88.8 4.9 %collective-permute-start.5 = (bf16[2,192,896]{2,1,0:T(8,128)(2,1)S(1)}, bf16[2,192,896]{2,1,0:T(8,128)(2,1)S(1)}, u32[]{:S(2)}, u32[]{:S(2)}) collective-permute-start(bf16[2,192,896]{2,1,0:T(8,128)(2,1)S(1)} %copy-done.3), channel_id=1, source_target_pairs={{0,248},{8,0},{16,8},{24,16},{32,24},{40,32},{48,40},{56,48},{64,5... | collective-permute-start | bytes 2064392 | tf_op jit(solution)/shard_map/ppermute | solution.py:23
  93.7 1.2 iota_compare_fusion.6
  94.9 12.3 %collective-permute-done.4 = bf16[2,192,896]{2,1,0:T(8,128)(2,1)S(1)} collective-permute-done((bf16[2,192,896]{2,1,0:T(8,128)(2,1)S(1)}, bf16[2,192,896]{2,1,0:T(8,128)(2,1)S(1)}, u32[]{:S(2)}, u32[]{:S(2)}) %collective-permute-start.4) | collective-permute-done | bytes 688160 | tf_op jit(solution)/shard_map/ppermute | solution.py:23
  107.4 1.3 select_select_fusion
  108.7 19.9 %reduce-scatter.2.cloned.1.call-done = bf16[64,3584]{1,0:T(8,128)(2,1)} async-done(((bf16[512,3584]{1,0:T(8,128)(2,1)}), bf16[64,3584]{1,0:T(8,128)(2,1)}) %reduce-scatter.2.cloned.1.call-update) | async-done | bytes 458768 | tf_op jit(solution)/shard_map/reduce_scatter | solution.py:248
  (53 shorter events, 12.2 us)
Async XLA Ops:
  7.2 20.4 %copy-start.5 = (s32[1,4]{1,0:T(1,128)S(1)}, s32[1,4]{1,0:T(1,128)}, u32[]{:S(2)}) copy-start(s32[1,4]{1,0:T(1,128)} %param.20) | copy-start | bytes 52
  7.2 20.8 %copy-start.2 = (bf16[512,896]{1,0:T(8,128)(2,1)S(1)}, bf16[512,896]{1,0:T(8,128)(2,1)}, u32[]{:S(2)}) copy-start(bf16[512,896]{1,0:T(8,128)(2,1)} %param.15) | copy-start | bytes 2752516
  7.2 121.4 %reduce-scatter.2.cloned.1.call-start = ((), (), s32[]{:S(2)}) async-start(), calls=%async_computation.1 | async-start | bytes 4128768 | tf_op jit(solution)/shard_map/reduce_scatter | solution.py:248
  19.2 17.1 %collective-permute-start = (bf16[200,896]{1,0:T(8,128)(2,1)}, bf16[200,896]{1,0:T(8,128)(2,1)}, u32[]{:S(2)}, u32[]{:S(2)}) collective-permute-start(bf16[200,896]{1,0:T(8,128)(2,1)} %pad_maximum_fusion.3), channel_id=1, source_target_pairs={{0,8},{8,16},{16,24},{24,32},{32,40},{40,48},{48,56},{56,64},{64,7... | collective-permute-start | bytes 1075208 | tf_op jit(solution)/shard_map/ppermute | solution.py:23
  25.5 12.7 %collective-permute-start.1 = (bf16[200,896]{1,0:T(8,128)(2,1)}, bf16[200,896]{1,0:T(8,128)(2,1)}, u32[]{:S(2)}, u32[]{:S(2)}) collective-permute-start(bf16[200,896]{1,0:T(8,128)(2,1)} %pad_maximum_fusion.4), channel_id=1, source_target_pairs={{0,248},{8,0},{16,8},{24,16},{32,24},{40,32},{48,40},{56,48},{64,5... | collective-permute-start | bytes 1075208 | tf_op jit(solution)/shard_map/ppermute | solution.py:23
  29.4 5.6 %copy-start.1 = (bf16[512,896]{1,0:T(8,128)(2,1)S(1)}, bf16[512,896]{1,0:T(8,128)(2,1)}, u32[]{:S(2)}) copy-start(bf16[512,896]{1,0:T(8,128)(2,1)} %param.16) | copy-start | bytes 2752516
  31.6 2.0 %copy-start = (f32[4,512,512]{1,2,0:T(8,128)}, f32[4,512,512]{1,2,0:T(8,128)S(1)}, u32[]{:S(2)}) copy-start(f32[4,512,512]{1,2,0:T(8,128)S(1)} %get-tuple-element.72) | copy-start | bytes 12582916
  55.0 14.8 %collective-permute-start.2 = (bf16[192,1024]{1,0:T(8,128)(2,1)S(1)}, bf16[192,1024]{1,0:T(8,128)(2,1)S(1)}, u32[]{:S(2)}, u32[]{:S(2)}) collective-permute-start(bf16[192,1024]{1,0:T(8,128)(2,1)S(1)} %get-tuple-element.48), channel_id=1, source_target_pairs={{0,248},{8,0},{16,8},{24,16},{32,24},{40,32},{48,40},{56,48},{64,5... | collective-permute-start | bytes 1179656 | tf_op jit(solution)/shard_map/ppermute | solution.py:23
  61.7 10.3 %collective-permute-start.3 = (bf16[192,1024]{1,0:T(8,128)(2,1)S(1)}, bf16[192,1024]{1,0:T(8,128)(2,1)S(1)}, u32[]{:S(2)}, u32[]{:S(2)}) collective-permute-start(bf16[192,1024]{1,0:T(8,128)(2,1)S(1)} %get-tuple-element.47), channel_id=1, source_target_pairs={{0,8},{8,16},{16,24},{24,32},{32,40},{40,48},{48,56},{56,64},{64,7... | collective-permute-start | bytes 1179656 | tf_op jit(solution)/shard_map/ppermute | solution.py:23
  80.0 8.4 %copy-start.4 = (bf16[2,192,896]{2,1,0:T(8,128)(2,1)S(1)}, bf16[2,192,896]{2,1,0:T(8,128)(2,1)}, u32[]{:S(2)}) copy-start(bf16[2,192,896]{2,1,0:T(8,128)(2,1)} %get-tuple-element.33) | copy-start | bytes 2064388
  80.0 8.8 %copy-start.3 = (bf16[2,192,896]{2,1,0:T(8,128)(2,1)S(1)}, bf16[2,192,896]{2,1,0:T(8,128)(2,1)}, u32[]{:S(2)}) copy-start(bf16[2,192,896]{2,1,0:T(8,128)(2,1)} %get-tuple-element.34) | copy-start | bytes 2064388
  88.5 18.8 %collective-permute-start.4 = (bf16[2,192,896]{2,1,0:T(8,128)(2,1)S(1)}, bf16[2,192,896]{2,1,0:T(8,128)(2,1)S(1)}, u32[]{:S(2)}, u32[]{:S(2)}) collective-permute-start(bf16[2,192,896]{2,1,0:T(8,128)(2,1)S(1)} %copy-done.4), channel_id=1, source_target_pairs={{0,8},{8,16},{16,24},{24,32},{32,40},{40,48},{48,56},{56,64},{64,7... | collective-permute-start | bytes 2064392 | tf_op jit(solution)/shard_map/ppermute | solution.py:23
  88.8 18.5 %collective-permute-start.5 = (bf16[2,192,896]{2,1,0:T(8,128)(2,1)S(1)}, bf16[2,192,896]{2,1,0:T(8,128)(2,1)S(1)}, u32[]{:S(2)}, u32[]{:S(2)}) collective-permute-start(bf16[2,192,896]{2,1,0:T(8,128)(2,1)S(1)} %copy-done.3), channel_id=1, source_target_pairs={{0,248},{8,0},{16,8},{24,16},{32,24},{40,32},{48,40},{56,48},{64,5... | collective-permute-start | bytes 2064392 | tf_op jit(solution)/shard_map/ppermute | solution.py:23
Sparse Core Ops, SparseCore 0:
  88.6 39.9 reduce-scatter.1

commit v7 on v6

--- a/solution.py
+++ b/solution.py
@@ -45,12 +45,27 @@
     return (numerator.reshape(row_count, head_count * HD), row_top.T, row_total.T)
 
 
-def prior_kernel(head_count, prior_ref, query_ref, key_ref, value_ref, out_ref, numer_ref):
+def read_tag(bundle_ref):
+    tag = bundle_ref[NEWCAP : NEWCAP + 1, :].astype(jnp.float32)
+    lanes = lax.broadcasted_iota(jnp.int32, tag.shape, 1)
+
+    def entry(i):
+        return jnp.sum(jnp.where(lanes == i, tag, 0.0), axis=1, keepdims=True)
+
+    return entry(0), entry(1) * 32 + entry(2)
+
+
+def prior_kernel(head_count, left_ref, right_ref, key_ref, value_ref, out_ref, numer_ref):
     slot = pl.program_id(0)
-    prior = prior_ref[slot]
-    row_count, feat_width = query_ref.shape
+    left_slot, left_prior = read_tag(left_ref)
+    right_prior = read_tag(right_ref)[1]
+    from_left = left_slot == slot.astype(jnp.float32)
+    prior = jnp.where(from_left, left_prior, right_prior)
+    row_count = NEWCAP
+    feat_width = left_ref.shape[1]
     key_count = key_ref.shape[0]
-    live = lax.broadcasted_iota(jnp.int32, (1, key_count), 1) < prior
+    query_rows = jnp.where(from_left, left_ref[:NEWCAP, :], right_ref[:NEWCAP, :])
+    live = lax.broadcasted_iota(jnp.int32, (1, key_count), 1).astype(jnp.float32) < prior
     tail_lanes = lax.broadcasted_iota(jnp.int32, (row_count, out_ref.shape[1] - feat_width), 1)
     tail = jnp.zeros((row_count, out_ref.shape[1] - feat_width), jnp.float32)
     numer_ref[...] = jnp.zeros((row_count, feat_width), jnp.float32)
@@ -59,7 +74,7 @@
         high = min(feat_width, -(-((h + 1) * HD) // 128) * 128)
         lanes = low + lax.broadcasted_iota(jnp.int32, (1, high - low), 1)
         in_head = (lanes >= h * HD) & (lanes < (h + 1) * HD)
-        head_query = jnp.where(in_head, query_ref[:, low:high], jnp.zeros((), query_ref.dtype))
+        head_query = jnp.where(in_head, query_rows[:, low:high], jnp.zeros((), query_rows.dtype))
         scores = lax.dot_general(
             head_query, key_ref[:, low:high], (((1,), (1,)), ((), ())),
             preferred_element_type=jnp.float32,
@@ -81,36 +96,37 @@
     out_ref[:, feat_width:] = tail.astype(out_ref.dtype)
 
 
-def serve_slots(priors, query_stack, cache_keys, cache_values, head_count):
-    slot_count, row_count, feat_width = query_stack.shape
-    key_count = cache_keys.shape[1]
+def serve_slots(from_left, from_right, cache_keys, cache_values, head_count):
+    slot_count, key_count, feat_width = cache_keys.shape
+    row_count = NEWCAP
     window_lanes = sum(
         min(feat_width, -(-((h + 1) * HD) // 128) * 128) - (h * HD) // 128 * 128
         for h in range(head_count)
     )
     flops = slot_count * 4 * row_count * key_count * window_lanes
-    moved = 2 * (query_stack.size + cache_keys.size + cache_values.size) + 2 * slot_count * row_count * RESULT_WIDTH
+    moved = (
+        2 * (from_left.size + from_right.size + cache_keys.size + cache_values.size)
+        + 2 * slot_count * row_count * RESULT_WIDTH
+    )
+    bundle_rows = from_left.shape[0]
     return pl.pallas_call(
         functools.partial(prior_kernel, head_count),
         out_shape=jax.ShapeDtypeStruct((slot_count, row_count, RESULT_WIDTH), jnp.bfloat16),
-        grid_spec=pltpu.PrefetchScalarGridSpec(
-            num_scalar_prefetch=1,
-            grid=(slot_count,),
-            in_specs=[
-                pl.BlockSpec((None, row_count, feat_width), lambda s, pr: (s, 0, 0)),
-                pl.BlockSpec((None, key_count, feat_width), lambda s, pr: (s, 0, 0)),
-                pl.BlockSpec((None, key_count, feat_width), lambda s, pr: (s, 0, 0)),
-            ],
-            out_specs=pl.BlockSpec((None, row_count, RESULT_WIDTH), lambda s, pr: (s, 0, 0)),
-            scratch_shapes=[pltpu.VMEM((row_count, feat_width), jnp.float32)],
-        ),
+        grid=(slot_count,),
+        in_specs=[
+            pl.BlockSpec((bundle_rows, feat_width), lambda s: (0, 0)),
+            pl.BlockSpec((bundle_rows, feat_width), lambda s: (0, 0)),
+            pl.BlockSpec((None, key_count, feat_width), lambda s: (s, 0, 0)),
+            pl.BlockSpec((None, key_count, feat_width), lambda s: (s, 0, 0)),
+        ],
+        out_specs=pl.BlockSpec((None, row_count, RESULT_WIDTH), lambda s: (s, 0, 0)),
+        scratch_shapes=[pltpu.VMEM((row_count, feat_width), jnp.float32)],
         cost_estimate=pl.CostEstimate(
             flops=flops,
             transcendentals=slot_count * head_count * row_count * key_count,
             bytes_accessed=moved,
         ),
-    )(priors, query_stack, cache_keys, cache_values)
-
+    )(from_left, from_right, cache_keys, cache_values)
 
 def body(
     queries,
@@ -155,32 +171,19 @@
         tag_rows = jnp.zeros((TAG_ROWS, feat_width), jnp.bfloat16).at[0, :4].set(tag)
         return jnp.concatenate([rows_of(queries, start), tag_rows], axis=0)
 
-    def read_tag(bundle):
-        tag = bundle[NEWCAP, :4].astype(jnp.float32).astype(jnp.int32)
-        return tag[0], tag[1] * 32 + tag[2], tag[3]
-
     right_start, right_len, right_slot, right_prior = request_at(1)
     left_start, left_len, left_slot, left_prior = request_at(-1)
 
     from_left = shifted(query_bundle(right_start, right_len, right_slot, right_prior), "req", 1)
     from_right = shifted(query_bundle(left_start, left_len, left_slot, left_prior), "req", -1)
 
-    segment = jnp.sum((positions[:, None] >= req_ends[None, :]).astype(jnp.int32), axis=1)
+    served = serve_slots(from_left, from_right, cache_keys, cache_values, head_count)
+    left_is_zero = from_left[NEWCAP, 0] == 0
+    held_ends, served = lax.optimization_barrier((req_ends, served))
+    segment = jnp.sum((positions[:, None] >= held_ends[None, :]).astype(jnp.int32), axis=1)
     own_live = (segment[:, None] == segment[None, :]) & (positions[None, :] <= positions[:, None])
     own_numer, own_top, own_total = attend_part(queries, keys_new, values_new, own_live, head_count)
 
-    left_tag = read_tag(from_left)
-    right_tag = read_tag(from_right)
-    left_is_zero = left_tag[0] == 0
-    left_rows = from_left[:NEWCAP]
-    right_rows = from_right[:NEWCAP]
-    query_stack = jnp.stack(
-        [jnp.where(left_is_zero, left_rows, right_rows), jnp.where(left_is_zero, right_rows, left_rows)]
-    )
-    priors = jnp.stack(
-        [jnp.where(left_is_zero, left_tag[1], right_tag[1]), jnp.where(left_is_zero, right_tag[1], left_tag[1])]
-    )
-    served = serve_slots(priors, query_stack, cache_keys, cache_values, head_count)
     back_left = jnp.where(left_is_zero, served[0], served[1])
     back_right = jnp.where(left_is_zero, served[1], served[0])
     got_right = shifted(back_left, "req", -1)
@@ -253,10 +256,12 @@
     )
 
     slot_ids = jnp.arange(slot_count, dtype=jnp.int32)
+    left_slot_id = from_left[NEWCAP, 0].astype(jnp.int32)
+    right_slot_id = from_right[NEWCAP, 0].astype(jnp.int32)
 
     def stored(from_left_rows, from_right_rows):
-        at_left = (slot_ids == left_tag[0])[:, None, None]
-        at_right = (slot_ids == right_tag[0])[:, None, None]
+        at_left = (slot_ids == left_slot_id)[:, None, None]
+        at_right = (slot_ids == right_slot_id)[:, None, None]
         return jnp.where(
             at_left,
             from_left_rows[None],

time: 136 us -> 135 us (level)
  local copies, waits for them, and re-layouts: 15.2 us -> 19.1 us
  other arithmetic: 14 us -> 12.4 us
  starting transfers between devices: 14.1 us -> 12.5 us
    another operation x4 -> x1, other arithmetic: 2.91 us -> 0.18 us  [the longest x2 2.07 us: body(): jnp.stack([jnp.where(left_is_zero, left_rows, right_rows), jnp.where(left...]
    reduce_sum x1, other arithmetic: 1.05 us -> 3.23 us  [attend_part(): row_total = jnp.sum(weights, axis=2)]
    slice x2, local copies, waits for them, and re-layouts: 0.05 us -> 2.01 us  [split_result(): scaled = result[:, :feat_width]]
    ppermute x6, starting transfers between devices: 14.1 us -> 12.5 us  [shifted(): return lax.ppermute(value, axis, pairs)]
    convert_element_type x2, other arithmetic: 0.03 us -> 1.62 us  [split_result(): result[:, feat_width:feat_width + 3 * head_count].astype(jnp.float32)]
    unnamed x15 -> x17, local copies, waits for them, and re-layouts: 6.07 us -> 5.65 us
  transfers between devices with their start and end apart: 7 -> 7, of which waited for: 4 -> 5; matrix products, arithmetic and copies ran while one was open for 11% -> 13% of each run, Pallas kernels for 0% -> 0%
where the time goes in v7:
time: 135 us
  waiting for transfers between devices  40.6 us (30%)
  between operations  25.9 us (19%)
  local copies, waits for them, and re-layouts  19.1 us (14%)
  matrix products  15.8 us (12%)
  starting transfers between devices  12.5 us (9%)
  other arithmetic  12.4 us (9%)
  Pallas kernels  8.44 us (6%)
    ppermute x6, waiting for transfers between devices, shifted(): return lax.ppermute(value, axis, pairs)  20.9 us
    reduce_scatter x1, waiting for transfers between devices, body(): lax.psum_scatter(jnp.dot(attended, out_proj, preferred_element_type=jnp.f...  19.7 us
    ppermute x6, starting transfers between devices, shifted(): return lax.ppermute(value, axis, pairs)  12.5 us
    pallas_call x1, Pallas kernels, serve_slots(): pl.pallas_call(functools.partial(prior_kernel, head_count), out_shape=jax...  8.44 us
    dot_general x1, matrix products, body(): jnp.dot(attended, out_proj, preferred_element_type=jnp.float32)  8.36 us
    unnamed x17, local copies, waits for them, and re-layouts  5.65 us
    dot_general x1, matrix products, attend_part(): jnp.einsum('hts,shd->thd', weights.astype(jnp.bfloat16), value_heads, pre...  4.55 us
    reduce_sum x1, other arithmetic, attend_part(): row_total = jnp.sum(weights, axis=2)  3.23 us
  transfers between devices with their start and end apart: 7, of which 5 were waited for; matrix products, arithmetic and copies ran while one was open for 13% of the time, Pallas kernels for 0%

profile of v7, /device:TPU:8, one launch (start us, length us, event | category | flops | bytes accessed | tf_op | source)
XLA Modules:
  0.0 134.7 jit_solution(14745083888678115721)
XLA Ops:
  7.3 1.4 %fusion.62 = (s32[1,1]{1,0:T(1,128)}, s32[1,1]{1,0:T(1,128)}) fusion(s32[1,4]{1,0:T(1,128)} %param.20), kind=kLoop, calls=%fused_computation.102 | loop fusion | bytes 16 | tf_op jit(solution)/shard_map/slice | solution.py:161
  10.6 1.4 %fusion.61 = (s32[1,1]{1,0:T(1,128)}, s32[1,1]{1,0:T(1,128)}) fusion(s32[1,2]{1,0:T(1,128)} %param.23), kind=kLoop, calls=%fused_computation.101 | loop fusion | bytes 16 | tf_op jit(solution)/shard_map/slice | solution.py:163
  14.6 1.3 fusion.60
  17.1 1.3 constant_dynamic-slice_fusion
  18.5 1.7 %collective-permute-start = (bf16[200,896]{1,0:T(8,128)(2,1)S(1)}, bf16[200,896]{1,0:T(8,128)(2,1)}, u32[]{:S(2)}, u32[]{:S(2)}) collective-permute-start(bf16[200,896]{1,0:T(8,128)(2,1)S(1)} %pad_maximum_fusion.2), channel_id=1, source_target_pairs={{0,8},{8,16},{16,24},{24,32},{32,40},{40,48},{48,56},{56,64},{64,7... | collective-permute-start | bytes 1075208 | tf_op jit(solution)/shard_map/ppermute | solution.py:23
  25.5 2.3 %copy.51 = bf16[512,896]{0,1:T(8,128)(2,1)} copy(bf16[512,896]{1,0:T(8,128)(2,1)} %param.14) | data formatting | bytes 1835008 | tf_op args[0]
  27.9 1.3 copy.52
  29.3 1.3 copy.53
  32.1 2.9 %collective-permute-done.1.right_ref = bf16[200,896]{1,0:T(8,128)(2,1)} collective-permute-done((bf16[200,896]{1,0:T(8,128)(2,1)}, bf16[200,896]{1,0:T(8,128)(2,1)}, u32[]{:S(2)}, u32[]{:S(2)}) %collective-permute-start.1) | collective-permute-done | bytes 358432 | tf_op jit(solution)/shard_map/ppermute | solution.py:23
  35.0 8.4 %shard_map.121 = bf16[2,192,1024]{2,1,0:T(8,128)(2,1)} custom-call(bf16[200,896]{1,0:T(8,128)(2,1)} %collective-permute-done.left_ref, bf16[200,896]{1,0:T(8,128)(2,1)} %collective-permute-done.1.right_ref, bf16[2,1024,896]{2,1,0:T(8,128)(2,1)} %key_ref.1, bf16[2,1024,896]{2,1,0:T(8,128)(2,1)} %value_ref.1), custom_call_target="tpu_custom_call" | custom-call | flops 2013265920 | bytes 8843264 | tf_op jit(solution)/shard_map/pallas_call | solution.py:112
  43.4 1.2 slice.145
  45.4 2.0 %select_bitcast_fusion = (bf16[192,1024]{1,0:T(8,128)(2,1)}, bf16[192,1024]{1,0:T(8,128)(2,1)}) fusion(pred[]{:T(512)} %bitcast.26, bf16[2,192,1024]{2,1,0:T(8,128)(2,1)} %shard_map.121), kind=kLoop, calls=%fused_computation.29 | loop fusion | flops 393216 | bytes 1572865 | tf_op jit(solution)/shard_map/jit(_where)/select_n | solution.py:188
  47.4 5.0 %collective-permute-start.2 = (bf16[192,1024]{1,0:T(8,128)(2,1)}, bf16[192,1024]{1,0:T(8,128)(2,1)}, u32[]{:S(2)}, u32[]{:S(2)}) collective-permute-start(bf16[192,1024]{1,0:T(8,128)(2,1)} %get-tuple-element.52), channel_id=1, source_target_pairs={{0,248},{8,0},{16,8},{24,16},{32,24},{40,32},{48,40},{56,48},{64,5... | collective-permute-start | bytes 1179656 | tf_op jit(solution)/shard_map/ppermute | solution.py:23
  52.7 2.9 %fusion = (f32[4,512]{1,0:T(4,128)S(1)}, f32[4,512,512]{1,2,0:T(8,128)}) fusion(pred[512,512]{0,1:T(8,128)(4,1)S(1)} %fusion.15, bf16[512,4,224]{0,2,1:T(8,128)(2,1)S(1)} %bitcast.72, bf16[512,4,224]{0,2,1:T(8,128)(2,1)S(1)} %bitcast.73), kind=kOutput, calls=%fused_computation.3 | convolution fusion | flops 472905728 | bytes 6299648 | tf_op jit(solution)/shard_map/thd,shd->hts/dot_general | solution.py:32
  55.8 3.2 %fusion.1 = f32[4,512]{1,0:T(4,128)S(1)} fusion(f32[4,512,512]{1,2,0:T(8,128)} %get-tuple-element.68, f32[4,512]{1,0:T(4,128)S(1)} %get-tuple-element.67, pred[512,512]{0,1:T(8,128)(4,1)S(1)} %fusion.15), kind=kLoop, calls=%fused_computation.4 | loop fusion | flops 5240832 | bytes 4472832 | tf_op jit(solution)/shard_map/reduce_sum | solution.py:38
  60.2 6.2 %collective-permute-done.3 = bf16[192,1024]{1,0:T(8,128)(2,1)S(1)} collective-permute-done((bf16[192,1024]{1,0:T(8,128)(2,1)}, bf16[192,1024]{1,0:T(8,128)(2,1)S(1)}, u32[]{:S(2)}, u32[]{:S(2)}) %collective-permute-start.3) | collective-permute-done | bytes 393248 | tf_op jit(solution)/shard_map/ppermute | solution.py:23
  72.4 1.8 %copy.57 = f32[512,896]{0,1:T(8,128)} copy(f32[512,896]{1,0:T(8,128)S(1)} %fusion.17) | data formatting | bytes 3670016 | tf_op jit(solution)/shard_map/reshape | solution.py:246
  74.2 4.5 %fusion.12 = bf16[512,4,224]{0,2,1:T(8,128)(2,1)S(1)} fusion(f32[512,4,224]{0,2,1:T(8,128)} %bitcast.70, bf16[512,4,224]{0,2,1:T(8,128)(2,1)} %bitcast.71, f32[4,512,512]{1,2,0:T(8,128)} %get-tuple-element.68, f32[4,512]{1,0:T(4,128)S(1)} %get-tuple-element.67, pred[512,512]{0,1:T(8,128)(4,1)S(1)} %fusion.15, f32[512,4]{0,1:T(4,128)S(1)} %copy.60, ...), kind=kOutput, calls=%fused_computation.15 | convolution fusion | flops 477298688 | bytes 8159232 | tf_op jit(solution)/shard_map/hts,shd->thd/dot_general | solution.py:39
  78.7 8.4 %convolution_convert_fusion = bf16[512,3584]{1,0:T(8,128)(2,1)} fusion(bf16[512,896]{0,1:T(8,128)(2,1)S(1)} %bitcast.77, bf16[896,3584]{1,0:T(8,128)(2,1)} %param.19), kind=kOutput, calls=%fused_computation | convolution fusion | flops 3290169344 | bytes 11010048 | tf_op jit(solution)/shard_map/dot_general | solution.py:252
  87.2 5.1 %collective-permute-start.5 = (bf16[2,192,896]{2,1,0:T(8,128)(2,1)S(1)}, bf16[2,192,896]{2,1,0:T(8,128)(2,1)}, u32[]{:S(2)}, u32[]{:S(2)}) collective-permute-start(bf16[2,192,896]{2,1,0:T(8,128)(2,1)S(1)} %get-tuple-element.38), channel_id=1, source_target_pairs={{0,248},{8,0},{16,8},{24,16},{32,24},{40,32},{48,40},{56,48},{64,5... | collective-permute-start | bytes 2064392 | tf_op jit(solution)/shard_map/ppermute | solution.py:23
  93.0 1.2 slice.153
  94.9 10.7 %collective-permute-done.4 = bf16[2,192,896]{2,1,0:T(8,128)(2,1)S(1)} collective-permute-done((bf16[2,192,896]{2,1,0:T(8,128)(2,1)S(1)}, bf16[2,192,896]{2,1,0:T(8,128)(2,1)S(1)}, u32[]{:S(2)}, u32[]{:S(2)}) %collective-permute-start.4) | collective-permute-done | bytes 688160 | tf_op jit(solution)/shard_map/ppermute | solution.py:23
  106.9 1.3 select_select_fusion
  108.2 19.7 %reduce-scatter.2.cloned.1.call-done = bf16[64,3584]{1,0:T(8,128)(2,1)} async-done(((bf16[512,3584]{1,0:T(8,128)(2,1)}), bf16[64,3584]{1,0:T(8,128)(2,1)}) %reduce-scatter.2.cloned.1.call-update) | async-done | bytes 458768 | tf_op jit(solution)/shard_map/reduce_scatter | solution.py:251
  (50 shorter events, 12.2 us)
Async XLA Ops:
  7.2 20.6 %copy-start.6 = (s32[1,4]{1,0:T(1,128)S(1)}, s32[1,4]{1,0:T(1,128)}, u32[]{:S(2)}) copy-start(s32[1,4]{1,0:T(1,128)} %param.20) | copy-start | bytes 52
  7.2 20.8 %copy-start.1 = (bf16[512,896]{1,0:T(8,128)(2,1)S(1)}, bf16[512,896]{1,0:T(8,128)(2,1)}, u32[]{:S(2)}) copy-start(bf16[512,896]{1,0:T(8,128)(2,1)} %param.15) | copy-start | bytes 2752516
  7.2 22.1 %copy-start = (bf16[512,896]{1,0:T(8,128)(2,1)S(1)}, bf16[512,896]{1,0:T(8,128)(2,1)}, u32[]{:S(2)}) copy-start(bf16[512,896]{1,0:T(8,128)(2,1)} %param.16) | copy-start | bytes 2752516
  7.2 120.7 %reduce-scatter.2.cloned.1.call-start = ((), (), s32[]{:S(2)}) async-start(), calls=%async_computation.1 | async-start | bytes 4128768 | tf_op jit(solution)/shard_map/reduce_scatter | solution.py:251
  18.5 13.5 %collective-permute-start = (bf16[200,896]{1,0:T(8,128)(2,1)S(1)}, bf16[200,896]{1,0:T(8,128)(2,1)}, u32[]{:S(2)}, u32[]{:S(2)}) collective-permute-start(bf16[200,896]{1,0:T(8,128)(2,1)S(1)} %pad_maximum_fusion.2), channel_id=1, source_target_pairs={{0,8},{8,16},{16,24},{24,32},{32,40},{40,48},{48,56},{56,64},{64,7... | collective-permute-start | bytes 1075208 | tf_op jit(solution)/shard_map/ppermute | solution.py:23
  24.9 10.1 %collective-permute-start.1 = (bf16[200,896]{1,0:T(8,128)(2,1)}, bf16[200,896]{1,0:T(8,128)(2,1)}, u32[]{:S(2)}, u32[]{:S(2)}) collective-permute-start(bf16[200,896]{1,0:T(8,128)(2,1)} %pad_maximum_fusion.3), channel_id=1, source_target_pairs={{0,248},{8,0},{16,8},{24,16},{32,24},{40,32},{48,40},{56,48},{64,5... | collective-permute-start | bytes 1075208 | tf_op jit(solution)/shard_map/ppermute | solution.py:23
  32.1 20.7 %copy-start.2 = (bf16[512,896]{0,1:T(8,128)(2,1)S(1)}, bf16[512,896]{0,1:T(8,128)(2,1)}, u32[]{:S(2)}) copy-start(bf16[512,896]{0,1:T(8,128)(2,1)} %copy.51) | copy-start | bytes 2752516
  32.1 20.7 %copy-start.3 = (bf16[512,896]{0,1:T(8,128)(2,1)S(1)}, bf16[512,896]{0,1:T(8,128)(2,1)}, u32[]{:S(2)}) copy-start(bf16[512,896]{0,1:T(8,128)(2,1)} %copy.52) | copy-start | bytes 2752516
  47.4 12.8 %collective-permute-start.2 = (bf16[192,1024]{1,0:T(8,128)(2,1)}, bf16[192,1024]{1,0:T(8,128)(2,1)}, u32[]{:S(2)}, u32[]{:S(2)}) collective-permute-start(bf16[192,1024]{1,0:T(8,128)(2,1)} %get-tuple-element.52), channel_id=1, source_target_pairs={{0,248},{8,0},{16,8},{24,16},{32,24},{40,32},{48,40},{56,48},{64,5... | collective-permute-start | bytes 1179656 | tf_op jit(solution)/shard_map/ppermute | solution.py:23
  52.4 14.0 %collective-permute-start.3 = (bf16[192,1024]{1,0:T(8,128)(2,1)}, bf16[192,1024]{1,0:T(8,128)(2,1)S(1)}, u32[]{:S(2)}, u32[]{:S(2)}) collective-permute-start(bf16[192,1024]{1,0:T(8,128)(2,1)} %get-tuple-element.51), channel_id=1, source_target_pairs={{0,8},{8,16},{16,24},{24,32},{32,40},{40,48},{48,56},{56,64},{64,7... | collective-permute-start | bytes 1179656 | tf_op jit(solution)/shard_map/ppermute | solution.py:23
  66.4 0.7 copy-start.5
  78.7 8.4 %copy-start.4 = (bf16[2,192,896]{2,1,0:T(8,128)(2,1)S(1)}, bf16[2,192,896]{2,1,0:T(8,128)(2,1)}, u32[]{:S(2)}) copy-start(bf16[2,192,896]{2,1,0:T(8,128)(2,1)} %get-tuple-element.37) | copy-start | bytes 2064388
  87.1 18.5 %collective-permute-start.4 = (bf16[2,192,896]{2,1,0:T(8,128)(2,1)S(1)}, bf16[2,192,896]{2,1,0:T(8,128)(2,1)S(1)}, u32[]{:S(2)}, u32[]{:S(2)}) collective-permute-start(bf16[2,192,896]{2,1,0:T(8,128)(2,1)S(1)} %copy-done.4), channel_id=1, source_target_pairs={{0,8},{8,16},{16,24},{24,32},{32,40},{40,48},{48,56},{56,64},{64,7... | collective-permute-start | bytes 2064392 | tf_op jit(solution)/shard_map/ppermute | solution.py:23
  87.2 18.5 %collective-permute-start.5 = (bf16[2,192,896]{2,1,0:T(8,128)(2,1)S(1)}, bf16[2,192,896]{2,1,0:T(8,128)(2,1)}, u32[]{:S(2)}, u32[]{:S(2)}) collective-permute-start(bf16[2,192,896]{2,1,0:T(8,128)(2,1)S(1)} %get-tuple-element.38), channel_id=1, source_target_pairs={{0,248},{8,0},{16,8},{24,16},{32,24},{40,32},{48,40},{56,48},{64,5... | collective-permute-start | bytes 2064392 | tf_op jit(solution)/shard_map/ppermute | solution.py:23
Sparse Core Ops, SparseCore 0:
  87.2 40.6 reduce-scatter.1

commit v8 on v7

--- a/solution.py
+++ b/solution.py
@@ -55,7 +55,7 @@
     return entry(0), entry(1) * 32 + entry(2)
 
 
-def prior_kernel(head_count, left_ref, right_ref, key_ref, value_ref, out_ref, numer_ref):
+def prior_kernel(head_count, left_ref, right_ref, key_ref, value_ref, to_left_ref, to_right_ref, numer_ref):
     slot = pl.program_id(0)
     left_slot, left_prior = read_tag(left_ref)
     right_prior = read_tag(right_ref)[1]
@@ -66,8 +66,9 @@
     key_count = key_ref.shape[0]
     query_rows = jnp.where(from_left, left_ref[:NEWCAP, :], right_ref[:NEWCAP, :])
     live = lax.broadcasted_iota(jnp.int32, (1, key_count), 1).astype(jnp.float32) < prior
-    tail_lanes = lax.broadcasted_iota(jnp.int32, (row_count, out_ref.shape[1] - feat_width), 1)
-    tail = jnp.zeros((row_count, out_ref.shape[1] - feat_width), jnp.float32)
+    result_width = to_left_ref.shape[1]
+    tail_lanes = lax.broadcasted_iota(jnp.int32, (row_count, result_width - feat_width), 1)
+    tail = jnp.zeros((row_count, result_width - feat_width), jnp.float32)
     numer_ref[...] = jnp.zeros((row_count, feat_width), jnp.float32)
     for h in range(head_count):
         low = (h * HD) // 128 * 128
@@ -92,8 +93,13 @@
             piece = log_total.astype(jnp.bfloat16).astype(jnp.float32)
             tail = jnp.where(tail_lanes == part * head_count + h, piece, tail)
             log_total = log_total - piece
-    out_ref[:, :feat_width] = numer_ref[...].astype(out_ref.dtype)
-    out_ref[:, feat_width:] = tail.astype(out_ref.dtype)
+    for side_ref, mine in ((to_left_ref, from_left), (to_right_ref, jnp.logical_not(from_left))):
+        side_ref[:, :feat_width] = jnp.where(
+            mine, numer_ref[...].astype(side_ref.dtype), side_ref[:, :feat_width]
+        )
+        side_ref[:, feat_width:] = jnp.where(
+            mine, tail.astype(side_ref.dtype), side_ref[:, feat_width:]
+        )
 
 
 def serve_slots(from_left, from_right, cache_keys, cache_values, head_count):
@@ -111,7 +117,10 @@
     bundle_rows = from_left.shape[0]
     return pl.pallas_call(
         functools.partial(prior_kernel, head_count),
-        out_shape=jax.ShapeDtypeStruct((slot_count, row_count, RESULT_WIDTH), jnp.bfloat16),
+        out_shape=(
+            jax.ShapeDtypeStruct((row_count, RESULT_WIDTH), jnp.bfloat16),
+            jax.ShapeDtypeStruct((row_count, RESULT_WIDTH), jnp.bfloat16),
+        ),
         grid=(slot_count,),
         in_specs=[
             pl.BlockSpec((bundle_rows, feat_width), lambda s: (0, 0)),
@@ -119,7 +128,10 @@
             pl.BlockSpec((None, key_count, feat_width), lambda s: (s, 0, 0)),
             pl.BlockSpec((None, key_count, feat_width), lambda s: (s, 0, 0)),
         ],
-        out_specs=pl.BlockSpec((None, row_count, RESULT_WIDTH), lambda s: (s, 0, 0)),
+        out_specs=(
+            pl.BlockSpec((row_count, RESULT_WIDTH), lambda s: (0, 0)),
+            pl.BlockSpec((row_count, RESULT_WIDTH), lambda s: (0, 0)),
+        ),
         scratch_shapes=[pltpu.VMEM((row_count, feat_width), jnp.float32)],
         cost_estimate=pl.CostEstimate(
             flops=flops,
@@ -178,14 +190,12 @@
     from_right = shifted(query_bundle(left_start, left_len, left_slot, left_prior), "req", -1)
 
     served = serve_slots(from_left, from_right, cache_keys, cache_values, head_count)
-    left_is_zero = from_left[NEWCAP, 0] == 0
     held_ends, served = lax.optimization_barrier((req_ends, served))
     segment = jnp.sum((positions[:, None] >= held_ends[None, :]).astype(jnp.int32), axis=1)
     own_live = (segment[:, None] == segment[None, :]) & (positions[None, :] <= positions[:, None])
     own_numer, own_top, own_total = attend_part(queries, keys_new, values_new, own_live, head_count)
 
-    back_left = jnp.where(left_is_zero, served[0], served[1])
-    back_right = jnp.where(left_is_zero, served[1], served[0])
+    back_left, back_right = served
     got_right = shifted(back_left, "req", -1)
     got_left = shifted(back_right, "req", 1)
 

time: 135 us -> 132 us (0.978)
  other arithmetic: 12.4 us -> 10.3 us
    select_n x1 -> x0, other arithmetic: 2.05 us -> none  [body(): back_right = jnp.where(left_is_zero, served[1], served[0])]
  transfers between devices with their start and end apart: 7 -> 7, of which waited for: 5 -> 5; matrix products, arithmetic and copies ran while one was open for 13% -> 15% of each run, Pallas kernels for 0% -> 0%
where the time goes in v8:
time: 132 us; the launch traced here: 131 us
  waiting for transfers between devices  39.5 us (30%)
  between operations  25.2 us (19%)
  local copies, waits for them, and re-layouts  19 us (14%)
  matrix products  15.8 us (12%)
  starting transfers between devices  12.5 us (9%)
  other arithmetic  10.3 us (8%)
  Pallas kernels  8.72 us (7%)
    reduce_scatter x1, waiting for transfers between devices, body(): lax.psum_scatter(jnp.dot(attended, out_proj, preferred_element_type=jnp.f...  19.7 us
    ppermute x6, waiting for transfers between devices, shifted(): return lax.ppermute(value, axis, pairs)  19.7 us
    ppermute x6, starting transfers between devices, shifted(): return lax.ppermute(value, axis, pairs)  12.5 us
    pallas_call x1, Pallas kernels, serve_slots(): pl.pallas_call(functools.partial(prior_kernel, head_count), out_shape=(ja...  8.72 us
    dot_general x1, matrix products, body(): jnp.dot(attended, out_proj, preferred_element_type=jnp.float32)  8.36 us
    unnamed x17, local copies, waits for them, and re-layouts  5.65 us
    dot_general x1, matrix products, attend_part(): jnp.einsum('hts,shd->thd', weights.astype(jnp.bfloat16), value_heads, pre...  4.55 us
    reduce_sum x1, other arithmetic, attend_part(): row_total = jnp.sum(weights, axis=2)  3.23 us
  transfers between devices with their start and end apart: 7, of which 5 were waited for; matrix products, arithmetic and copies ran while one was open for 15% of the time, Pallas kernels for 0%

profile of v8, /device:TPU:8, one launch (start us, length us, event | category | flops | bytes accessed | tf_op | source)
XLA Modules:
  0.0 131.0 jit_solution(8929195998679561667)
XLA Ops:
  7.3 1.4 %fusion.62 = (s32[1,1]{1,0:T(1,128)}, s32[1,1]{1,0:T(1,128)}) fusion(s32[1,4]{1,0:T(1,128)} %param.20), kind=kLoop, calls=%fused_computation.100 | loop fusion | bytes 16 | tf_op jit(solution)/shard_map/slice | solution.py:173
  10.6 1.4 %fusion.61 = (s32[1,1]{1,0:T(1,128)}, s32[1,1]{1,0:T(1,128)}) fusion(s32[1,2]{1,0:T(1,128)} %param.23), kind=kLoop, calls=%fused_computation.99 | loop fusion | bytes 16 | tf_op jit(solution)/shard_map/slice | solution.py:175
  14.6 1.3 %fusion.60 = (s32[1,1]{1,0:T(1,128)}, s32[1,1]{1,0:T(1,128)}) fusion(s32[1,2]{1,0:T(1,128)} %param.22), kind=kLoop, calls=%fused_computation.98 | loop fusion | bytes 16 | tf_op jit(solution)/shard_map/slice | solution.py:174
  17.1 1.3 constant_dynamic-slice_fusion
  18.5 1.7 %collective-permute-start = (bf16[200,896]{1,0:T(8,128)(2,1)S(1)}, bf16[200,896]{1,0:T(8,128)(2,1)}, u32[]{:S(2)}, u32[]{:S(2)}) collective-permute-start(bf16[200,896]{1,0:T(8,128)(2,1)S(1)} %pad_maximum_fusion.2), channel_id=1, source_target_pairs={{0,8},{8,16},{16,24},{24,32},{32,40},{40,48},{48,56},{56,64},{64,7... | collective-permute-start | bytes 1075208 | tf_op jit(solution)/shard_map/ppermute | solution.py:23
  25.5 2.3 %copy.51 = bf16[512,896]{0,1:T(8,128)(2,1)} copy(bf16[512,896]{1,0:T(8,128)(2,1)} %param.14) | data formatting | bytes 1835008 | tf_op args[0]
  27.9 1.3 %copy.52 = bf16[512,896]{0,1:T(8,128)(2,1)} copy(bf16[512,896]{1,0:T(8,128)(2,1)S(1)} %copy-done.1) | data formatting | bytes 1835008 | tf_op args[1]
  29.3 1.3 copy.53
  32.1 2.9 %collective-permute-done.1.right_ref = bf16[200,896]{1,0:T(8,128)(2,1)} collective-permute-done((bf16[200,896]{1,0:T(8,128)(2,1)}, bf16[200,896]{1,0:T(8,128)(2,1)}, u32[]{:S(2)}, u32[]{:S(2)}) %collective-permute-start.1) | collective-permute-done | bytes 358432 | tf_op jit(solution)/shard_map/ppermute | solution.py:23
  35.0 8.7 %shard_map.121 = (bf16[192,1024]{1,0:T(8,128)(2,1)}, bf16[192,1024]{1,0:T(8,128)(2,1)}) custom-call(bf16[200,896]{1,0:T(8,128)(2,1)} %collective-permute-done.left_ref, bf16[200,896]{1,0:T(8,128)(2,1)} %collective-permute-done.1.right_ref, bf16[2,1024,896]{2,1,0:T(8,128)(2,1)} %key_ref.1, bf16[2,1024,896]{2,1,0:T(8,128)(2,1)} %value_ref.1), custom_call_target="tpu_custom_call" | custom-call | flops 2013265920 | bytes 8843264 | tf_op jit(solution)/shard_map/pallas_call | solution.py:118
  43.7 5.0 %collective-permute-start.2 = (bf16[192,1024]{1,0:T(8,128)(2,1)}, bf16[192,1024]{1,0:T(8,128)(2,1)}, u32[]{:S(2)}, u32[]{:S(2)}) collective-permute-start(bf16[192,1024]{1,0:T(8,128)(2,1)} %get-tuple-element.39), channel_id=1, source_target_pairs={{0,248},{8,0},{16,8},{24,16},{32,24},{40,32},{48,40},{56,48},{64,5... | collective-permute-start | bytes 1179656 | tf_op jit(solution)/shard_map/ppermute | solution.py:23
  49.0 2.9 %fusion = (f32[4,512]{1,0:T(4,128)S(1)}, f32[4,512,512]{1,2,0:T(8,128)}) fusion(pred[512,512]{0,1:T(8,128)(4,1)S(1)} %fusion.15, bf16[512,4,224]{0,2,1:T(8,128)(2,1)S(1)} %bitcast.67, bf16[512,4,224]{0,2,1:T(8,128)(2,1)S(1)} %bitcast.68), kind=kOutput, calls=%fused_computation.3 | convolution fusion | flops 472905728 | bytes 6299648 | tf_op jit(solution)/shard_map/thd,shd->hts/dot_general | solution.py:32
  52.1 3.2 %fusion.1 = f32[4,512]{1,0:T(4,128)S(1)} fusion(f32[4,512,512]{1,2,0:T(8,128)} %get-tuple-element.72, f32[4,512]{1,0:T(4,128)S(1)} %get-tuple-element.71, pred[512,512]{0,1:T(8,128)(4,1)S(1)} %fusion.15), kind=kLoop, calls=%fused_computation.4 | loop fusion | flops 5240832 | bytes 4472832 | tf_op jit(solution)/shard_map/reduce_sum | solution.py:38
  56.5 6.1 %collective-permute-done.3 = bf16[192,1024]{1,0:T(8,128)(2,1)S(1)} collective-permute-done((bf16[192,1024]{1,0:T(8,128)(2,1)}, bf16[192,1024]{1,0:T(8,128)(2,1)S(1)}, u32[]{:S(2)}, u32[]{:S(2)}) %collective-permute-start.3) | collective-permute-done | bytes 393248 | tf_op jit(solution)/shard_map/ppermute | solution.py:23
  68.6 1.8 %copy.57 = f32[512,896]{0,1:T(8,128)} copy(f32[512,896]{1,0:T(8,128)S(1)} %fusion.17) | data formatting | bytes 3670016 | tf_op jit(solution)/shard_map/reshape | solution.py:256
  70.4 4.5 %fusion.12 = bf16[512,4,224]{0,2,1:T(8,128)(2,1)S(1)} fusion(f32[512,4,224]{0,2,1:T(8,128)} %bitcast.65, bf16[512,4,224]{0,2,1:T(8,128)(2,1)} %bitcast.66, f32[4,512,512]{1,2,0:T(8,128)} %get-tuple-element.72, f32[4,512]{1,0:T(4,128)S(1)} %get-tuple-element.71, pred[512,512]{0,1:T(8,128)(4,1)S(1)} %fusion.15, f32[512,4]{0,1:T(4,128)S(1)} %copy.60, ...), kind=kOutput, calls=%fused_computation.15 | convolution fusion | flops 477298688 | bytes 8159232 | tf_op jit(solution)/shard_map/hts,shd->thd/dot_general | solution.py:39
  75.0 8.4 %convolution_convert_fusion = bf16[512,3584]{1,0:T(8,128)(2,1)} fusion(bf16[512,896]{0,1:T(8,128)(2,1)S(1)} %bitcast.72, bf16[896,3584]{1,0:T(8,128)(2,1)} %param.19), kind=kOutput, calls=%fused_computation | convolution fusion | flops 3290169344 | bytes 11010048 | tf_op jit(solution)/shard_map/dot_general | solution.py:262
  83.5 5.1 %collective-permute-start.5 = (bf16[2,192,896]{2,1,0:T(8,128)(2,1)S(1)}, bf16[2,192,896]{2,1,0:T(8,128)(2,1)}, u32[]{:S(2)}, u32[]{:S(2)}) collective-permute-start(bf16[2,192,896]{2,1,0:T(8,128)(2,1)S(1)} %get-tuple-element.44), channel_id=1, source_target_pairs={{0,248},{8,0},{16,8},{24,16},{32,24},{40,32},{48,40},{56,48},{64,5... | collective-permute-start | bytes 2064392 | tf_op jit(solution)/shard_map/ppermute | solution.py:23
  88.6 1.2 slice.140
  90.5 1.2 slice.142
  92.3 9.6 %collective-permute-done.4 = bf16[2,192,896]{2,1,0:T(8,128)(2,1)S(1)} collective-permute-done((bf16[2,192,896]{2,1,0:T(8,128)(2,1)S(1)}, bf16[2,192,896]{2,1,0:T(8,128)(2,1)S(1)}, u32[]{:S(2)}, u32[]{:S(2)}) %collective-permute-start.4) | collective-permute-done | bytes 688160 | tf_op jit(solution)/shard_map/ppermute | solution.py:23
  102.0 1.2 slice_bitcast_fusion
  103.1 1.3 select_select_fusion
  104.4 19.7 %reduce-scatter.2.cloned.1.call-done = bf16[64,3584]{1,0:T(8,128)(2,1)} async-done(((bf16[512,3584]{1,0:T(8,128)(2,1)}), bf16[64,3584]{1,0:T(8,128)(2,1)}) %reduce-scatter.2.cloned.1.call-update) | async-done | bytes 458768 | tf_op jit(solution)/shard_map/reduce_scatter | solution.py:261
  (49 shorter events, 11.1 us)
Async XLA Ops:
  7.2 20.6 %copy-start.6 = (s32[1,4]{1,0:T(1,128)S(1)}, s32[1,4]{1,0:T(1,128)}, u32[]{:S(2)}) copy-start(s32[1,4]{1,0:T(1,128)} %param.20) | copy-start | bytes 52
  7.2 20.8 %copy-start.1 = (bf16[512,896]{1,0:T(8,128)(2,1)S(1)}, bf16[512,896]{1,0:T(8,128)(2,1)}, u32[]{:S(2)}) copy-start(bf16[512,896]{1,0:T(8,128)(2,1)} %param.15) | copy-start | bytes 2752516
  7.2 22.1 %copy-start = (bf16[512,896]{1,0:T(8,128)(2,1)S(1)}, bf16[512,896]{1,0:T(8,128)(2,1)}, u32[]{:S(2)}) copy-start(bf16[512,896]{1,0:T(8,128)(2,1)} %param.16) | copy-start | bytes 2752516
  7.2 117.0 %reduce-scatter.2.cloned.1.call-start = ((), (), s32[]{:S(2)}) async-start(), calls=%async_computation.1 | async-start | bytes 4128768 | tf_op jit(solution)/shard_map/reduce_scatter | solution.py:261
  18.5 13.5 %collective-permute-start = (bf16[200,896]{1,0:T(8,128)(2,1)S(1)}, bf16[200,896]{1,0:T(8,128)(2,1)}, u32[]{:S(2)}, u32[]{:S(2)}) collective-permute-start(bf16[200,896]{1,0:T(8,128)(2,1)S(1)} %pad_maximum_fusion.2), channel_id=1, source_target_pairs={{0,8},{8,16},{16,24},{24,32},{32,40},{40,48},{48,56},{56,64},{64,7... | collective-permute-start | bytes 1075208 | tf_op jit(solution)/shard_map/ppermute | solution.py:23
  24.9 10.1 %collective-permute-start.1 = (bf16[200,896]{1,0:T(8,128)(2,1)}, bf16[200,896]{1,0:T(8,128)(2,1)}, u32[]{:S(2)}, u32[]{:S(2)}) collective-permute-start(bf16[200,896]{1,0:T(8,128)(2,1)} %pad_maximum_fusion.3), channel_id=1, source_target_pairs={{0,248},{8,0},{16,8},{24,16},{32,24},{40,32},{48,40},{56,48},{64,5... | collective-permute-start | bytes 1075208 | tf_op jit(solution)/shard_map/ppermute | solution.py:23
  32.1 17.0 %copy-start.2 = (bf16[512,896]{0,1:T(8,128)(2,1)S(1)}, bf16[512,896]{0,1:T(8,128)(2,1)}, u32[]{:S(2)}) copy-start(bf16[512,896]{0,1:T(8,128)(2,1)} %copy.51) | copy-start | bytes 2752516
  32.1 17.0 %copy-start.3 = (bf16[512,896]{0,1:T(8,128)(2,1)S(1)}, bf16[512,896]{0,1:T(8,128)(2,1)}, u32[]{:S(2)}) copy-start(bf16[512,896]{0,1:T(8,128)(2,1)} %copy.52) | copy-start | bytes 2752516
  43.7 12.8 %collective-permute-start.2 = (bf16[192,1024]{1,0:T(8,128)(2,1)}, bf16[192,1024]{1,0:T(8,128)(2,1)}, u32[]{:S(2)}, u32[]{:S(2)}) collective-permute-start(bf16[192,1024]{1,0:T(8,128)(2,1)} %get-tuple-element.39), channel_id=1, source_target_pairs={{0,248},{8,0},{16,8},{24,16},{32,24},{40,32},{48,40},{56,48},{64,5... | collective-permute-start | bytes 1179656 | tf_op jit(solution)/shard_map/ppermute | solution.py:23
  48.7 14.0 %collective-permute-start.3 = (bf16[192,1024]{1,0:T(8,128)(2,1)}, bf16[192,1024]{1,0:T(8,128)(2,1)S(1)}, u32[]{:S(2)}, u32[]{:S(2)}) collective-permute-start(bf16[192,1024]{1,0:T(8,128)(2,1)} %get-tuple-element.40), channel_id=1, source_target_pairs={{0,8},{8,16},{16,24},{24,32},{32,40},{40,48},{48,56},{56,64},{64,7... | collective-permute-start | bytes 1179656 | tf_op jit(solution)/shard_map/ppermute | solution.py:23
  62.7 0.7 copy-start.5
  75.0 8.4 %copy-start.4 = (bf16[2,192,896]{2,1,0:T(8,128)(2,1)S(1)}, bf16[2,192,896]{2,1,0:T(8,128)(2,1)}, u32[]{:S(2)}) copy-start(bf16[2,192,896]{2,1,0:T(8,128)(2,1)} %get-tuple-element.43) | copy-start | bytes 2064388
  83.4 18.5 %collective-permute-start.4 = (bf16[2,192,896]{2,1,0:T(8,128)(2,1)S(1)}, bf16[2,192,896]{2,1,0:T(8,128)(2,1)S(1)}, u32[]{:S(2)}, u32[]{:S(2)}) collective-permute-start(bf16[2,192,896]{2,1,0:T(8,128)(2,1)S(1)} %copy-done.4), channel_id=1, source_target_pairs={{0,8},{8,16},{16,24},{24,32},{32,40},{40,48},{48,56},{56,64},{64,7... | collective-permute-start | bytes 2064392 | tf_op jit(solution)/shard_map/ppermute | solution.py:23
  83.5 18.5 %collective-permute-start.5 = (bf16[2,192,896]{2,1,0:T(8,128)(2,1)S(1)}, bf16[2,192,896]{2,1,0:T(8,128)(2,1)}, u32[]{:S(2)}, u32[]{:S(2)}) collective-permute-start(bf16[2,192,896]{2,1,0:T(8,128)(2,1)S(1)} %get-tuple-element.44), channel_id=1, source_target_pairs={{0,248},{8,0},{16,8},{24,16},{32,24},{40,32},{48,40},{56,48},{64,5... | collective-permute-start | bytes 2064392 | tf_op jit(solution)/shard_map/ppermute | solution.py:23
Sparse Core Ops, SparseCore 0:
  83.5 40.6 reduce-scatter.1

commit v9 on v8

--- a/solution.py
+++ b/solution.py
@@ -215,37 +215,28 @@
     from_left_kv = shifted(right_kv, "req", 1)
     from_right_kv = shifted(left_kv, "req", -1)
 
-    def split_result(result):
-        scaled = result[:, :feat_width]
-        parts = result[:, feat_width : feat_width + 3 * head_count].astype(jnp.float32)
-        log_total = (
-            parts[:, :head_count]
-            + parts[:, head_count : 2 * head_count]
-            + parts[:, 2 * head_count : 3 * head_count]
-        )
-        return scaled, log_total
-
-    got_right = split_result(got_right)
-    got_left = split_result(got_left)
+    (own_numer, own_top, own_total), got_right, got_left = lax.optimization_barrier(
+        ((own_numer, own_top, own_total), got_right, got_left)
+    )
 
     def place(result, start, length):
-        scaled, log_total = result
         shift = tok_count - start
         keep = ((positions - start >= 0) & (positions - start < length))[:, None]
-
-        def moved(x):
-            padded = jnp.pad(x, ((tok_count, tok_count - NEWCAP), (0, 0)))
-            return lax.dynamic_slice_in_dim(padded, shift, tok_count, 0)
-
-        return keep, moved(scaled), moved(log_total)
-
-    keep_r, scaled_r, log_r = place(got_right, right_start, right_len)
-    keep_l, scaled_l, log_l = place(got_left, left_start, left_len)
-    prior_scaled = jnp.where(
-        keep_r, scaled_r, jnp.where(keep_l, scaled_l, jnp.zeros((), jnp.bfloat16))
-    ).astype(jnp.float32)
-    prior_top = jnp.where(keep_r, log_r, jnp.where(keep_l, log_l, floor_value))
-    prior_total = jnp.where(keep_r | keep_l, 1.0, 0.0)
+        padded = jnp.pad(result, ((tok_count, tok_count - NEWCAP), (0, 0)))
+        moved = lax.dynamic_slice_in_dim(padded, shift, tok_count, 0)
+        return keep, moved
+
+    keep_r, moved_r = place(got_right, right_start, right_len)
+    keep_l, moved_l = place(got_left, left_start, left_len)
+    prior = jnp.where(keep_r, moved_r, jnp.where(keep_l, moved_l, jnp.zeros((), moved_r.dtype)))
+    prior_scaled = prior[:, :feat_width].astype(jnp.float32)
+    parts = prior[:, feat_width : feat_width + 3 * head_count].astype(jnp.float32)
+    log_total = (
+        parts[:, :head_count] + parts[:, head_count : 2 * head_count] + parts[:, 2 * head_count :]
+    )
+    has_prior = keep_r | keep_l
+    prior_top = jnp.where(has_prior, log_total, floor_value)
+    prior_total = jnp.where(has_prior, 1.0, 0.0)
 
     both_top = jnp.maximum(own_top, prior_top)
     own_scale = jnp.exp(own_top - both_top)

time: 132 us -> 132 us (level)
  matrix products: 15.8 us -> 17.7 us
  waiting for transfers between devices: 39.5 us -> 37.7 us
    mul x0 -> x4, local copies, waits for them, and re-layouts: none -> 3.92 us  [the longest x2 2.01 us: body(): prior_scaled.reshape(tok_count, head_count, HD) * prior_scale[:, :, None]]
    ppermute x6, waiting for transfers between devices: 19.7 us -> 16.8 us  [shifted(): return lax.ppermute(value, axis, pairs)]
    dot_general x1, matrix products: 8.36 us -> 10.9 us  [body(): jnp.dot(attended, out_proj, preferred_element_type=jnp.float32)]
    slice x2 -> x0, local copies, waits for them, and re-layouts: 2.01 us -> none  [split_result(): scaled = result[:, :feat_width]]
    div x0 -> x2, local copies, waits for them, and re-layouts: none -> 1.94 us  [body(): numerator / denominator[:, :, None]]
    select_n x1 -> x2, other arithmetic: 0.01 us -> 1.9 us  [the longest x1 1.89 us: body(): jnp.where(keep_r, moved_r, jnp.where(keep_l, moved_l, jnp.zeros((), moved...]
    reshape x1 -> x0, local copies, waits for them, and re-layouts: 1.79 us -> none  [body(): prior_scaled.reshape(tok_count, head_count, HD) * prior_scale[:, :, None]]
    optimization_barrier x0 -> x1, local copies, waits for them, and re-layouts: none -> 1.72 us  [body(): lax.optimization_barrier(((own_numer, own_top, own_total), got_right, got...]
  transfers between devices with their start and end apart: 7 -> 7, of which waited for: 5 -> 4; matrix products, arithmetic and copies ran while one was open for 15% -> 16% of each run, Pallas kernels for 0% -> 0%
where the time goes in v9:
time: 132 us
  waiting for transfers between devices  37.7 us (29%)
  between operations  25.1 us (19%)
  local copies, waits for them, and re-layouts  20.1 us (15%)
  matrix products  17.7 us (13%)
  starting transfers between devices  12.6 us (10%)
  other arithmetic  9.97 us (8%)
  Pallas kernels  8.75 us (7%)
    reduce_scatter x1, waiting for transfers between devices, body(): lax.psum_scatter(jnp.dot(attended, out_proj, preferred_element_type=jnp.f...  20.8 us
    ppermute x6, waiting for transfers between devices, shifted(): return lax.ppermute(value, axis, pairs)  16.8 us
    ppermute x6, starting transfers between devices, shifted(): return lax.ppermute(value, axis, pairs)  12.6 us
    dot_general x1, matrix products, body(): jnp.dot(attended, out_proj, preferred_element_type=jnp.float32)  10.9 us
    pallas_call x1, Pallas kernels, serve_slots(): pl.pallas_call(functools.partial(prior_kernel, head_count), out_shape=(ja...  8.75 us
    unnamed x15, local copies, waits for them, and re-layouts  4.09 us
    dot_general x1, matrix products, attend_part(): jnp.einsum('hts,shd->thd', weights.astype(jnp.bfloat16), value_heads, pre...  3.93 us
    reduce_sum x1, other arithmetic, attend_part(): row_total = jnp.sum(weights, axis=2)  3.23 us
  transfers between devices with their start and end apart: 7, of which 4 were waited for; matrix products, arithmetic and copies ran while one was open for 16% of the time, Pallas kernels for 0%

profile of v9, /device:TPU:8, one launch (start us, length us, event | category | flops | bytes accessed | tf_op | source)
XLA Modules:
  0.0 131.9 jit_solution(15275125109958506746)
XLA Ops:
  7.3 1.4 %fusion.54 = (s32[1,1]{1,0:T(1,128)}, s32[1,1]{1,0:T(1,128)}) fusion(s32[1,2]{1,0:T(1,128)} %param.23), kind=kLoop, calls=%fused_computation.89 | loop fusion | bytes 16 | tf_op jit(solution)/shard_map/slice | solution.py:175
  10.6 1.3 fusion.55
  13.2 1.3 %fusion.53 = (s32[1,1]{1,0:T(1,128)}, s32[1,1]{1,0:T(1,128)}) fusion(s32[1,2]{1,0:T(1,128)} %param.22), kind=kLoop, calls=%fused_computation.88 | loop fusion | bytes 16 | tf_op jit(solution)/shard_map/slice | solution.py:174
  18.5 1.7 %collective-permute-start = (bf16[200,896]{1,0:T(8,128)(2,1)S(1)}, bf16[200,896]{1,0:T(8,128)(2,1)}, u32[]{:S(2)}, u32[]{:S(2)}) collective-permute-start(bf16[200,896]{1,0:T(8,128)(2,1)S(1)} %pad_maximum_fusion.2), channel_id=1, source_target_pairs={{0,8},{8,16},{16,24},{24,32},{32,40},{40,48},{48,56},{56,64},{64,7... | collective-permute-start | bytes 1075208 | tf_op jit(solution)/shard_map/ppermute | solution.py:23
  25.4 1.5 %copy.44 = bf16[512,896]{0,1:T(8,128)(2,1)S(1)} copy(bf16[512,896]{1,0:T(8,128)(2,1)} %param.14) | data formatting | bytes 1835008 | tf_op args[0]
  27.1 1.3 copy.45
  28.4 1.3 copy.46
  31.4 3.5 %collective-permute-done.1.right_ref = bf16[200,896]{1,0:T(8,128)(2,1)} collective-permute-done((bf16[200,896]{1,0:T(8,128)(2,1)}, bf16[200,896]{1,0:T(8,128)(2,1)}, u32[]{:S(2)}, u32[]{:S(2)}) %collective-permute-start.1) | collective-permute-done | bytes 358432 | tf_op jit(solution)/shard_map/ppermute | solution.py:23
  34.9 8.8 %shard_map.121 = (bf16[192,1024]{1,0:T(8,128)(2,1)}, bf16[192,1024]{1,0:T(8,128)(2,1)}) custom-call(bf16[200,896]{1,0:T(8,128)(2,1)} %collective-permute-done.left_ref, bf16[200,896]{1,0:T(8,128)(2,1)} %collective-permute-done.1.right_ref, bf16[2,1024,896]{2,1,0:T(8,128)(2,1)} %key_ref.1, bf16[2,1024,896]{2,1,0:T(8,128)(2,1)} %value_ref.1), custom_call_target="tpu_custom_call" | custom-call | flops 2013265920 | bytes 8843264 | tf_op jit(solution)/shard_map/pallas_call | solution.py:118
  43.9 5.1 %collective-permute-start.2 = (bf16[192,1024]{1,0:T(8,128)(2,1)}, bf16[192,1024]{1,0:T(8,128)(2,1)}, u32[]{:S(2)}, u32[]{:S(2)}) collective-permute-start(bf16[192,1024]{1,0:T(8,128)(2,1)} %get-tuple-element.44), channel_id=1, source_target_pairs={{0,248},{8,0},{16,8},{24,16},{32,24},{40,32},{48,40},{56,48},{64,5... | collective-permute-start | bytes 1179656 | tf_op jit(solution)/shard_map/ppermute | solution.py:23
  49.0 2.9 %fusion = (f32[4,512]{1,0:T(4,128)S(1)}, f32[4,512,512]{1,2,0:T(8,128)}) fusion(pred[512,512]{0,1:T(8,128)(4,1)S(1)} %fusion.12, bf16[512,4,224]{0,2,1:T(8,128)(2,1)S(1)} %bitcast.60, bf16[512,4,224]{0,2,1:T(8,128)(2,1)S(1)} %bitcast.61), kind=kOutput, calls=%fused_computation.3 | convolution fusion | flops 472905728 | bytes 6299648 | tf_op jit(solution)/shard_map/thd,shd->hts/dot_general | solution.py:32
  52.0 3.2 %fusion.1 = f32[4,512]{1,0:T(4,128)S(1)} fusion(f32[4,512,512]{1,2,0:T(8,128)} %get-tuple-element.83, f32[4,512]{1,0:T(4,128)S(1)} %get-tuple-element.82, pred[512,512]{0,1:T(8,128)(4,1)S(1)} %fusion.12), kind=kLoop, calls=%fused_computation.4 | loop fusion | flops 5240832 | bytes 4472832 | tf_op jit(solution)/shard_map/reduce_sum | solution.py:38
  55.4 3.9 %fusion.3 = f32[4,512,224]{1,2,0:T(8,128)S(1)} fusion(bf16[512,4,224]{0,2,1:T(8,128)(2,1)} %bitcast.59, f32[4,512,512]{1,2,0:T(8,128)} %get-tuple-element.83, f32[4,512]{1,0:T(4,128)S(1)} %get-tuple-element.82, pred[512,512]{0,1:T(8,128)(4,1)S(1)} %fusion.12), kind=kOutput, calls=%fused_computation.6 | convolution fusion | flops 475004928 | bytes 7217152 | tf_op jit(solution)/shard_map/hts,shd->thd/dot_general | solution.py:39
  59.4 3.7 %collective-permute-done.3 = bf16[192,1024]{1,0:T(8,128)(2,1)} collective-permute-done((bf16[192,1024]{1,0:T(8,128)(2,1)}, bf16[192,1024]{1,0:T(8,128)(2,1)}, u32[]{:S(2)}, u32[]{:S(2)}) %collective-permute-start.3) | collective-permute-done | bytes 393248 | tf_op jit(solution)/shard_map/ppermute | solution.py:23
  63.1 1.7 %copy.51 = f32[512,896]{1,0:T(8,128)} copy(f32[512,896]{0,1:T(8,128)S(1)} %bitcast.56) | data formatting | bytes 3670016 | tf_op jit(solution)/shard_map/optimization_barrier | solution.py:218
  64.8 1.9 %fusion.10 = bf16[512,1024]{1,0:T(8,128)(2,1)S(1)} fusion(s32[]{:T(128)S(6)} %select_n.139, bf16[192,1024]{1,0:T(8,128)(2,1)} %collective-permute-done.2, s32[]{:T(128)S(6)} %select_n.140, bf16[192,1024]{1,0:T(8,128)(2,1)} %collective-permute-done.3, pred[512]{0:T(512)(128)(4,1)S(1)} %get-tuple-element.61, pred[512]{0:T(512)(128)(4,1)S(1)} %get-tuple-element.60), kind=kLoop, calls=%fused_computation.15 | loop fusion | flops 1048576 | bytes 1836040 | tf_op jit(solution)/shard_map/jit(_where)/select_n | solution.py:231
  67.7 1.8 %copy.54 = f32[512,896]{1,0:T(8,128)} copy(f32[512,896]{0,1:T(8,128)S(1)} %bitcast.53) | data formatting | bytes 3670016 | tf_op jit(solution)/shard_map/mul | solution.py:247
  69.7 1.7 %copy.52 = f32[512,896]{1,0:T(8,128)} copy(f32[512,896]{0,1:T(8,128)S(1)} %bitcast.54) | data formatting | bytes 3670016 | tf_op jit(solution)/shard_map/mul | solution.py:246
  71.6 1.7 %copy.56 = f32[512,896]{1,0:T(8,128)} copy(f32[512,896]{0,1:T(8,128)S(1)} %bitcast.55) | data formatting | bytes 3670016 | tf_op jit(solution)/shard_map/div | solution.py:250
  73.3 10.9 %convolution_convert_fusion = bf16[512,3584]{1,0:T(8,128)(2,1)} fusion(bf16[896,3584]{1,0:T(8,128)(2,1)} %param.19, f32[512,896]{1,0:T(8,128)} %copy.56, f32[512,896]{1,0:T(8,128)} %copy.54, f32[512,896]{1,0:T(8,128)} %copy.51, f32[512,896]{1,0:T(8,128)} %copy.52, bf16[512,1024]{1,0:T(8,128)(2,1)S(1)} %fusion.10), kind=kOutput, calls=%fused_computation | convolution fusion | flops 3292921856 | bytes 18350080 | tf_op jit(solution)/shard_map/dot_general | solution.py:253
  84.3 5.1 %collective-permute-start.5 = (bf16[2,192,896]{2,1,0:T(8,128)(2,1)S(1)}, bf16[2,192,896]{2,1,0:T(8,128)(2,1)S(1)}, u32[]{:S(2)}, u32[]{:S(2)}) collective-permute-start(bf16[2,192,896]{2,1,0:T(8,128)(2,1)S(1)} %copy-done.3), channel_id=1, source_target_pairs={{0,248},{8,0},{16,8},{24,16},{32,24},{40,32},{48,40},{56,48},{64,5... | collective-permute-start | bytes 2064392 | tf_op jit(solution)/shard_map/ppermute | solution.py:23
  93.1 9.6 %collective-permute-done.4 = bf16[2,192,896]{2,1,0:T(8,128)(2,1)S(1)} collective-permute-done((bf16[2,192,896]{2,1,0:T(8,128)(2,1)S(1)}, bf16[2,192,896]{2,1,0:T(8,128)(2,1)S(1)}, u32[]{:S(2)}, u32[]{:S(2)}) %collective-permute-start.4) | collective-permute-done | bytes 688160 | tf_op jit(solution)/shard_map/ppermute | solution.py:23
  102.9 1.3 select_select_fusion
  104.2 20.8 %reduce-scatter.2.cloned.1.call-done = bf16[64,3584]{1,0:T(8,128)(2,1)} async-done(((bf16[512,3584]{1,0:T(8,128)(2,1)}), bf16[64,3584]{1,0:T(8,128)(2,1)}) %reduce-scatter.2.cloned.1.call-update) | async-done | bytes 458768 | tf_op jit(solution)/shard_map/reduce_scatter | solution.py:252
  (48 shorter events, 9.3 us)
Async XLA Ops:
  7.2 19.7 %copy-start.5 = (s32[1,4]{1,0:T(1,128)S(1)}, s32[1,4]{1,0:T(1,128)}, u32[]{:S(2)}) copy-start(s32[1,4]{1,0:T(1,128)} %param.20) | copy-start | bytes 52
  7.2 19.9 %copy-start = (bf16[512,896]{1,0:T(8,128)(2,1)S(1)}, bf16[512,896]{1,0:T(8,128)(2,1)}, u32[]{:S(2)}) copy-start(bf16[512,896]{1,0:T(8,128)(2,1)} %param.15) | copy-start | bytes 2752516
  7.2 21.2 %copy-start.1 = (bf16[512,896]{1,0:T(8,128)(2,1)S(1)}, bf16[512,896]{1,0:T(8,128)(2,1)}, u32[]{:S(2)}) copy-start(bf16[512,896]{1,0:T(8,128)(2,1)} %param.16) | copy-start | bytes 2752516
  7.2 117.8 %reduce-scatter.2.cloned.1.call-start = ((), (), s32[]{:S(2)}) async-start(), calls=%async_computation.1 | async-start | bytes 4128768 | tf_op jit(solution)/shard_map/reduce_scatter | solution.py:252
  18.5 12.9 %collective-permute-start = (bf16[200,896]{1,0:T(8,128)(2,1)S(1)}, bf16[200,896]{1,0:T(8,128)(2,1)}, u32[]{:S(2)}, u32[]{:S(2)}) collective-permute-start(bf16[200,896]{1,0:T(8,128)(2,1)S(1)} %pad_maximum_fusion.2), channel_id=1, source_target_pairs={{0,8},{8,16},{16,24},{24,32},{32,40},{40,48},{48,56},{56,64},{64,7... | collective-permute-start | bytes 1075208 | tf_op jit(solution)/shard_map/ppermute | solution.py:23
  24.7 10.1 %collective-permute-start.1 = (bf16[200,896]{1,0:T(8,128)(2,1)}, bf16[200,896]{1,0:T(8,128)(2,1)}, u32[]{:S(2)}, u32[]{:S(2)}) collective-permute-start(bf16[200,896]{1,0:T(8,128)(2,1)} %pad_maximum_fusion.3), channel_id=1, source_target_pairs={{0,248},{8,0},{16,8},{24,16},{32,24},{40,32},{48,40},{56,48},{64,5... | collective-permute-start | bytes 1075208 | tf_op jit(solution)/shard_map/ppermute | solution.py:23
  31.4 17.6 %copy-start.2 = (bf16[512,896]{0,1:T(8,128)(2,1)S(1)}, bf16[512,896]{0,1:T(8,128)(2,1)}, u32[]{:S(2)}) copy-start(bf16[512,896]{0,1:T(8,128)(2,1)} %copy.45) | copy-start | bytes 2752516
  43.9 15.4 %collective-permute-start.2 = (bf16[192,1024]{1,0:T(8,128)(2,1)}, bf16[192,1024]{1,0:T(8,128)(2,1)}, u32[]{:S(2)}, u32[]{:S(2)}) collective-permute-start(bf16[192,1024]{1,0:T(8,128)(2,1)} %get-tuple-element.44), channel_id=1, source_target_pairs={{0,248},{8,0},{16,8},{24,16},{32,24},{40,32},{48,40},{56,48},{64,5... | collective-permute-start | bytes 1179656 | tf_op jit(solution)/shard_map/ppermute | solution.py:23
  49.0 14.1 %collective-permute-start.3 = (bf16[192,1024]{1,0:T(8,128)(2,1)}, bf16[192,1024]{1,0:T(8,128)(2,1)}, u32[]{:S(2)}, u32[]{:S(2)}) collective-permute-start(bf16[192,1024]{1,0:T(8,128)(2,1)} %get-tuple-element.45), channel_id=1, source_target_pairs={{0,8},{8,16},{16,24},{24,32},{32,40},{40,48},{48,56},{56,64},{64,7... | collective-permute-start | bytes 1179656 | tf_op jit(solution)/shard_map/ppermute | solution.py:23
  73.3 10.9 %copy-start.4 = (bf16[2,192,896]{2,1,0:T(8,128)(2,1)S(1)}, bf16[2,192,896]{2,1,0:T(8,128)(2,1)}, u32[]{:S(2)}) copy-start(bf16[2,192,896]{2,1,0:T(8,128)(2,1)} %get-tuple-element.53) | copy-start | bytes 2064388
  73.3 11.0 %copy-start.3 = (bf16[2,192,896]{2,1,0:T(8,128)(2,1)S(1)}, bf16[2,192,896]{2,1,0:T(8,128)(2,1)}, u32[]{:S(2)}) copy-start(bf16[2,192,896]{2,1,0:T(8,128)(2,1)} %get-tuple-element.54) | copy-start | bytes 2064388
  84.2 18.5 %collective-permute-start.4 = (bf16[2,192,896]{2,1,0:T(8,128)(2,1)S(1)}, bf16[2,192,896]{2,1,0:T(8,128)(2,1)S(1)}, u32[]{:S(2)}, u32[]{:S(2)}) collective-permute-start(bf16[2,192,896]{2,1,0:T(8,128)(2,1)S(1)} %copy-done.4), channel_id=1, source_target_pairs={{0,8},{8,16},{16,24},{24,32},{32,40},{40,48},{48,56},{56,64},{64,7... | collective-permute-start | bytes 2064392 | tf_op jit(solution)/shard_map/ppermute | solution.py:23
  84.3 18.5 %collective-permute-start.5 = (bf16[2,192,896]{2,1,0:T(8,128)(2,1)S(1)}, bf16[2,192,896]{2,1,0:T(8,128)(2,1)S(1)}, u32[]{:S(2)}, u32[]{:S(2)}) collective-permute-start(bf16[2,192,896]{2,1,0:T(8,128)(2,1)S(1)} %copy-done.3), channel_id=1, source_target_pairs={{0,248},{8,0},{16,8},{24,16},{32,24},{40,32},{48,40},{56,48},{64,5... | collective-permute-start | bytes 2064392 | tf_op jit(solution)/shard_map/ppermute | solution.py:23
Sparse Core Ops, SparseCore 0:
  84.3 40.6 reduce-scatter.1

commit v10 on v8

--- a/solution.py
+++ b/solution.py
@@ -251,13 +251,16 @@
     own_scale = jnp.exp(own_top - both_top)
     prior_scale = jnp.exp(prior_top - both_top)
     denominator = own_total * own_scale + prior_total * prior_scale
-    numerator = (
-        own_numer.reshape(tok_count, head_count, HD) * own_scale[:, :, None]
-        + prior_scaled.reshape(tok_count, head_count, HD) * prior_scale[:, :, None]
-    )
-    attended = (
-        (numerator / denominator[:, :, None]).reshape(tok_count, feat_width).astype(jnp.bfloat16)
-    )
+    lane_head = jnp.arange(feat_width, dtype=jnp.int32)[None, :] // HD
+
+    def widened(per_head):
+        full = jnp.zeros((tok_count, feat_width), jnp.float32)
+        for h in range(head_count):
+            full = jnp.where(lane_head == h, per_head[:, h : h + 1], full)
+        return full
+
+    numerator = own_numer * widened(own_scale) + prior_scaled * widened(prior_scale)
+    attended = (numerator / widened(denominator)).astype(jnp.bfloat16)
     mixed = lax.psum_scatter(
         jnp.dot(attended, out_proj, preferred_element_type=jnp.float32).astype(jnp.bfloat16),
         "tp",

time: 132 us -> 128 us (0.970)
  starting transfers between devices: 12.5 us -> 9.4 us
  matrix products: 15.8 us -> 18.2 us
    ppermute x6, starting transfers between devices: 12.5 us -> 9.36 us  [shifted(): return lax.ppermute(value, axis, pairs)]
    dot_general x1, matrix products: 8.36 us -> 10.4 us  [body(): jnp.dot(attended, out_proj, preferred_element_type=jnp.float32)]
    slice x0 -> x3, local copies, waits for them, and re-layouts: none -> 1.73 us  [widened(): full = jnp.where(lane_head == h, per_head[:, h:h + 1], full)]
    unnamed x17 -> x21, local copies, waits for them, and re-layouts: 5.65 us -> 5.05 us
  transfers between devices with their start and end apart: 7 -> 7, of which waited for: 5 -> 3; matrix products, arithmetic and copies ran while one was open for 15% -> 19% of each run, Pallas kernels for 0% -> 0%
where the time goes in v10:
time: 128 us; the launch traced here: 127 us
  waiting for transfers between devices  38.7 us (30%)
  between operations  25.3 us (20%)
  matrix products  18.2 us (14%)
  local copies, waits for them, and re-layouts  17.7 us (14%)
  starting transfers between devices  9.4 us (7%)
  other arithmetic  9 us (7%)
  Pallas kernels  8.72 us (7%)
    reduce_scatter x1, waiting for transfers between devices, body(): lax.psum_scatter(jnp.dot(attended, out_proj, preferred_element_type=jnp.f...  19.4 us
    ppermute x6, waiting for transfers between devices, shifted(): return lax.ppermute(value, axis, pairs)  19.3 us
    dot_general x1, matrix products, body(): jnp.dot(attended, out_proj, preferred_element_type=jnp.float32)  10.4 us
    ppermute x6, starting transfers between devices, shifted(): return lax.ppermute(value, axis, pairs)  9.36 us
    pallas_call x1, Pallas kernels, serve_slots(): pl.pallas_call(functools.partial(prior_kernel, head_count), out_shape=(ja...  8.72 us
    unnamed x21, local copies, waits for them, and re-layouts  5.05 us
    dot_general x1, matrix products, attend_part(): jnp.einsum('hts,shd->thd', weights.astype(jnp.bfloat16), value_heads, pre...  4.91 us
    reduce_sum x1, other arithmetic, attend_part(): row_total = jnp.sum(weights, axis=2)  3.31 us
  transfers between devices with their start and end apart: 7, of which 3 were waited for; matrix products, arithmetic and copies ran while one was open for 19% of the time, Pallas kernels for 0%

profile of v10, /device:TPU:8, one launch (start us, length us, event | category | flops | bytes accessed | tf_op | source)
XLA Modules:
  0.0 127.0 jit_solution(10555873396193699319)
XLA Ops:
  7.2 1.3 %fusion.84 = (s32[1,1]{1,0:T(1,128)}, s32[1,1]{1,0:T(1,128)}) fusion(s32[1,4]{1,0:T(1,128)} %param.20), kind=kLoop, calls=%fused_computation.142 | loop fusion | bytes 16 | tf_op jit(solution)/shard_map/slice | solution.py:173
  10.5 1.3 %fusion.83 = (s32[1,1]{1,0:T(1,128)}, s32[1,1]{1,0:T(1,128)}) fusion(s32[1,2]{1,0:T(1,128)} %param.23), kind=kLoop, calls=%fused_computation.141 | loop fusion | bytes 16 | tf_op jit(solution)/shard_map/slice | solution.py:175
  14.5 1.3 %fusion.82 = (s32[1,1]{1,0:T(1,128)}, s32[1,1]{1,0:T(1,128)}) fusion(s32[1,2]{1,0:T(1,128)} %param.22), kind=kLoop, calls=%fused_computation.140 | loop fusion | bytes 16 | tf_op jit(solution)/shard_map/slice | solution.py:174
  17.1 1.3 %constant_dynamic-slice_fusion = (bf16[192,896]{1,0:T(8,128)(2,1)S(1)}, bf16[192,896]{1,0:T(8,128)(2,1)S(1)}) fusion(bf16[512,896]{1,0:T(8,128)(2,1)} %param.14, s32[]{:T(128)S(6)} %select_n.211, s32[]{:T(128)S(6)} %select_n.204), kind=kLoop, calls=%fused_computation.116 | loop fusion | bytes 1376264 | tf_op jit(solution)/shard_map/dynamic_slice | solution.py:179
  18.5 2.3 %collective-permute-start.1 = (bf16[200,896]{1,0:T(8,128)(2,1)S(1)}, bf16[200,896]{1,0:T(8,128)(2,1)}, u32[]{:S(2)}, u32[]{:S(2)}) collective-permute-start(bf16[200,896]{1,0:T(8,128)(2,1)S(1)} %pad_maximum_fusion.3), channel_id=1, source_target_pairs={{0,248},{8,0},{16,8},{24,16},{32,24},{40,32},{48,40},{56,48},{64,5... | collective-permute-start | bytes 1075208 | tf_op jit(solution)/shard_map/ppermute | solution.py:23
  25.5 1.3 %copy.32 = bf16[512,896]{0,1:T(8,128)(2,1)} copy(bf16[512,896]{1,0:T(8,128)(2,1)S(1)} %copy-done) | data formatting | bytes 1835008 | tf_op args[0]
  27.1 1.3 %copy.33 = bf16[512,896]{0,1:T(8,128)(2,1)} copy(bf16[512,896]{1,0:T(8,128)(2,1)S(1)} %copy-done.2) | data formatting | bytes 1835008 | tf_op args[1]
  28.4 1.3 %copy.34 = bf16[512,896]{0,1:T(8,128)(2,1)} copy(bf16[512,896]{1,0:T(8,128)(2,1)S(1)} %copy-done.1) | data formatting | bytes 1835008 | tf_op args[2]
  31.2 9.3 %collective-permute-done.left_ref = bf16[200,896]{1,0:T(8,128)(2,1)} collective-permute-done((bf16[200,896]{1,0:T(8,128)(2,1)}, bf16[200,896]{1,0:T(8,128)(2,1)}, u32[]{:S(2)}, u32[]{:S(2)}) %collective-permute-start) | collective-permute-done | bytes 358432 | tf_op jit(solution)/shard_map/ppermute | solution.py:23
  40.5 8.7 %shard_map.121 = (bf16[192,1024]{1,0:T(8,128)(2,1)}, bf16[192,1024]{1,0:T(8,128)(2,1)}) custom-call(bf16[200,896]{1,0:T(8,128)(2,1)} %collective-permute-done.left_ref, bf16[200,896]{1,0:T(8,128)(2,1)} %collective-permute-done.1.right_ref, bf16[2,1024,896]{2,1,0:T(8,128)(2,1)} %key_ref.1, bf16[2,1024,896]{2,1,0:T(8,128)(2,1)} %value_ref.1), custom_call_target="tpu_custom_call" | custom-call | flops 2013265920 | bytes 8843264 | tf_op jit(solution)/shard_map/pallas_call | solution.py:118
  49.2 5.1 %collective-permute-start.2 = (bf16[192,1024]{1,0:T(8,128)(2,1)}, bf16[192,1024]{1,0:T(8,128)(2,1)S(1)}, u32[]{:S(2)}, u32[]{:S(2)}) collective-permute-start(bf16[192,1024]{1,0:T(8,128)(2,1)} %get-tuple-element.39), channel_id=1, source_target_pairs={{0,248},{8,0},{16,8},{24,16},{32,24},{40,32},{48,40},{56,48},{64,5... | collective-permute-start | bytes 1179656 | tf_op jit(solution)/shard_map/ppermute | solution.py:23
  54.6 2.9 %fusion = (f32[4,512]{1,0:T(4,128)S(1)}, f32[4,512,512]{1,2,0:T(8,128)}) fusion(pred[512,512]{0,1:T(8,128)(4,1)S(1)} %fusion.10, bf16[512,4,224]{0,2,1:T(8,128)(2,1)S(1)} %bitcast.58, bf16[512,4,224]{0,2,1:T(8,128)(2,1)S(1)} %bitcast.60), kind=kOutput, calls=%fused_computation.3 | convolution fusion | flops 472905728 | bytes 6299648 | tf_op jit(solution)/shard_map/thd,shd->hts/dot_general | solution.py:32
  57.6 3.3 %fusion.1 = f32[4,512]{1,0:T(4,128)S(1)} fusion(f32[4,512,512]{1,2,0:T(8,128)} %get-tuple-element.84, f32[4,512]{1,0:T(4,128)S(1)} %get-tuple-element.83, pred[512,512]{0,1:T(8,128)(4,1)S(1)} %fusion.10), kind=kLoop, calls=%fused_computation.4 | loop fusion | flops 5240832 | bytes 4472832 | tf_op jit(solution)/shard_map/reduce_sum | solution.py:38
  61.1 4.9 %fusion.3 = f32[4,512,224]{1,2,0:T(8,128)} fusion(bf16[512,4,224]{0,2,1:T(8,128)(2,1)S(1)} %bitcast.59, f32[4,512,512]{1,2,0:T(8,128)} %get-tuple-element.84, f32[4,512]{1,0:T(4,128)S(1)} %get-tuple-element.83, pred[512,512]{0,1:T(8,128)(4,1)S(1)} %fusion.10), kind=kOutput, calls=%fused_computation.6 | convolution fusion | flops 475004928 | bytes 7217152 | tf_op jit(solution)/shard_map/hts,shd->thd/dot_general | solution.py:39
  66.0 1.8 %copy.37 = f32[512,896]{1,0:T(8,128)S(1)} copy(f32[512,896]{0,1:T(8,128)} %bitcast.57) | data formatting | bytes 3670016 | tf_op jit(solution)/shard_map/reshape | solution.py:45
  68.8 1.0 slice.167
  72.1 10.4 %convolution_convert_fusion = bf16[512,3584]{1,0:T(8,128)(2,1)} fusion(bf16[896,3584]{1,0:T(8,128)(2,1)} %param.19, f32[512,896]{1,0:T(8,128)S(1)} %copy.37, s32[]{:T(128)S(6)} %select_n.224, bf16[192,896]{1,0:T(8,128)(2,1)S(1)} %slice-done, s32[]{:T(128)S(6)} %select_n.225, bf16[192,896]{1,0:T(8,128)(2,1)S(1)} %slice.167, f32[512]{0:T(512)S(1)} %get-tuple-element.54, ...), kind=kOutput, calls=%fused_computation | convolution fusion | flops 3299344384 | bytes 12644872 | tf_op jit(solution)/shard_map/dot_general | solution.py:265
  82.5 1.1 copy-done.6
  83.6 2.0 %collective-permute-start.5 = (bf16[2,192,896]{2,1,0:T(8,128)(2,1)S(1)}, bf16[2,192,896]{2,1,0:T(8,128)(2,1)S(1)}, u32[]{:S(2)}, u32[]{:S(2)}) collective-permute-start(bf16[2,192,896]{2,1,0:T(8,128)(2,1)S(1)} %get-tuple-element.44), channel_id=1, source_target_pairs={{0,248},{8,0},{16,8},{24,16},{32,24},{40,32},{48,40},{56,48},{64,5... | collective-permute-start | bytes 2064392 | tf_op jit(solution)/shard_map/ppermute | solution.py:23
  85.6 1.2 slice.202
  87.5 1.2 slice.200
  89.3 10.0 %collective-permute-done.4 = bf16[2,192,896]{2,1,0:T(8,128)(2,1)S(1)} collective-permute-done((bf16[2,192,896]{2,1,0:T(8,128)(2,1)S(1)}, bf16[2,192,896]{2,1,0:T(8,128)(2,1)S(1)}, u32[]{:S(2)}, u32[]{:S(2)}) %collective-permute-start.4) | collective-permute-done | bytes 688160 | tf_op jit(solution)/shard_map/ppermute | solution.py:23
  99.5 1.3 %select_select_fusion = (bf16[2,192,896]{2,1,0:T(8,128)(2,1)}, bf16[2,192,896]{2,1,0:T(8,128)(2,1)}) fusion(pred[2]{0:T(512)(128)(4,1)S(1)} %get-tuple-element.91, pred[2]{0:T(512)(128)(4,1)S(1)} %get-tuple-element.92, bf16[192,896]{1,0:T(8,128)(2,1)S(1)} %get-tuple-element.71, bf16[192,896]{1,0:T(8,128)(2,1)S(1)} %get-tuple-element.69, ...), kind=kLoop, calls=%fused_computation.40 | loop fusion | flops 1376256 | bytes 2752516 | tf_op jit(solution)/shard_map/jit(_where)/select_n | solution.py:278
  100.8 19.4 %reduce-scatter.2.cloned.1.call-done = bf16[64,3584]{1,0:T(8,128)(2,1)} async-done(((bf16[512,3584]{1,0:T(8,128)(2,1)}), bf16[64,3584]{1,0:T(8,128)(2,1)}) %reduce-scatter.2.cloned.1.call-update) | async-done | bytes 458768 | tf_op jit(solution)/shard_map/reduce_scatter | solution.py:264
  (55 shorter events, 6.6 us)
Async XLA Ops:
  7.2 18.4 %copy-start = (bf16[512,896]{1,0:T(8,128)(2,1)S(1)}, bf16[512,896]{1,0:T(8,128)(2,1)}, u32[]{:S(2)}) copy-start(bf16[512,896]{1,0:T(8,128)(2,1)} %param.14) | copy-start | bytes 2752516
  7.2 113.0 %reduce-scatter.2.cloned.1.call-start = ((), (), s32[]{:S(2)}) async-start(), calls=%async_computation.1 | async-start | bytes 4128768 | tf_op jit(solution)/shard_map/reduce_scatter | solution.py:264
  17.0 9.9 %copy-start.8 = (s32[1,4]{1,0:T(1,128)S(1)}, s32[1,4]{1,0:T(1,128)}, u32[]{:S(2)}) copy-start(s32[1,4]{1,0:T(1,128)} %param.20) | copy-start | bytes 52
  17.1 10.0 %copy-start.2 = (bf16[512,896]{1,0:T(8,128)(2,1)S(1)}, bf16[512,896]{1,0:T(8,128)(2,1)}, u32[]{:S(2)}) copy-start(bf16[512,896]{1,0:T(8,128)(2,1)} %param.15) | copy-start | bytes 2752516
  18.5 12.7 %collective-permute-start.1 = (bf16[200,896]{1,0:T(8,128)(2,1)S(1)}, bf16[200,896]{1,0:T(8,128)(2,1)}, u32[]{:S(2)}, u32[]{:S(2)}) collective-permute-start(bf16[200,896]{1,0:T(8,128)(2,1)S(1)} %pad_maximum_fusion.3), channel_id=1, source_target_pairs={{0,248},{8,0},{16,8},{24,16},{32,24},{40,32},{48,40},{56,48},{64,5... | collective-permute-start | bytes 1075208 | tf_op jit(solution)/shard_map/ppermute | solution.py:23
  24.7 3.7 %copy-start.1 = (bf16[512,896]{1,0:T(8,128)(2,1)S(1)}, bf16[512,896]{1,0:T(8,128)(2,1)}, u32[]{:S(2)}) copy-start(bf16[512,896]{1,0:T(8,128)(2,1)} %param.16) | copy-start | bytes 2752516
  25.5 15.0 %collective-permute-start = (bf16[200,896]{1,0:T(8,128)(2,1)}, bf16[200,896]{1,0:T(8,128)(2,1)}, u32[]{:S(2)}, u32[]{:S(2)}) collective-permute-start(bf16[200,896]{1,0:T(8,128)(2,1)} %pad_maximum_fusion.2), channel_id=1, source_target_pairs={{0,8},{8,16},{16,24},{24,32},{32,40},{40,48},{48,56},{56,64},{64,7... | collective-permute-start | bytes 1075208 | tf_op jit(solution)/shard_map/ppermute | solution.py:23
  31.2 23.4 %copy-start.3 = (bf16[512,896]{0,1:T(8,128)(2,1)S(1)}, bf16[512,896]{0,1:T(8,128)(2,1)}, u32[]{:S(2)}) copy-start(bf16[512,896]{0,1:T(8,128)(2,1)} %copy.32) | copy-start | bytes 2752516
  31.2 23.4 %copy-start.5 = (bf16[512,896]{0,1:T(8,128)(2,1)S(1)}, bf16[512,896]{0,1:T(8,128)(2,1)}, u32[]{:S(2)}) copy-start(bf16[512,896]{0,1:T(8,128)(2,1)} %copy.33) | copy-start | bytes 2752516
  49.2 18.6 %collective-permute-start.2 = (bf16[192,1024]{1,0:T(8,128)(2,1)}, bf16[192,1024]{1,0:T(8,128)(2,1)S(1)}, u32[]{:S(2)}, u32[]{:S(2)}) collective-permute-start(bf16[192,1024]{1,0:T(8,128)(2,1)} %get-tuple-element.39), channel_id=1, source_target_pairs={{0,248},{8,0},{16,8},{24,16},{32,24},{40,32},{48,40},{56,48},{64,5... | collective-permute-start | bytes 1179656 | tf_op jit(solution)/shard_map/ppermute | solution.py:23
  54.3 13.6 %collective-permute-start.3 = (bf16[192,1024]{1,0:T(8,128)(2,1)}, bf16[192,1024]{1,0:T(8,128)(2,1)}, u32[]{:S(2)}, u32[]{:S(2)}) collective-permute-start(bf16[192,1024]{1,0:T(8,128)(2,1)} %get-tuple-element.40), channel_id=1, source_target_pairs={{0,8},{8,16},{16,24},{24,32},{32,40},{40,48},{48,56},{56,64},{64,7... | collective-permute-start | bytes 1179656 | tf_op jit(solution)/shard_map/ppermute | solution.py:23
  57.6 3.5 %copy-start.4 = (bf16[512,896]{0,1:T(8,128)(2,1)S(1)}, bf16[512,896]{0,1:T(8,128)(2,1)}, u32[]{:S(2)}) copy-start(bf16[512,896]{0,1:T(8,128)(2,1)} %copy.34) | copy-start | bytes 2752516
  67.8 3.1 %copy-start.7 = (bf16[192,1024]{1,0:T(8,128)(2,1)}, bf16[192,1024]{1,0:T(8,128)(2,1)S(1)}, u32[]{:S(2)}) copy-start(bf16[192,1024]{1,0:T(8,128)(2,1)S(1)} %collective-permute-done.2) | copy-start | bytes 1179652
  70.9 1.2 slice-start
  82.5 1.1 copy-start.6
  83.6 15.7 %collective-permute-start.4 = (bf16[2,192,896]{2,1,0:T(8,128)(2,1)S(1)}, bf16[2,192,896]{2,1,0:T(8,128)(2,1)S(1)}, u32[]{:S(2)}, u32[]{:S(2)}) collective-permute-start(bf16[2,192,896]{2,1,0:T(8,128)(2,1)S(1)} %copy-done.6), channel_id=1, source_target_pairs={{0,8},{8,16},{16,24},{24,32},{32,40},{40,48},{48,56},{56,64},{64,7... | collective-permute-start | bytes 2064392 | tf_op jit(solution)/shard_map/ppermute | solution.py:23
  83.6 15.8 %collective-permute-start.5 = (bf16[2,192,896]{2,1,0:T(8,128)(2,1)S(1)}, bf16[2,192,896]{2,1,0:T(8,128)(2,1)S(1)}, u32[]{:S(2)}, u32[]{:S(2)}) collective-permute-start(bf16[2,192,896]{2,1,0:T(8,128)(2,1)S(1)} %get-tuple-element.44), channel_id=1, source_target_pairs={{0,248},{8,0},{16,8},{24,16},{32,24},{40,32},{48,40},{56,48},{64,5... | collective-permute-start | bytes 2064392 | tf_op jit(solution)/shard_map/ppermute | solution.py:23
Sparse Core Ops, SparseCore 0:
  82.7 37.4 reduce-scatter.1

commit v11 on v10

--- a/solution.py
+++ b/solution.py
@@ -186,8 +186,14 @@
     right_start, right_len, right_slot, right_prior = request_at(1)
     left_start, left_len, left_slot, left_prior = request_at(-1)
 
-    from_left = shifted(query_bundle(right_start, right_len, right_slot, right_prior), "req", 1)
-    from_right = shifted(query_bundle(left_start, left_len, left_slot, left_prior), "req", -1)
+    right_bundle, left_bundle = lax.optimization_barrier(
+        (
+            query_bundle(right_start, right_len, right_slot, right_prior),
+            query_bundle(left_start, left_len, left_slot, left_prior),
+        )
+    )
+    from_left = shifted(right_bundle, "req", 1)
+    from_right = shifted(left_bundle, "req", -1)
 
     served = serve_slots(from_left, from_right, cache_keys, cache_values, head_count)
     held_ends, served = lax.optimization_barrier((req_ends, served))

time: 128 us -> 129 us (level)
  starting transfers between devices: 9.4 us -> 13 us
  waiting for transfers between devices: 38.7 us -> 36.1 us
    ppermute x6, waiting for transfers between devices: 19.3 us -> 14.2 us  [shifted(): return lax.ppermute(value, axis, pairs)]
    ppermute x6, starting transfers between devices: 9.36 us -> 13 us  [shifted(): return lax.ppermute(value, axis, pairs)]
    reduce_scatter x1, waiting for transfers between devices: 19.4 us -> 21.9 us  [body(): lax.psum_scatter(jnp.dot(attended, out_proj, preferred_element_type=jnp.f...]
  transfers between devices with their start and end apart: 7 -> 7, of which waited for: 3 -> 4; matrix products, arithmetic and copies ran while one was open for 19% -> 18% of each run, Pallas kernels for 0% -> 0%
where the time goes in v11:
time: 129 us; the launch traced here: 128 us
  waiting for transfers between devices  36.1 us (28%)
  between operations  25.5 us (20%)
  matrix products  18.2 us (14%)
  local copies, waits for them, and re-layouts  17.7 us (14%)
  starting transfers between devices  13 us (10%)
  other arithmetic  9.01 us (7%)
  Pallas kernels  8.72 us (7%)
    reduce_scatter x1, waiting for transfers between devices, body(): lax.psum_scatter(jnp.dot(attended, out_proj, preferred_element_type=jnp.f...  21.9 us
    ppermute x6, waiting for transfers between devices, shifted(): return lax.ppermute(value, axis, pairs)  14.2 us
    ppermute x6, starting transfers between devices, shifted(): return lax.ppermute(value, axis, pairs)  13 us
    dot_general x1, matrix products, body(): jnp.dot(attended, out_proj, preferred_element_type=jnp.float32)  10.4 us
    pallas_call x1, Pallas kernels, serve_slots(): pl.pallas_call(functools.partial(prior_kernel, head_count), out_shape=(ja...  8.72 us
    unnamed x21, local copies, waits for them, and re-layouts  5.05 us
    dot_general x1, matrix products, attend_part(): jnp.einsum('hts,shd->thd', weights.astype(jnp.bfloat16), value_heads, pre...  4.91 us
    reduce_sum x1, other arithmetic, attend_part(): row_total = jnp.sum(weights, axis=2)  3.31 us
  transfers between devices with their start and end apart: 7, of which 4 were waited for; matrix products, arithmetic and copies ran while one was open for 18% of the time, Pallas kernels for 0%

profile of v11, /device:TPU:8, one launch (start us, length us, event | category | flops | bytes accessed | tf_op | source)
XLA Modules:
  0.0 128.2 jit_solution(13411879192912623015)
XLA Ops:
  7.2 1.3 %fusion.84 = (s32[1,1]{1,0:T(1,128)}, s32[1,1]{1,0:T(1,128)}) fusion(s32[1,4]{1,0:T(1,128)} %param.20), kind=kLoop, calls=%fused_computation.142 | loop fusion | bytes 16 | tf_op jit(solution)/shard_map/slice | solution.py:173
  13.1 1.3 %fusion.83 = (s32[1,1]{1,0:T(1,128)}, s32[1,1]{1,0:T(1,128)}) fusion(s32[1,2]{1,0:T(1,128)} %param.23), kind=kLoop, calls=%fused_computation.141 | loop fusion | bytes 16 | tf_op jit(solution)/shard_map/slice | solution.py:175
  17.0 1.3 %fusion.82 = (s32[1,1]{1,0:T(1,128)}, s32[1,1]{1,0:T(1,128)}) fusion(s32[1,2]{1,0:T(1,128)} %param.22), kind=kLoop, calls=%fused_computation.140 | loop fusion | bytes 16 | tf_op jit(solution)/shard_map/slice | solution.py:174
  21.1 1.3 %constant_dynamic-slice_fusion = (bf16[192,896]{1,0:T(8,128)(2,1)S(1)}, bf16[192,896]{1,0:T(8,128)(2,1)S(1)}) fusion(bf16[512,896]{1,0:T(8,128)(2,1)} %param.14, s32[]{:T(128)S(6)} %select_n.211, s32[]{:T(128)S(6)} %select_n.204), kind=kLoop, calls=%fused_computation.116 | loop fusion | bytes 1376264 | tf_op jit(solution)/shard_map/dynamic_slice | solution.py:179
  23.4 1.6 %collective-permute-start = (bf16[200,896]{1,0:T(8,128)(2,1)}, bf16[200,896]{1,0:T(8,128)(2,1)}, u32[]{:S(2)}, u32[]{:S(2)}) collective-permute-start(bf16[200,896]{1,0:T(8,128)(2,1)} %get-tuple-element.38), channel_id=1, source_target_pairs={{0,8},{8,16},{16,24},{24,32},{32,40},{40,48},{48,56},{56,64},{64,7... | collective-permute-start | bytes 1075208 | tf_op jit(solution)/shard_map/ppermute | solution.py:23
  25.6 1.3 %copy.32 = bf16[512,896]{0,1:T(8,128)(2,1)} copy(bf16[512,896]{1,0:T(8,128)(2,1)S(1)} %copy-done) | data formatting | bytes 1835008 | tf_op args[0]
  27.2 1.3 %copy.33 = bf16[512,896]{0,1:T(8,128)(2,1)} copy(bf16[512,896]{1,0:T(8,128)(2,1)S(1)} %copy-done.2) | data formatting | bytes 1835008 | tf_op args[1]
  28.5 1.3 %copy.34 = bf16[512,896]{0,1:T(8,128)(2,1)} copy(bf16[512,896]{1,0:T(8,128)(2,1)S(1)} %copy-done.1) | data formatting | bytes 1835008 | tf_op args[2]
  31.3 2.5 %collective-permute-done.left_ref = bf16[200,896]{1,0:T(8,128)(2,1)} collective-permute-done((bf16[200,896]{1,0:T(8,128)(2,1)}, bf16[200,896]{1,0:T(8,128)(2,1)}, u32[]{:S(2)}, u32[]{:S(2)}) %collective-permute-start) | collective-permute-done | bytes 358432 | tf_op jit(solution)/shard_map/ppermute | solution.py:23
  33.8 1.1 collective-permute-done.1.right_ref
  34.9 8.7 %shard_map.121 = (bf16[192,1024]{1,0:T(8,128)(2,1)}, bf16[192,1024]{1,0:T(8,128)(2,1)}) custom-call(bf16[200,896]{1,0:T(8,128)(2,1)} %collective-permute-done.left_ref, bf16[200,896]{1,0:T(8,128)(2,1)} %collective-permute-done.1.right_ref, bf16[2,1024,896]{2,1,0:T(8,128)(2,1)} %key_ref.1, bf16[2,1024,896]{2,1,0:T(8,128)(2,1)} %value_ref.1), custom_call_target="tpu_custom_call" | custom-call | flops 2013265920 | bytes 8843264 | tf_op jit(solution)/shard_map/pallas_call | solution.py:118
  43.6 5.9 %collective-permute-start.2 = (bf16[192,1024]{1,0:T(8,128)(2,1)}, bf16[192,1024]{1,0:T(8,128)(2,1)S(1)}, u32[]{:S(2)}, u32[]{:S(2)}) collective-permute-start(bf16[192,1024]{1,0:T(8,128)(2,1)} %get-tuple-element.43), channel_id=1, source_target_pairs={{0,248},{8,0},{16,8},{24,16},{32,24},{40,32},{48,40},{56,48},{64,5... | collective-permute-start | bytes 1179656 | tf_op jit(solution)/shard_map/ppermute | solution.py:23
  49.9 2.9 %fusion = (f32[4,512]{1,0:T(4,128)S(1)}, f32[4,512,512]{1,2,0:T(8,128)}) fusion(pred[512,512]{0,1:T(8,128)(4,1)S(1)} %fusion.10, bf16[512,4,224]{0,2,1:T(8,128)(2,1)S(1)} %bitcast.58, bf16[512,4,224]{0,2,1:T(8,128)(2,1)S(1)} %bitcast.60), kind=kOutput, calls=%fused_computation.3 | convolution fusion | flops 472905728 | bytes 6299648 | tf_op jit(solution)/shard_map/thd,shd->hts/dot_general | solution.py:32
  52.9 3.3 %fusion.1 = f32[4,512]{1,0:T(4,128)S(1)} fusion(f32[4,512,512]{1,2,0:T(8,128)} %get-tuple-element.88, f32[4,512]{1,0:T(4,128)S(1)} %get-tuple-element.87, pred[512,512]{0,1:T(8,128)(4,1)S(1)} %fusion.10), kind=kLoop, calls=%fused_computation.4 | loop fusion | flops 5240832 | bytes 4472832 | tf_op jit(solution)/shard_map/reduce_sum | solution.py:38
  56.4 4.9 %fusion.3 = f32[4,512,224]{1,2,0:T(8,128)} fusion(bf16[512,4,224]{0,2,1:T(8,128)(2,1)S(1)} %bitcast.59, f32[4,512,512]{1,2,0:T(8,128)} %get-tuple-element.88, f32[4,512]{1,0:T(4,128)S(1)} %get-tuple-element.87, pred[512,512]{0,1:T(8,128)(4,1)S(1)} %fusion.10), kind=kOutput, calls=%fused_computation.6 | convolution fusion | flops 475004928 | bytes 7217152 | tf_op jit(solution)/shard_map/hts,shd->thd/dot_general | solution.py:39
  61.3 1.8 %copy.37 = f32[512,896]{1,0:T(8,128)S(1)} copy(f32[512,896]{0,1:T(8,128)} %bitcast.57) | data formatting | bytes 3670016 | tf_op jit(solution)/shard_map/reshape | solution.py:45
  67.4 10.4 %convolution_convert_fusion = bf16[512,3584]{1,0:T(8,128)(2,1)} fusion(bf16[896,3584]{1,0:T(8,128)(2,1)} %param.19, f32[512,896]{1,0:T(8,128)S(1)} %copy.37, s32[]{:T(128)S(6)} %select_n.224, bf16[192,896]{1,0:T(8,128)(2,1)S(1)} %slice-done, s32[]{:T(128)S(6)} %select_n.225, bf16[192,896]{1,0:T(8,128)(2,1)S(1)} %slice.167, f32[512]{0:T(512)S(1)} %get-tuple-element.58, ...), kind=kOutput, calls=%fused_computation | convolution fusion | flops 3299344384 | bytes 12644872 | tf_op jit(solution)/shard_map/dot_general | solution.py:271
  77.8 1.1 copy-done.6
  78.9 4.8 %collective-permute-start.5 = (bf16[2,192,896]{2,1,0:T(8,128)(2,1)S(1)}, bf16[2,192,896]{2,1,0:T(8,128)(2,1)S(1)}, u32[]{:S(2)}, u32[]{:S(2)}) collective-permute-start(bf16[2,192,896]{2,1,0:T(8,128)(2,1)S(1)} %get-tuple-element.48), channel_id=1, source_target_pairs={{0,248},{8,0},{16,8},{24,16},{32,24},{40,32},{48,40},{56,48},{64,5... | collective-permute-start | bytes 2064392 | tf_op jit(solution)/shard_map/ppermute | solution.py:23
  83.8 1.2 slice.202
  85.6 1.2 slice.200
  87.5 10.6 %collective-permute-done.4 = bf16[2,192,896]{2,1,0:T(8,128)(2,1)S(1)} collective-permute-done((bf16[2,192,896]{2,1,0:T(8,128)(2,1)S(1)}, bf16[2,192,896]{2,1,0:T(8,128)(2,1)S(1)}, u32[]{:S(2)}, u32[]{:S(2)}) %collective-permute-start.4) | collective-permute-done | bytes 688160 | tf_op jit(solution)/shard_map/ppermute | solution.py:23
  98.2 1.3 %select_select_fusion = (bf16[2,192,896]{2,1,0:T(8,128)(2,1)}, bf16[2,192,896]{2,1,0:T(8,128)(2,1)}) fusion(pred[2]{0:T(512)(128)(4,1)S(1)} %iota_compare_fusion.6, pred[2]{0:T(512)(128)(4,1)S(1)} %iota_compare_fusion.7, bf16[192,896]{1,0:T(8,128)(2,1)S(1)} %get-tuple-element.75, bf16[192,896]{1,0:T(8,128)(2,1)S(1)} %get-tuple-element.73, ...), kind=kLoop, calls=%fused_computation.40 | loop fusion | flops 1376256 | bytes 2752516 | tf_op jit(solution)/shard_map/jit(_where)/select_n | solution.py:284
  99.5 21.9 %reduce-scatter.2.cloned.1.call-done = bf16[64,3584]{1,0:T(8,128)(2,1)} async-done(((bf16[512,3584]{1,0:T(8,128)(2,1)}), bf16[64,3584]{1,0:T(8,128)(2,1)}) %reduce-scatter.2.cloned.1.call-update) | async-done | bytes 458768 | tf_op jit(solution)/shard_map/reduce_scatter | solution.py:270
  (55 shorter events, 8.3 us)
Async XLA Ops:
  7.2 18.4 %copy-start = (bf16[512,896]{1,0:T(8,128)(2,1)S(1)}, bf16[512,896]{1,0:T(8,128)(2,1)}, u32[]{:S(2)}) copy-start(bf16[512,896]{1,0:T(8,128)(2,1)} %param.14) | copy-start | bytes 2752516
  7.2 114.2 %reduce-scatter.2.cloned.1.call-start = ((), (), s32[]{:S(2)}) async-start(), calls=%async_computation.1 | async-start | bytes 4128768 | tf_op jit(solution)/shard_map/reduce_scatter | solution.py:270
  21.1 5.9 %copy-start.8 = (s32[1,4]{1,0:T(1,128)S(1)}, s32[1,4]{1,0:T(1,128)}, u32[]{:S(2)}) copy-start(s32[1,4]{1,0:T(1,128)} %param.20) | copy-start | bytes 52
  21.1 6.1 %copy-start.2 = (bf16[512,896]{1,0:T(8,128)(2,1)S(1)}, bf16[512,896]{1,0:T(8,128)(2,1)}, u32[]{:S(2)}) copy-start(bf16[512,896]{1,0:T(8,128)(2,1)} %param.15) | copy-start | bytes 2752516
  23.4 5.1 %copy-start.1 = (bf16[512,896]{1,0:T(8,128)(2,1)S(1)}, bf16[512,896]{1,0:T(8,128)(2,1)}, u32[]{:S(2)}) copy-start(bf16[512,896]{1,0:T(8,128)(2,1)} %param.16) | copy-start | bytes 2752516
  23.4 10.4 %collective-permute-start = (bf16[200,896]{1,0:T(8,128)(2,1)}, bf16[200,896]{1,0:T(8,128)(2,1)}, u32[]{:S(2)}, u32[]{:S(2)}) collective-permute-start(bf16[200,896]{1,0:T(8,128)(2,1)} %get-tuple-element.38), channel_id=1, source_target_pairs={{0,8},{8,16},{16,24},{24,32},{32,40},{40,48},{48,56},{56,64},{64,7... | collective-permute-start | bytes 1075208 | tf_op jit(solution)/shard_map/ppermute | solution.py:23
  25.0 9.9 %collective-permute-start.1 = (bf16[200,896]{1,0:T(8,128)(2,1)S(1)}, bf16[200,896]{1,0:T(8,128)(2,1)}, u32[]{:S(2)}, u32[]{:S(2)}) collective-permute-start(bf16[200,896]{1,0:T(8,128)(2,1)S(1)} %get-tuple-element.39), channel_id=1, source_target_pairs={{0,248},{8,0},{16,8},{24,16},{32,24},{40,32},{48,40},{56,48},{64,5... | collective-permute-start | bytes 1075208 | tf_op jit(solution)/shard_map/ppermute | solution.py:23
  31.3 18.6 %copy-start.3 = (bf16[512,896]{0,1:T(8,128)(2,1)S(1)}, bf16[512,896]{0,1:T(8,128)(2,1)}, u32[]{:S(2)}) copy-start(bf16[512,896]{0,1:T(8,128)(2,1)} %copy.32) | copy-start | bytes 2752516
  31.3 18.6 %copy-start.5 = (bf16[512,896]{0,1:T(8,128)(2,1)S(1)}, bf16[512,896]{0,1:T(8,128)(2,1)}, u32[]{:S(2)}) copy-start(bf16[512,896]{0,1:T(8,128)(2,1)} %copy.33) | copy-start | bytes 2752516
  43.6 19.5 %collective-permute-start.2 = (bf16[192,1024]{1,0:T(8,128)(2,1)}, bf16[192,1024]{1,0:T(8,128)(2,1)S(1)}, u32[]{:S(2)}, u32[]{:S(2)}) collective-permute-start(bf16[192,1024]{1,0:T(8,128)(2,1)} %get-tuple-element.43), channel_id=1, source_target_pairs={{0,248},{8,0},{16,8},{24,16},{32,24},{40,32},{48,40},{56,48},{64,5... | collective-permute-start | bytes 1179656 | tf_op jit(solution)/shard_map/ppermute | solution.py:23
  49.6 13.6 %collective-permute-start.3 = (bf16[192,1024]{1,0:T(8,128)(2,1)}, bf16[192,1024]{1,0:T(8,128)(2,1)}, u32[]{:S(2)}, u32[]{:S(2)}) collective-permute-start(bf16[192,1024]{1,0:T(8,128)(2,1)} %get-tuple-element.44), channel_id=1, source_target_pairs={{0,8},{8,16},{16,24},{24,32},{32,40},{40,48},{48,56},{56,64},{64,7... | collective-permute-start | bytes 1179656 | tf_op jit(solution)/shard_map/ppermute | solution.py:23
  52.9 3.5 %copy-start.4 = (bf16[512,896]{0,1:T(8,128)(2,1)S(1)}, bf16[512,896]{0,1:T(8,128)(2,1)}, u32[]{:S(2)}) copy-start(bf16[512,896]{0,1:T(8,128)(2,1)} %copy.34) | copy-start | bytes 2752516
  63.1 3.1 %copy-start.7 = (bf16[192,1024]{1,0:T(8,128)(2,1)}, bf16[192,1024]{1,0:T(8,128)(2,1)S(1)}, u32[]{:S(2)}) copy-start(bf16[192,1024]{1,0:T(8,128)(2,1)S(1)} %collective-permute-done.2) | copy-start | bytes 1179652
  66.2 1.2 slice-start
  77.8 1.1 copy-start.6
  78.9 19.1 %collective-permute-start.4 = (bf16[2,192,896]{2,1,0:T(8,128)(2,1)S(1)}, bf16[2,192,896]{2,1,0:T(8,128)(2,1)S(1)}, u32[]{:S(2)}, u32[]{:S(2)}) collective-permute-start(bf16[2,192,896]{2,1,0:T(8,128)(2,1)S(1)} %copy-done.6), channel_id=1, source_target_pairs={{0,8},{8,16},{16,24},{24,32},{32,40},{40,48},{48,56},{56,64},{64,7... | collective-permute-start | bytes 2064392 | tf_op jit(solution)/shard_map/ppermute | solution.py:23
  78.9 19.2 %collective-permute-start.5 = (bf16[2,192,896]{2,1,0:T(8,128)(2,1)S(1)}, bf16[2,192,896]{2,1,0:T(8,128)(2,1)S(1)}, u32[]{:S(2)}, u32[]{:S(2)}) collective-permute-start(bf16[2,192,896]{2,1,0:T(8,128)(2,1)S(1)} %get-tuple-element.48), channel_id=1, source_target_pairs={{0,248},{8,0},{16,8},{24,16},{32,24},{40,32},{48,40},{56,48},{64,5... | collective-permute-start | bytes 2064392 | tf_op jit(solution)/shard_map/ppermute | solution.py:23
Sparse Core Ops, SparseCore 0:
  78.0 43.4 reduce-scatter.1

commit v12 on v10

--- a/solution.py
+++ b/solution.py
@@ -52,7 +52,10 @@
     def entry(i):
         return jnp.sum(jnp.where(lanes == i, tag, 0.0), axis=1, keepdims=True)
 
-    return entry(0), entry(1) * 32 + entry(2)
+    first = entry(0) == 1.0
+    slot = jnp.where(first, entry(1), entry(2))
+    prior = jnp.where(first, entry(3) * 32 + entry(4), entry(5) * 32 + entry(6))
+    return slot, prior
 
 
 def prior_kernel(head_count, left_ref, right_ref, key_ref, value_ref, to_left_ref, to_right_ref, numer_ref):
@@ -178,16 +181,24 @@
     def rows_of(source, start):
         return lax.dynamic_slice_in_dim(source, start, NEWCAP, 0)
 
-    def query_bundle(start, length, slot, prior):
-        tag = jnp.stack([slot, prior // 32, prior % 32, length]).astype(jnp.bfloat16)
-        tag_rows = jnp.zeros((TAG_ROWS, feat_width), jnp.bfloat16).at[0, :4].set(tag)
+    raw_tag = jnp.stack(
+        [
+            cache_slot[0, 0], cache_slot[0, 1],
+            prior_len[0, 0] // 32, prior_len[0, 0] % 32,
+            prior_len[0, 1] // 32, prior_len[0, 1] % 32,
+        ]
+    )
+
+    def query_bundle(start, pick):
+        tag = jnp.concatenate([pick.astype(jnp.int32)[None], raw_tag]).astype(jnp.bfloat16)
+        tag_rows = jnp.zeros((TAG_ROWS, feat_width), jnp.bfloat16).at[0, : tag.shape[0]].set(tag)
         return jnp.concatenate([rows_of(queries, start), tag_rows], axis=0)
 
     right_start, right_len, right_slot, right_prior = request_at(1)
     left_start, left_len, left_slot, left_prior = request_at(-1)
 
-    from_left = shifted(query_bundle(right_start, right_len, right_slot, right_prior), "req", 1)
-    from_right = shifted(query_bundle(left_start, left_len, left_slot, left_prior), "req", -1)
+    from_left = shifted(query_bundle(right_start, first_right), "req", 1)
+    from_right = shifted(query_bundle(left_start, jnp.logical_not(first_right)), "req", -1)
 
     served = serve_slots(from_left, from_right, cache_keys, cache_values, head_count)
     held_ends, served = lax.optimization_barrier((req_ends, served))
@@ -269,8 +280,11 @@
     )
 
     slot_ids = jnp.arange(slot_count, dtype=jnp.int32)
-    left_slot_id = from_left[NEWCAP, 0].astype(jnp.int32)
-    right_slot_id = from_right[NEWCAP, 0].astype(jnp.int32)
+    def slot_id(bundle):
+        return jnp.where(bundle[NEWCAP, 0] == 1, bundle[NEWCAP, 1], bundle[NEWCAP, 2]).astype(jnp.int32)
+
+    left_slot_id = slot_id(from_left)
+    right_slot_id = slot_id(from_right)
 
     def stored(from_left_rows, from_right_rows):
         at_left = (slot_ids == left_slot_id)[:, None, None]

time: 128 us -> 126 us (0.984)
  waiting for transfers between devices: 38.7 us -> 34 us
  between operations: 25.3 us -> 28 us
    ppermute x6, waiting for transfers between devices: 19.3 us -> 13.8 us  [shifted(): return lax.ppermute(value, axis, pairs)]
    slice x4 -> x3, local copies, waits for them, and re-layouts: 5 us -> 4.06 us  [the longest x2 2.75 us: slot_id(): bundle[NEWCAP, 2]]
    unnamed x21 -> x23, local copies, waits for them, and re-layouts: 5.05 us -> 5.04 us
where the time goes in v12:
time: 126 us; the launch traced here: 125 us
  waiting for transfers between devices  34 us (27%)
  between operations  28 us (22%)
  matrix products  18.2 us (14%)
  local copies, waits for them, and re-layouts  16.9 us (13%)
  other arithmetic  10.2 us (8%)
  starting transfers between devices  9.32 us (7%)
  Pallas kernels  8.74 us (7%)
    reduce_scatter x1, waiting for transfers between devices, body(): lax.psum_scatter(jnp.dot(attended, out_proj, preferred_element_type=jnp.f...  20.2 us
    ppermute x6, waiting for transfers between devices, shifted(): return lax.ppermute(value, axis, pairs)  13.8 us
    dot_general x1, matrix products, body(): jnp.dot(attended, out_proj, preferred_element_type=jnp.float32)  10.4 us
    ppermute x6, starting transfers between devices, shifted(): return lax.ppermute(value, axis, pairs)  9.28 us
    pallas_call x1, Pallas kernels, serve_slots(): pl.pallas_call(functools.partial(prior_kernel, head_count), out_shape=(ja...  8.74 us
    unnamed x23, local copies, waits for them, and re-layouts  5.04 us
    dot_general x1, matrix products, attend_part(): jnp.einsum('hts,shd->thd', weights.astype(jnp.bfloat16), value_heads, pre...  4.91 us
    reduce_sum x1, other arithmetic, attend_part(): row_total = jnp.sum(weights, axis=2)  3.31 us
  transfers between devices with their start and end apart: 7, of which 3 were waited for; matrix products, arithmetic and copies ran while one was open for 19% of the time, Pallas kernels for 0%

profile of v12, /device:TPU:8, one launch (start us, length us, event | category | flops | bytes accessed | tf_op | source)
XLA Modules:
  0.0 125.4 jit_solution(3358279868960568532)
XLA Ops:
  7.2 1.3 %fusion.65 = (s32[1,1]{1,0:T(1,128)}, s32[1,1]{1,0:T(1,128)}) fusion(s32[1,4]{1,0:T(1,128)} %param.20), kind=kLoop, calls=%fused_computation.120 | loop fusion | bytes 16 | tf_op jit(solution)/shard_map/slice | solution.py:176
  10.6 1.3 %fusion.66 = (s32[1,1]{1,0:T(1,128)}, s32[1,1]{1,0:T(1,128)}) fusion(s32[1,2]{1,0:T(1,128)} %param.23), kind=kLoop, calls=%fused_computation.121 | loop fusion | bytes 16 | tf_op jit(solution)/shard_map/slice | solution.py:188
  17.8 1.3 %constant_dynamic-slice_fusion = (bf16[192,896]{1,0:T(8,128)(2,1)S(1)}, bf16[192,896]{1,0:T(8,128)(2,1)S(1)}) fusion(bf16[512,896]{1,0:T(8,128)(2,1)} %param.14, s32[]{:T(128)S(6)} %select_n.207, s32[]{:T(128)S(6)} %select_n.201), kind=kLoop, calls=%fused_computation.94 | loop fusion | bytes 1376264 | tf_op jit(solution)/shard_map/dynamic_slice | solution.py:182
  20.0 2.2 %collective-permute-start.1 = (bf16[200,896]{1,0:T(8,128)(2,1)}, bf16[200,896]{1,0:T(8,128)(2,1)S(1)}, u32[]{:S(2)}, u32[]{:S(2)}) collective-permute-start(bf16[200,896]{1,0:T(8,128)(2,1)} %fusion.38), channel_id=1, source_target_pairs={{0,248},{8,0},{16,8},{24,16},{32,24},{40,32},{48,40},{56,48},{64,5... | collective-permute-start | bytes 1075208 | tf_op jit(solution)/shard_map/ppermute | solution.py:23
  25.8 1.3 %copy.32 = bf16[512,896]{0,1:T(8,128)(2,1)} copy(bf16[512,896]{1,0:T(8,128)(2,1)S(1)} %copy-done) | data formatting | bytes 1835008 | tf_op args[0]
  27.4 1.3 %copy.33 = bf16[512,896]{0,1:T(8,128)(2,1)} copy(bf16[512,896]{1,0:T(8,128)(2,1)S(1)} %copy-done.2) | data formatting | bytes 1835008 | tf_op args[1]
  28.7 1.3 %copy.34 = bf16[512,896]{0,1:T(8,128)(2,1)} copy(bf16[512,896]{1,0:T(8,128)(2,1)S(1)} %copy-done.1) | data formatting | bytes 1835008 | tf_op args[2]
  30.5 1.0 pad_maximum_fusion
  31.5 6.6 %collective-permute-done.left_ref = bf16[200,896]{1,0:T(8,128)(2,1)} collective-permute-done((bf16[200,896]{1,0:T(8,128)(2,1)}, bf16[200,896]{1,0:T(8,128)(2,1)}, u32[]{:S(2)}, u32[]{:S(2)}) %collective-permute-start) | collective-permute-done | bytes 358432 | tf_op jit(solution)/shard_map/ppermute | solution.py:23
  38.1 8.7 %shard_map.121 = (bf16[192,1024]{1,0:T(8,128)(2,1)}, bf16[192,1024]{1,0:T(8,128)(2,1)}) custom-call(bf16[200,896]{1,0:T(8,128)(2,1)} %collective-permute-done.left_ref, bf16[200,896]{1,0:T(8,128)(2,1)} %copy-done.8, bf16[2,1024,896]{2,1,0:T(8,128)(2,1)} %key_ref.1, bf16[2,1024,896]{2,1,0:T(8,128)(2,1)} %value_ref.1), custom_call_target="tpu_custom_call" | custom-call | flops 2013265920 | bytes 8843264 | tf_op jit(solution)/shard_map/pallas_call | solution.py:121
  46.8 5.1 %collective-permute-start.2 = (bf16[192,1024]{1,0:T(8,128)(2,1)}, bf16[192,1024]{1,0:T(8,128)(2,1)S(1)}, u32[]{:S(2)}, u32[]{:S(2)}) collective-permute-start(bf16[192,1024]{1,0:T(8,128)(2,1)} %get-tuple-element.39), channel_id=1, source_target_pairs={{0,248},{8,0},{16,8},{24,16},{32,24},{40,32},{48,40},{56,48},{64,5... | collective-permute-start | bytes 1179656 | tf_op jit(solution)/shard_map/ppermute | solution.py:23
  52.2 2.9 %fusion = (f32[4,512]{1,0:T(4,128)S(1)}, f32[4,512,512]{1,2,0:T(8,128)}) fusion(pred[512,512]{0,1:T(8,128)(4,1)S(1)} %fusion.10, bf16[512,4,224]{0,2,1:T(8,128)(2,1)S(1)} %bitcast.54, bf16[512,4,224]{0,2,1:T(8,128)(2,1)S(1)} %bitcast.56), kind=kOutput, calls=%fused_computation.3 | convolution fusion | flops 472905728 | bytes 6299648 | tf_op jit(solution)/shard_map/thd,shd->hts/dot_general | solution.py:32
  55.2 3.3 %fusion.1 = f32[4,512]{1,0:T(4,128)S(1)} fusion(f32[4,512,512]{1,2,0:T(8,128)} %get-tuple-element.88, f32[4,512]{1,0:T(4,128)S(1)} %get-tuple-element.87, pred[512,512]{0,1:T(8,128)(4,1)S(1)} %fusion.10), kind=kLoop, calls=%fused_computation.4 | loop fusion | flops 5240832 | bytes 4472832 | tf_op jit(solution)/shard_map/reduce_sum | solution.py:38
  58.7 4.9 %fusion.3 = f32[4,512,224]{1,2,0:T(8,128)} fusion(bf16[512,4,224]{0,2,1:T(8,128)(2,1)S(1)} %bitcast.55, f32[4,512,512]{1,2,0:T(8,128)} %get-tuple-element.88, f32[4,512]{1,0:T(4,128)S(1)} %get-tuple-element.87, pred[512,512]{0,1:T(8,128)(4,1)S(1)} %fusion.10), kind=kOutput, calls=%fused_computation.6 | convolution fusion | flops 475004928 | bytes 7217152 | tf_op jit(solution)/shard_map/hts,shd->thd/dot_general | solution.py:39
  63.6 1.8 %copy.37 = f32[512,896]{1,0:T(8,128)S(1)} copy(f32[512,896]{0,1:T(8,128)} %bitcast.53) | data formatting | bytes 3670016 | tf_op jit(solution)/shard_map/reshape | solution.py:45
  66.4 1.0 slice.173
  69.7 10.4 %convolution_convert_fusion = bf16[512,3584]{1,0:T(8,128)(2,1)} fusion(bf16[896,3584]{1,0:T(8,128)(2,1)} %param.19, f32[512,896]{1,0:T(8,128)S(1)} %copy.37, s32[]{:T(128)S(6)} %select_n.217, bf16[192,896]{1,0:T(8,128)(2,1)S(1)} %slice-done, s32[]{:T(128)S(6)} %select_n.218, bf16[192,896]{1,0:T(8,128)(2,1)S(1)} %slice.173, f32[512]{0:T(512)S(1)} %get-tuple-element.54, ...), kind=kOutput, calls=%fused_computation | convolution fusion | flops 3299344384 | bytes 12644872 | tf_op jit(solution)/shard_map/dot_general | solution.py:276
  80.1 1.1 copy-done.6
  81.2 2.0 %collective-permute-start.5 = (bf16[2,192,896]{2,1,0:T(8,128)(2,1)S(1)}, bf16[2,192,896]{2,1,0:T(8,128)(2,1)S(1)}, u32[]{:S(2)}, u32[]{:S(2)}) collective-permute-start(bf16[2,192,896]{2,1,0:T(8,128)(2,1)S(1)} %get-tuple-element.44), channel_id=1, source_target_pairs={{0,248},{8,0},{16,8},{24,16},{32,24},{40,32},{48,40},{56,48},{64,5... | collective-permute-start | bytes 2064392 | tf_op jit(solution)/shard_map/ppermute | solution.py:23
  83.2 1.4 %fusion.64 = (bf16[1,1]{1,0:T(2,128)(2,1)}, bf16[1,1]{1,0:T(2,128)(2,1)}, bf16[1,1]{1,0:T(2,128)(2,1)}) fusion(bf16[200,896]{1,0:T(8,128)(2,1)} %copy-done.8), kind=kLoop, calls=%fused_computation.119 | loop fusion | bytes 12 | tf_op jit(solution)/shard_map/slice | solution.py:284
  86.5 1.4 %fusion.63 = (bf16[1,1]{1,0:T(2,128)(2,1)}, bf16[1,1]{1,0:T(2,128)(2,1)}, bf16[1,1]{1,0:T(2,128)(2,1)}) fusion(bf16[200,896]{1,0:T(8,128)(2,1)} %collective-permute-done.left_ref), kind=kLoop, calls=%fused_computation.118 | loop fusion | bytes 12 | tf_op jit(solution)/shard_map/slice | solution.py:284
  89.8 7.2 %collective-permute-done.4 = bf16[2,192,896]{2,1,0:T(8,128)(2,1)S(1)} collective-permute-done((bf16[2,192,896]{2,1,0:T(8,128)(2,1)S(1)}, bf16[2,192,896]{2,1,0:T(8,128)(2,1)S(1)}, u32[]{:S(2)}, u32[]{:S(2)}) %collective-permute-start.4) | collective-permute-done | bytes 688160 | tf_op jit(solution)/shard_map/ppermute | solution.py:23
  97.1 1.3 %select_select_fusion = (bf16[2,192,896]{2,1,0:T(8,128)(2,1)}, bf16[2,192,896]{2,1,0:T(8,128)(2,1)}) fusion(pred[2]{0:T(512)(128)(4,1)S(1)} %get-tuple-element.95, pred[2]{0:T(512)(128)(4,1)S(1)} %get-tuple-element.96, bf16[192,896]{1,0:T(8,128)(2,1)S(1)} %get-tuple-element.71, bf16[192,896]{1,0:T(8,128)(2,1)S(1)} %get-tuple-element.69, ...), kind=kLoop, calls=%fused_computation.43 | loop fusion | flops 1376256 | bytes 2752516 | tf_op jit(solution)/shard_map/jit(_where)/select_n | solution.py:292
  98.4 20.2 %reduce-scatter.2.cloned.1.call-done = bf16[64,3584]{1,0:T(8,128)(2,1)} async-done(((bf16[512,3584]{1,0:T(8,128)(2,1)}), bf16[64,3584]{1,0:T(8,128)(2,1)}) %reduce-scatter.2.cloned.1.call-update) | async-done | bytes 458768 | tf_op jit(solution)/shard_map/reduce_scatter | solution.py:275
  (57 shorter events, 7.1 us)
Async XLA Ops:
  7.2 18.6 %copy-start = (bf16[512,896]{1,0:T(8,128)(2,1)S(1)}, bf16[512,896]{1,0:T(8,128)(2,1)}, u32[]{:S(2)}) copy-start(bf16[512,896]{1,0:T(8,128)(2,1)} %param.14) | copy-start | bytes 2752516
  7.2 111.4 %reduce-scatter.2.cloned.1.call-start = ((), (), s32[]{:S(2)}) async-start(), calls=%async_computation.1 | async-start | bytes 4128768 | tf_op jit(solution)/shard_map/reduce_scatter | solution.py:275
  17.8 9.4 %copy-start.9 = (s32[1,4]{1,0:T(1,128)S(1)}, s32[1,4]{1,0:T(1,128)}, u32[]{:S(2)}) copy-start(s32[1,4]{1,0:T(1,128)} %param.20) | copy-start | bytes 52
  17.8 9.5 %copy-start.2 = (bf16[512,896]{1,0:T(8,128)(2,1)S(1)}, bf16[512,896]{1,0:T(8,128)(2,1)}, u32[]{:S(2)}) copy-start(bf16[512,896]{1,0:T(8,128)(2,1)} %param.15) | copy-start | bytes 2752516
  20.0 11.4 %collective-permute-start.1 = (bf16[200,896]{1,0:T(8,128)(2,1)}, bf16[200,896]{1,0:T(8,128)(2,1)S(1)}, u32[]{:S(2)}, u32[]{:S(2)}) collective-permute-start(bf16[200,896]{1,0:T(8,128)(2,1)} %fusion.38), channel_id=1, source_target_pairs={{0,248},{8,0},{16,8},{24,16},{32,24},{40,32},{48,40},{56,48},{64,5... | collective-permute-start | bytes 1075208 | tf_op jit(solution)/shard_map/ppermute | solution.py:23
  22.3 6.4 %copy-start.1 = (bf16[512,896]{1,0:T(8,128)(2,1)S(1)}, bf16[512,896]{1,0:T(8,128)(2,1)}, u32[]{:S(2)}) copy-start(bf16[512,896]{1,0:T(8,128)(2,1)} %param.16) | copy-start | bytes 2752516
  23.1 15.0 %collective-permute-start = (bf16[200,896]{1,0:T(8,128)(2,1)}, bf16[200,896]{1,0:T(8,128)(2,1)}, u32[]{:S(2)}, u32[]{:S(2)}) collective-permute-start(bf16[200,896]{1,0:T(8,128)(2,1)} %fusion.37), channel_id=1, source_target_pairs={{0,8},{8,16},{16,24},{24,32},{32,40},{40,48},{48,56},{56,64},{64,7... | collective-permute-start | bytes 1075208 | tf_op jit(solution)/shard_map/ppermute | solution.py:23
  31.5 20.7 %copy-start.3 = (bf16[512,896]{0,1:T(8,128)(2,1)S(1)}, bf16[512,896]{0,1:T(8,128)(2,1)}, u32[]{:S(2)}) copy-start(bf16[512,896]{0,1:T(8,128)(2,1)} %copy.32) | copy-start | bytes 2752516
  31.5 20.7 %copy-start.5 = (bf16[512,896]{0,1:T(8,128)(2,1)S(1)}, bf16[512,896]{0,1:T(8,128)(2,1)}, u32[]{:S(2)}) copy-start(bf16[512,896]{0,1:T(8,128)(2,1)} %copy.33) | copy-start | bytes 2752516
  31.5 6.6 %copy-start.8 = (bf16[200,896]{1,0:T(8,128)(2,1)}, bf16[200,896]{1,0:T(8,128)(2,1)S(1)}, u32[]{:S(2)}) copy-start(bf16[200,896]{1,0:T(8,128)(2,1)S(1)} %collective-permute-done.1.right_ref) | copy-start | bytes 1075204
  46.8 18.6 %collective-permute-start.2 = (bf16[192,1024]{1,0:T(8,128)(2,1)}, bf16[192,1024]{1,0:T(8,128)(2,1)S(1)}, u32[]{:S(2)}, u32[]{:S(2)}) collective-permute-start(bf16[192,1024]{1,0:T(8,128)(2,1)} %get-tuple-element.39), channel_id=1, source_target_pairs={{0,248},{8,0},{16,8},{24,16},{32,24},{40,32},{48,40},{56,48},{64,5... | collective-permute-start | bytes 1179656 | tf_op jit(solution)/shard_map/ppermute | solution.py:23
  51.9 13.6 %collective-permute-start.3 = (bf16[192,1024]{1,0:T(8,128)(2,1)}, bf16[192,1024]{1,0:T(8,128)(2,1)}, u32[]{:S(2)}, u32[]{:S(2)}) collective-permute-start(bf16[192,1024]{1,0:T(8,128)(2,1)} %get-tuple-element.40), channel_id=1, source_target_pairs={{0,8},{8,16},{16,24},{24,32},{32,40},{40,48},{48,56},{56,64},{64,7... | collective-permute-start | bytes 1179656 | tf_op jit(solution)/shard_map/ppermute | solution.py:23
  55.2 3.5 %copy-start.4 = (bf16[512,896]{0,1:T(8,128)(2,1)S(1)}, bf16[512,896]{0,1:T(8,128)(2,1)}, u32[]{:S(2)}) copy-start(bf16[512,896]{0,1:T(8,128)(2,1)} %copy.34) | copy-start | bytes 2752516
  65.4 3.1 %copy-start.7 = (bf16[192,1024]{1,0:T(8,128)(2,1)}, bf16[192,1024]{1,0:T(8,128)(2,1)S(1)}, u32[]{:S(2)}) copy-start(bf16[192,1024]{1,0:T(8,128)(2,1)S(1)} %collective-permute-done.2) | copy-start | bytes 1179652
  68.5 1.2 slice-start
  80.1 1.1 copy-start.6
  81.2 15.7 %collective-permute-start.4 = (bf16[2,192,896]{2,1,0:T(8,128)(2,1)S(1)}, bf16[2,192,896]{2,1,0:T(8,128)(2,1)S(1)}, u32[]{:S(2)}, u32[]{:S(2)}) collective-permute-start(bf16[2,192,896]{2,1,0:T(8,128)(2,1)S(1)} %copy-done.6), channel_id=1, source_target_pairs={{0,8},{8,16},{16,24},{24,32},{32,40},{40,48},{48,56},{56,64},{64,7... | collective-permute-start | bytes 2064392 | tf_op jit(solution)/shard_map/ppermute | solution.py:23
  81.2 15.8 %collective-permute-start.5 = (bf16[2,192,896]{2,1,0:T(8,128)(2,1)S(1)}, bf16[2,192,896]{2,1,0:T(8,128)(2,1)S(1)}, u32[]{:S(2)}, u32[]{:S(2)}) collective-permute-start(bf16[2,192,896]{2,1,0:T(8,128)(2,1)S(1)} %get-tuple-element.44), channel_id=1, source_target_pairs={{0,248},{8,0},{16,8},{24,16},{32,24},{40,32},{48,40},{56,48},{64,5... | collective-permute-start | bytes 2064392 | tf_op jit(solution)/shard_map/ppermute | solution.py:23
Sparse Core Ops, SparseCore 0:
  80.3 38.2 reduce-scatter.1

commit v13 on v12

--- a/solution.py
+++ b/solution.py
@@ -143,6 +143,58 @@
         ),
     )(from_left, from_right, cache_keys, cache_values)
 
+
+def own_kernel(head_count, query_ref, key_ref, value_ref, seg_col_ref, seg_row_ref, numer_ref, stats_ref):
+    row_count, feat_width = query_ref.shape
+    rows = lax.broadcasted_iota(jnp.int32, (row_count, row_count), 0)
+    cols = lax.broadcasted_iota(jnp.int32, (row_count, row_count), 1)
+    live = (seg_col_ref[...] == seg_row_ref[...]) & (cols <= rows)
+    stat_lanes = lax.broadcasted_iota(jnp.int32, stats_ref.shape, 1)
+    stats = jnp.zeros(stats_ref.shape, jnp.float32)
+    numer_ref[...] = jnp.zeros((row_count, feat_width), jnp.float32)
+    for h in range(head_count):
+        low = (h * HD) // 128 * 128
+        high = min(feat_width, -(-((h + 1) * HD) // 128) * 128)
+        lanes = low + lax.broadcasted_iota(jnp.int32, (1, high - low), 1)
+        in_head = (lanes >= h * HD) & (lanes < (h + 1) * HD)
+        head_query = jnp.where(in_head, query_ref[:, low:high], jnp.zeros((), query_ref.dtype))
+        scores = lax.dot_general(
+            head_query, key_ref[:, low:high], (((1,), (1,)), ((), ())),
+            preferred_element_type=jnp.float32,
+        ) * (1.0 / math.sqrt(HD))
+        scores = jnp.where(live, scores, floor_value)
+        row_top = jnp.max(scores, axis=1, keepdims=True)
+        weights = jnp.where(live, jnp.exp(scores - row_top), 0.0)
+        row_total = jnp.sum(weights, axis=1, keepdims=True)
+        head_out = jnp.dot(
+            weights.astype(jnp.bfloat16), value_ref[:, low:high], preferred_element_type=jnp.float32
+        )
+        numer_ref[:, low:high] = numer_ref[:, low:high] + jnp.where(in_head, head_out, 0.0)
+        stats = jnp.where(stat_lanes == h, row_top, stats)
+        stats = jnp.where(stat_lanes == head_count + h, row_total, stats)
+    stats_ref[...] = stats
+
+
+def attend_own(queries, keys_new, values_new, segment, head_count):
+    row_count, feat_width = queries.shape
+    vmem = pl.BlockSpec(memory_space=pltpu.VMEM)
+    numer, stats = pl.pallas_call(
+        functools.partial(own_kernel, head_count),
+        out_shape=(
+            jax.ShapeDtypeStruct((row_count, feat_width), jnp.float32),
+            jax.ShapeDtypeStruct((row_count, 128), jnp.float32),
+        ),
+        in_specs=[vmem] * 5,
+        out_specs=(vmem, vmem),
+        cost_estimate=pl.CostEstimate(
+            flops=4 * row_count * row_count * 1280,
+            transcendentals=head_count * row_count * row_count,
+            bytes_accessed=6 * row_count * feat_width + 4 * row_count * (feat_width + 128),
+        ),
+    )(queries, keys_new, values_new, segment[:, None], segment[None, :])
+    return numer, stats[:, :head_count], stats[:, head_count : 2 * head_count]
+
+
 def body(
     queries,
     keys_new,
@@ -203,8 +255,7 @@
     served = serve_slots(from_left, from_right, cache_keys, cache_values, head_count)
     held_ends, served = lax.optimization_barrier((req_ends, served))
     segment = jnp.sum((positions[:, None] >= held_ends[None, :]).astype(jnp.int32), axis=1)
-    own_live = (segment[:, None] == segment[None, :]) & (positions[None, :] <= positions[:, None])
-    own_numer, own_top, own_total = attend_part(queries, keys_new, values_new, own_live, head_count)
+    own_numer, own_top, own_total = attend_own(queries, keys_new, values_new, segment, head_count)
 
     back_left, back_right = served
     got_right = shifted(back_left, "req", -1)

time: 126 us -> 122 us (0.968)
  matrix products: 18.2 us -> 10.5 us
  local copies, waits for them, and re-layouts: 16.9 us -> 9.75 us
  Pallas kernels: 8.74 us -> 14.8 us
  waiting for transfers between devices: 34 us -> 38.1 us
  starting transfers between devices: 9.32 us -> 12.4 us
  other arithmetic: 10.2 us -> 7.44 us
    dot_general x2 -> x0, matrix products: 7.77 us -> none  [the longest x1 4.91 us: attend_part(): jnp.einsum('hts,shd->thd', weights.astype(jnp.bfloat16), value_heads, pre...]
    pallas_call x0 -> x1, Pallas kernels: none -> 6.08 us  [attend_own(): pl.pallas_call(functools.partial(own_kernel, head_count), out_shape=(jax....]
    unnamed x23 -> x22, local copies, waits for them, and re-layouts: 5.04 us -> 0.1 us
    ppermute x6, waiting for transfers between devices: 13.8 us -> 17.2 us  [shifted(): return lax.ppermute(value, axis, pairs)]
    reduce_sum x1 -> x0, other arithmetic: 3.31 us -> none  [attend_part(): row_total = jnp.sum(weights, axis=2)]
    ppermute x6, starting transfers between devices: 9.28 us -> 12.4 us  [shifted(): return lax.ppermute(value, axis, pairs)]
    reshape x1 -> x0, local copies, waits for them, and re-layouts: 1.81 us -> none  [attend_part(): numerator.reshape(row_count, head_count * HD)]
  transfers between devices with their start and end apart: 7 -> 7, of which waited for: 3 -> 5; matrix products, arithmetic and copies ran while one was open for 19% -> 8% of each run, Pallas kernels for 0% -> 5%
where the time goes in v13:
time: 122 us; the launch traced here: 121 us
  waiting for transfers between devices  38.1 us (31%)
  between operations  28 us (23%)
  Pallas kernels  14.8 us (12%)
  starting transfers between devices  12.4 us (10%)
  matrix products  10.5 us (9%)
  local copies, waits for them, and re-layouts  9.75 us (8%)
  other arithmetic  7.44 us (6%)
    reduce_scatter x1, waiting for transfers between devices, body(): lax.psum_scatter(jnp.dot(attended, out_proj, preferred_element_type=jnp.f...  20.9 us
    ppermute x6, waiting for transfers between devices, shifted(): return lax.ppermute(value, axis, pairs)  17.2 us
    ppermute x6, starting transfers between devices, shifted(): return lax.ppermute(value, axis, pairs)  12.4 us
    dot_general x1, matrix products, body(): jnp.dot(attended, out_proj, preferred_element_type=jnp.float32)  10.5 us
    pallas_call x1, Pallas kernels, serve_slots(): pl.pallas_call(functools.partial(prior_kernel, head_count), out_shape=(ja...  8.74 us
    pallas_call x1, Pallas kernels, attend_own(): pl.pallas_call(functools.partial(own_kernel, head_count), out_shape=(jax....  6.08 us
    slice x2, local copies, waits for them, and re-layouts, slot_id(): bundle[NEWCAP, 2]  2.76 us
  transfers between devices with their start and end apart: 7, of which 5 were waited for; matrix products, arithmetic and copies ran while one was open for 8% of the time, Pallas kernels for 5%

profile of v13, /device:TPU:8, one launch (start us, length us, event | category | flops | bytes accessed | tf_op | source)
XLA Modules:
  0.0 121.1 jit_solution(164423547076418428)
XLA Ops:
  7.3 1.4 %fusion.51 = (s32[1,1]{1,0:T(1,128)}, s32[1,1]{1,0:T(1,128)}) fusion(s32[1,2]{1,0:T(1,128)} %param.23), kind=kLoop, calls=%fused_computation.104 | loop fusion | bytes 16 | tf_op jit(solution)/shard_map/slice | solution.py:240
  14.5 1.3 %fusion.50 = (s32[1,1]{1,0:T(1,128)}, s32[1,1]{1,0:T(1,128)}) fusion(s32[1,4]{1,0:T(1,128)} %param.20), kind=kLoop, calls=%fused_computation.103 | loop fusion | bytes 16 | tf_op jit(solution)/shard_map/slice | solution.py:228
  17.2 0.7 convert.31
  17.9 1.3 %constant_dynamic-slice_fusion = (bf16[192,896]{1,0:T(8,128)(2,1)S(1)}, bf16[192,896]{1,0:T(8,128)(2,1)S(1)}) fusion(bf16[512,896]{1,0:T(8,128)(2,1)} %query_ref.1, s32[]{:T(128)S(6)} %select_n.200, s32[]{:T(128)S(6)} %select_n.194), kind=kLoop, calls=%fused_computation.80 | loop fusion | bytes 1376264 | tf_op jit(solution)/shard_map/dynamic_slice | solution.py:234
  19.2 0.8 fusion.26
  20.0 1.6 %collective-permute-start = (bf16[200,896]{1,0:T(8,128)(2,1)}, bf16[200,896]{1,0:T(8,128)(2,1)}, u32[]{:S(2)}, u32[]{:S(2)}) collective-permute-start(bf16[200,896]{1,0:T(8,128)(2,1)} %fusion.26), channel_id=1, source_target_pairs={{0,8},{8,16},{16,24},{24,32},{32,40},{40,48},{48,56},{56,64},{64,7... | collective-permute-start | bytes 1075208 | tf_op jit(solution)/shard_map/ppermute | solution.py:23
  21.7 0.8 fusion.27
  22.5 0.6 collective-permute-start.1
  26.3 0.7 reduce-window.9
  27.6 2.9 %collective-permute-done.left_ref = bf16[200,896]{1,0:T(8,128)(2,1)} collective-permute-done((bf16[200,896]{1,0:T(8,128)(2,1)}, bf16[200,896]{1,0:T(8,128)(2,1)}, u32[]{:S(2)}, u32[]{:S(2)}) %collective-permute-start) | collective-permute-done | bytes 358432 | tf_op jit(solution)/shard_map/ppermute | solution.py:23
  30.4 2.2 %collective-permute-done.1.right_ref = bf16[200,896]{1,0:T(8,128)(2,1)} collective-permute-done((bf16[200,896]{1,0:T(8,128)(2,1)}, bf16[200,896]{1,0:T(8,128)(2,1)}, u32[]{:S(2)}, u32[]{:S(2)}) %collective-permute-start.1) | collective-permute-done | bytes 358432 | tf_op jit(solution)/shard_map/ppermute | solution.py:23
  32.6 8.7 %shard_map.121 = (bf16[192,1024]{1,0:T(8,128)(2,1)}, bf16[192,1024]{1,0:T(8,128)(2,1)}) custom-call(bf16[200,896]{1,0:T(8,128)(2,1)} %collective-permute-done.left_ref, bf16[200,896]{1,0:T(8,128)(2,1)} %collective-permute-done.1.right_ref, bf16[2,1024,896]{2,1,0:T(8,128)(2,1)} %key_ref.2, bf16[2,1024,896]{2,1,0:T(8,128)(2,1)} %value_ref.2), custom_call_target="tpu_custom_call" | custom-call | flops 2013265920 | bytes 8843264 | tf_op jit(solution)/shard_map/pallas_call | solution.py:121
  41.3 5.0 %collective-permute-start.2 = (bf16[192,1024]{1,0:T(8,128)(2,1)}, bf16[192,1024]{1,0:T(8,128)(2,1)S(1)}, u32[]{:S(2)}, u32[]{:S(2)}) collective-permute-start(bf16[192,1024]{1,0:T(8,128)(2,1)} %get-tuple-element.43), channel_id=1, source_target_pairs={{0,248},{8,0},{16,8},{24,16},{32,24},{40,32},{48,40},{56,48},{64,5... | collective-permute-start | bytes 1179656 | tf_op jit(solution)/shard_map/ppermute | solution.py:23
  47.1 0.7 convert_reduce_fusion
  47.8 0.9 copy.14.seg_col_ref
  48.7 6.1 %shard_map.122 = (f32[512,896]{1,0:T(8,128)}, f32[512,128]{1,0:T(8,128)}) custom-call(bf16[512,896]{1,0:T(8,128)(2,1)} %query_ref.1, bf16[512,896]{1,0:T(8,128)(2,1)} %key_ref.3, bf16[512,896]{1,0:T(8,128)(2,1)} %value_ref.3, s32[512,1]{1,0:T(8,128)} %copy.14.seg_col_ref, s32[1,512]{1,0:T(1,128)} %bitcast.38), custom_call_target="tpu_custom_call" | custom-call | flops 1342177280 | bytes 4849664 | tf_op jit(solution)/shard_map/pallas_call | solution.py:181
  54.8 5.5 %collective-permute-done.3 = bf16[192,1024]{1,0:T(8,128)(2,1)S(1)} collective-permute-done((bf16[192,1024]{1,0:T(8,128)(2,1)}, bf16[192,1024]{1,0:T(8,128)(2,1)S(1)}, u32[]{:S(2)}, u32[]{:S(2)}) %collective-permute-start.3) | collective-permute-done | bytes 393248 | tf_op jit(solution)/shard_map/ppermute | solution.py:23
  62.9 10.5 %convolution_convert_fusion = bf16[512,3584]{1,0:T(8,128)(2,1)} fusion(bf16[896,3584]{1,0:T(8,128)(2,1)} %param.19, f32[512,896]{1,0:T(8,128)S(1)} %copy-done.10, s32[]{:T(128)S(6)} %select_n.208, bf16[192,896]{1,0:T(8,128)(2,1)S(1)} %slice-done, s32[]{:T(128)S(6)} %select_n.209, bf16[192,896]{1,0:T(8,128)(2,1)S(1)} %slice-done.1, ...), kind=kOutput, calls=%fused_computation | convolution fusion | flops 3299344384 | bytes 12644872 | tf_op jit(solution)/shard_map/dot_general | solution.py:327
  73.5 5.1 %collective-permute-start.5 = (bf16[2,192,896]{2,1,0:T(8,128)(2,1)S(1)}, bf16[2,192,896]{2,1,0:T(8,128)(2,1)S(1)}, u32[]{:S(2)}, u32[]{:S(2)}) collective-permute-start(bf16[2,192,896]{2,1,0:T(8,128)(2,1)S(1)} %get-tuple-element.48), channel_id=1, source_target_pairs={{0,248},{8,0},{16,8},{24,16},{32,24},{40,32},{48,40},{56,48},{64,5... | collective-permute-start | bytes 2064392 | tf_op jit(solution)/shard_map/ppermute | solution.py:23
  78.6 1.4 %fusion.48 = (bf16[1,1]{1,0:T(2,128)(2,1)}, bf16[1,1]{1,0:T(2,128)(2,1)}, bf16[1,1]{1,0:T(2,128)(2,1)}) fusion(bf16[200,896]{1,0:T(8,128)(2,1)} %collective-permute-done.left_ref), kind=kLoop, calls=%fused_computation.101 | loop fusion | bytes 12 | tf_op jit(solution)/shard_map/slice | solution.py:335
  81.9 1.4 %fusion.49 = (bf16[1,1]{1,0:T(2,128)(2,1)}, bf16[1,1]{1,0:T(2,128)(2,1)}, bf16[1,1]{1,0:T(2,128)(2,1)}) fusion(bf16[200,896]{1,0:T(8,128)(2,1)} %collective-permute-done.1.right_ref), kind=kLoop, calls=%fused_computation.102 | loop fusion | bytes 12 | tf_op jit(solution)/shard_map/slice | solution.py:335
  85.2 6.7 %collective-permute-done.4 = bf16[2,192,896]{2,1,0:T(8,128)(2,1)S(1)} collective-permute-done((bf16[2,192,896]{2,1,0:T(8,128)(2,1)S(1)}, bf16[2,192,896]{2,1,0:T(8,128)(2,1)S(1)}, u32[]{:S(2)}, u32[]{:S(2)}) %collective-permute-start.4) | collective-permute-done | bytes 688160 | tf_op jit(solution)/shard_map/ppermute | solution.py:23
  92.0 1.3 %select_select_fusion = (bf16[2,192,896]{2,1,0:T(8,128)(2,1)}, bf16[2,192,896]{2,1,0:T(8,128)(2,1)}) fusion(pred[2]{0:T(512)(128)(4,1)S(1)} %get-tuple-element.97, pred[2]{0:T(512)(128)(4,1)S(1)} %get-tuple-element.98, bf16[192,896]{1,0:T(8,128)(2,1)S(1)} %get-tuple-element.75, bf16[192,896]{1,0:T(8,128)(2,1)S(1)} %get-tuple-element.73, ...), kind=kLoop, calls=%fused_computation.30 | loop fusion | flops 1376256 | bytes 2752516 | tf_op jit(solution)/shard_map/jit(_where)/select_n | solution.py:343
  93.4 20.9 %reduce-scatter.2.cloned.1.call-done = bf16[64,3584]{1,0:T(8,128)(2,1)} async-done(((bf16[512,3584]{1,0:T(8,128)(2,1)}), bf16[64,3584]{1,0:T(8,128)(2,1)}) %reduce-scatter.2.cloned.1.call-update) | async-done | bytes 458768 | tf_op jit(solution)/shard_map/reduce_scatter | solution.py:326
  (52 shorter events, 4.8 us)
Async XLA Ops:
  7.2 19.2 %copy-start.6 = (s32[1,4]{1,0:T(1,128)S(1)}, s32[1,4]{1,0:T(1,128)}, u32[]{:S(2)}) copy-start(s32[1,4]{1,0:T(1,128)} %param.20) | copy-start | bytes 52
  7.2 19.9 %copy-start.2 = (bf16[512,896]{1,0:T(8,128)(2,1)S(1)}, bf16[512,896]{1,0:T(8,128)(2,1)}, u32[]{:S(2)}) copy-start(bf16[512,896]{1,0:T(8,128)(2,1)} %value_ref.3) | copy-start | bytes 2752516
  7.2 19.9 %copy-start.1 = (bf16[512,896]{1,0:T(8,128)(2,1)S(1)}, bf16[512,896]{1,0:T(8,128)(2,1)}, u32[]{:S(2)}) copy-start(bf16[512,896]{1,0:T(8,128)(2,1)} %key_ref.3) | copy-start | bytes 2752516
  7.2 107.0 %reduce-scatter.2.cloned.1.call-start = ((), (), s32[]{:S(2)}) async-start(), calls=%async_computation.1 | async-start | bytes 4128768 | tf_op jit(solution)/shard_map/reduce_scatter | solution.py:326
  20.0 10.4 %collective-permute-start = (bf16[200,896]{1,0:T(8,128)(2,1)}, bf16[200,896]{1,0:T(8,128)(2,1)}, u32[]{:S(2)}, u32[]{:S(2)}) collective-permute-start(bf16[200,896]{1,0:T(8,128)(2,1)} %fusion.26), channel_id=1, source_target_pairs={{0,8},{8,16},{16,24},{24,32},{32,40},{40,48},{48,56},{56,64},{64,7... | collective-permute-start | bytes 1075208 | tf_op jit(solution)/shard_map/ppermute | solution.py:23
  22.5 10.1 %collective-permute-start.1 = (bf16[200,896]{1,0:T(8,128)(2,1)}, bf16[200,896]{1,0:T(8,128)(2,1)}, u32[]{:S(2)}, u32[]{:S(2)}) collective-permute-start(bf16[200,896]{1,0:T(8,128)(2,1)} %fusion.27), channel_id=1, source_target_pairs={{0,248},{8,0},{16,8},{24,16},{32,24},{40,32},{48,40},{56,48},{64,5... | collective-permute-start | bytes 1075208 | tf_op jit(solution)/shard_map/ppermute | solution.py:23
  41.3 13.4 %collective-permute-start.2 = (bf16[192,1024]{1,0:T(8,128)(2,1)}, bf16[192,1024]{1,0:T(8,128)(2,1)S(1)}, u32[]{:S(2)}, u32[]{:S(2)}) collective-permute-start(bf16[192,1024]{1,0:T(8,128)(2,1)} %get-tuple-element.43), channel_id=1, source_target_pairs={{0,248},{8,0},{16,8},{24,16},{32,24},{40,32},{48,40},{56,48},{64,5... | collective-permute-start | bytes 1179656 | tf_op jit(solution)/shard_map/ppermute | solution.py:23
  46.3 14.0 %collective-permute-start.3 = (bf16[192,1024]{1,0:T(8,128)(2,1)}, bf16[192,1024]{1,0:T(8,128)(2,1)S(1)}, u32[]{:S(2)}, u32[]{:S(2)}) collective-permute-start(bf16[192,1024]{1,0:T(8,128)(2,1)} %get-tuple-element.44), channel_id=1, source_target_pairs={{0,8},{8,16},{16,24},{24,32},{32,40},{40,48},{48,56},{56,64},{64,7... | collective-permute-start | bytes 1179656 | tf_op jit(solution)/shard_map/ppermute | solution.py:23
  47.8 0.9 copy-start.5
  54.8 5.8 %copy-start = (f32[512,128]{1,0:T(8,128)S(1)}, f32[512,128]{1,0:T(8,128)}, u32[]{:S(2)}) copy-start(f32[512,128]{1,0:T(8,128)} %get-tuple-element.42) | copy-start | bytes 786436
  54.8 6.2 %copy-start.3 = (bf16[192,1024]{1,0:T(8,128)(2,1)}, bf16[192,1024]{1,0:T(8,128)(2,1)S(1)}, u32[]{:S(2)}) copy-start(bf16[192,1024]{1,0:T(8,128)(2,1)S(1)} %collective-permute-done.2) | copy-start | bytes 1179652
  60.3 0.7 copy-start.4
  61.0 1.8 %copy-start.7 = (pred[896]{0:T(1024)(128)(4,1)S(1)}, pred[896]{0:T(1024)(128)(4,1)}, u32[]{:S(2)}) copy-start(pred[896]{0:T(1024)(128)(4,1)} %get-tuple-element.94) | copy-start | bytes 2692
  61.0 1.8 %copy-start.8 = (pred[896]{0:T(1024)(128)(4,1)S(1)}, pred[896]{0:T(1024)(128)(4,1)}, u32[]{:S(2)}) copy-start(pred[896]{0:T(1024)(128)(4,1)} %get-tuple-element.91) | copy-start | bytes 2692
  61.0 1.8 %copy-start.9 = (pred[896]{0:T(1024)(128)(4,1)S(1)}, pred[896]{0:T(1024)(128)(4,1)}, u32[]{:S(2)}) copy-start(pred[896]{0:T(1024)(128)(4,1)} %get-tuple-element.92) | copy-start | bytes 2692
  61.0 1.8 %copy-start.10 = (f32[512,896]{1,0:T(8,128)S(1)}, f32[512,896]{1,0:T(8,128)}, u32[]{:S(2)}) copy-start(f32[512,896]{1,0:T(8,128)} %get-tuple-element.41) | copy-start | bytes 5505028
  61.1 1.8 %slice-start = ((bf16[192,1024]{1,0:T(8,128)(2,1)}), bf16[192,896]{1,0:T(8,128)(2,1)S(1)}, s32[]{:S(2)}) async-start(bf16[192,1024]{1,0:T(8,128)(2,1)} %copy-done.3), calls=%async_computation.2 | async-start | bytes 688128 | tf_op jit(solution)/shard_map/slice | solution.py:281
  61.1 1.8 %slice-start.1 = ((bf16[192,1024]{1,0:T(8,128)(2,1)}), bf16[192,896]{1,0:T(8,128)(2,1)S(1)}, s32[]{:S(2)}) async-start(bf16[192,1024]{1,0:T(8,128)(2,1)} %copy-done.4), calls=%async_computation.3 | async-start | bytes 688128 | tf_op jit(solution)/shard_map/slice | solution.py:281
  73.4 18.5 %collective-permute-start.4 = (bf16[2,192,896]{2,1,0:T(8,128)(2,1)S(1)}, bf16[2,192,896]{2,1,0:T(8,128)(2,1)S(1)}, u32[]{:S(2)}, u32[]{:S(2)}) collective-permute-start(bf16[2,192,896]{2,1,0:T(8,128)(2,1)S(1)} %get-tuple-element.47), channel_id=1, source_target_pairs={{0,8},{8,16},{16,24},{24,32},{32,40},{40,48},{48,56},{56,64},{64,7... | collective-permute-start | bytes 2064392 | tf_op jit(solution)/shard_map/ppermute | solution.py:23
  73.5 18.5 %collective-permute-start.5 = (bf16[2,192,896]{2,1,0:T(8,128)(2,1)S(1)}, bf16[2,192,896]{2,1,0:T(8,128)(2,1)S(1)}, u32[]{:S(2)}, u32[]{:S(2)}) collective-permute-start(bf16[2,192,896]{2,1,0:T(8,128)(2,1)S(1)} %get-tuple-element.48), channel_id=1, source_target_pairs={{0,248},{8,0},{16,8},{24,16},{32,24},{40,32},{48,40},{56,48},{64,5... | collective-permute-start | bytes 2064392 | tf_op jit(solution)/shard_map/ppermute | solution.py:23
Sparse Core Ops, SparseCore 0:
  73.5 40.6 reduce-scatter.1

commit v14 on v13

--- a/solution.py
+++ b/solution.py
@@ -253,8 +253,7 @@
     from_right = shifted(query_bundle(left_start, jnp.logical_not(first_right)), "req", -1)
 
     served = serve_slots(from_left, from_right, cache_keys, cache_values, head_count)
-    held_ends, served = lax.optimization_barrier((req_ends, served))
-    segment = jnp.sum((positions[:, None] >= held_ends[None, :]).astype(jnp.int32), axis=1)
+    segment = jnp.sum((positions[:, None] >= req_ends[None, :]).astype(jnp.int32), axis=1)
     own_numer, own_top, own_total = attend_own(queries, keys_new, values_new, segment, head_count)
 
     back_left, back_right = served

time: 122 us -> 120 us (0.984)
  other arithmetic: 7.44 us -> 3.64 us
  starting transfers between devices: 12.4 us -> 14.2 us
  local copies, waits for them, and re-layouts: 9.75 us -> 11.2 us
    ppermute x6, starting transfers between devices: 12.4 us -> 14.2 us  [shifted(): return lax.ppermute(value, axis, pairs)]
    concatenate x2, other arithmetic: 1.53 us -> 0.06 us  [query_bundle(): return jnp.concatenate([rows_of(queries, start), tag_rows], axis=0)]
    unnamed x22 -> x20, local copies, waits for them, and re-layouts: 0.1 us -> 1.53 us
  transfers between devices with their start and end apart: 7 -> 7, of which waited for: 5 -> 4; matrix products, arithmetic and copies ran while one was open for 8% -> 5% of each run, Pallas kernels for 5% -> 5%
where the time goes in v14:
time: 120 us
  waiting for transfers between devices  37.6 us (31%)
  between operations  28 us (23%)
  Pallas kernels  14.8 us (12%)
  starting transfers between devices  14.2 us (12%)
  local copies, waits for them, and re-layouts  11.2 us (9%)
  matrix products  10.5 us (9%)
  other arithmetic  3.64 us (3%)
    reduce_scatter x1, waiting for transfers between devices, body(): lax.psum_scatter(jnp.dot(attended, out_proj, preferred_element_type=jnp.f...  20.9 us
    ppermute x6, waiting for transfers between devices, shifted(): return lax.ppermute(value, axis, pairs)  16.7 us
    ppermute x6, starting transfers between devices, shifted(): return lax.ppermute(value, axis, pairs)  14.2 us
    dot_general x1, matrix products, body(): jnp.dot(attended, out_proj, preferred_element_type=jnp.float32)  10.5 us
    pallas_call x1, Pallas kernels, serve_slots(): pl.pallas_call(functools.partial(prior_kernel, head_count), out_shape=(ja...  8.74 us
    pallas_call x1, Pallas kernels, attend_own(): pl.pallas_call(functools.partial(own_kernel, head_count), out_shape=(jax....  6.09 us
    slice x2, local copies, waits for them, and re-layouts, slot_id(): bundle[NEWCAP, 2]  2.89 us
  transfers between devices with their start and end apart: 7, of which 4 were waited for; matrix products, arithmetic and copies ran while one was open for 5% of the time, Pallas kernels for 5%

profile of v14, /device:TPU:8, one launch (start us, length us, event | category | flops | bytes accessed | tf_op | source)
XLA Modules:
  0.0 120.0 jit_solution(9415374954505786326)
XLA Ops:
  7.2 1.3 %fusion.50 = (s32[1,1]{1,0:T(1,128)}, s32[1,1]{1,0:T(1,128)}) fusion(s32[1,2]{1,0:T(1,128)} %param.23), kind=kLoop, calls=%fused_computation.103 | loop fusion | bytes 16 | tf_op jit(solution)/shard_map/slice | solution.py:240
  14.4 1.3 %fusion.51 = (s32[1,1]{1,0:T(1,128)}, s32[1,1]{1,0:T(1,128)}) fusion(s32[1,4]{1,0:T(1,128)} %param.20), kind=kLoop, calls=%fused_computation.104 | loop fusion | bytes 16 | tf_op jit(solution)/shard_map/slice | solution.py:228
  17.0 0.7 convert.31
  17.7 1.3 %constant_dynamic-slice_fusion = (bf16[192,896]{1,0:T(8,128)(2,1)S(1)}, bf16[192,896]{1,0:T(8,128)(2,1)S(1)}) fusion(bf16[512,896]{1,0:T(8,128)(2,1)} %query_ref.1, s32[]{:T(128)S(6)} %select_n.201, s32[]{:T(128)S(6)} %select_n.196), kind=kLoop, calls=%fused_computation.80 | loop fusion | bytes 1376264 | tf_op jit(solution)/shard_map/dynamic_slice | solution.py:234
  19.1 1.7 %collective-permute-start = (bf16[200,896]{1,0:T(8,128)(2,1)S(1)}, bf16[200,896]{1,0:T(8,128)(2,1)S(1)}, u32[]{:S(2)}, u32[]{:S(2)}) collective-permute-start(bf16[200,896]{1,0:T(8,128)(2,1)S(1)} %fusion.26), channel_id=1, source_target_pairs={{0,8},{8,16},{16,24},{24,32},{32,40},{40,48},{48,56},{56,64},{64,7... | collective-permute-start | bytes 1075208 | tf_op jit(solution)/shard_map/ppermute | solution.py:23
  20.9 0.7 collective-permute-start.1
  24.5 0.9 copy.14.seg_col_ref
  25.4 6.1 %shard_map.121 = (f32[512,896]{1,0:T(8,128)}, f32[512,128]{1,0:T(8,128)}) custom-call(bf16[512,896]{1,0:T(8,128)(2,1)} %query_ref.1, bf16[512,896]{1,0:T(8,128)(2,1)} %key_ref.2, bf16[512,896]{1,0:T(8,128)(2,1)} %value_ref.2, s32[512,1]{1,0:T(8,128)} %copy.14.seg_col_ref, s32[1,512]{1,0:T(1,128)} %bitcast.38), custom_call_target="tpu_custom_call" | custom-call | flops 1342177280 | bytes 4849664 | tf_op jit(solution)/shard_map/pallas_call | solution.py:181
  31.5 0.7 copy-done.5
  32.2 0.7 copy-done.6
  33.0 8.7 %shard_map.122 = (bf16[192,1024]{1,0:T(8,128)(2,1)}, bf16[192,1024]{1,0:T(8,128)(2,1)}) custom-call(bf16[200,896]{1,0:T(8,128)(2,1)} %copy-done.5, bf16[200,896]{1,0:T(8,128)(2,1)} %copy-done.6, bf16[2,1024,896]{2,1,0:T(8,128)(2,1)} %key_ref.3, bf16[2,1024,896]{2,1,0:T(8,128)(2,1)} %value_ref.3), custom_call_target="tpu_custom_call" | custom-call | flops 2013265920 | bytes 8843264 | tf_op jit(solution)/shard_map/pallas_call | solution.py:121
  41.7 6.6 %collective-permute-start.2 = (bf16[192,1024]{1,0:T(8,128)(2,1)}, bf16[192,1024]{1,0:T(8,128)(2,1)S(1)}, u32[]{:S(2)}, u32[]{:S(2)}) collective-permute-start(bf16[192,1024]{1,0:T(8,128)(2,1)} %get-tuple-element.37), channel_id=1, source_target_pairs={{0,248},{8,0},{16,8},{24,16},{32,24},{40,32},{48,40},{56,48},{64,5... | collective-permute-start | bytes 1179656 | tf_op jit(solution)/shard_map/ppermute | solution.py:23
  49.0 7.7 %collective-permute-done.2 = bf16[192,1024]{1,0:T(8,128)(2,1)S(1)} collective-permute-done((bf16[192,1024]{1,0:T(8,128)(2,1)}, bf16[192,1024]{1,0:T(8,128)(2,1)S(1)}, u32[]{:S(2)}, u32[]{:S(2)}) %collective-permute-start.2) | collective-permute-done | bytes 393248 | tf_op jit(solution)/shard_map/ppermute | solution.py:23
  56.7 2.6 %collective-permute-done.3 = bf16[192,1024]{1,0:T(8,128)(2,1)S(1)} collective-permute-done((bf16[192,1024]{1,0:T(8,128)(2,1)}, bf16[192,1024]{1,0:T(8,128)(2,1)S(1)}, u32[]{:S(2)}, u32[]{:S(2)}) %collective-permute-start.3) | collective-permute-done | bytes 393248 | tf_op jit(solution)/shard_map/ppermute | solution.py:23
  60.0 0.6 slice_reduce_fusion.3
  60.6 0.6 slice_reduce_fusion.11
  61.1 0.6 slice_reduce_fusion.7
  61.8 10.5 %convolution_convert_fusion = bf16[512,3584]{1,0:T(8,128)(2,1)} fusion(bf16[896,3584]{1,0:T(8,128)(2,1)} %param.19, f32[512,896]{1,0:T(8,128)S(1)} %copy-done.9, s32[]{:T(128)S(6)} %select_n.208, bf16[192,896]{1,0:T(8,128)(2,1)S(1)} %slice-done, s32[]{:T(128)S(6)} %select_n.209, bf16[192,896]{1,0:T(8,128)(2,1)S(1)} %slice-done.1, ...), kind=kOutput, calls=%fused_computation | convolution fusion | flops 3299344384 | bytes 12644872 | tf_op jit(solution)/shard_map/dot_general | solution.py:326
  72.4 5.1 %collective-permute-start.5 = (bf16[2,192,896]{2,1,0:T(8,128)(2,1)S(1)}, bf16[2,192,896]{2,1,0:T(8,128)(2,1)S(1)}, u32[]{:S(2)}, u32[]{:S(2)}) collective-permute-start(bf16[2,192,896]{2,1,0:T(8,128)(2,1)S(1)} %get-tuple-element.42), channel_id=1, source_target_pairs={{0,248},{8,0},{16,8},{24,16},{32,24},{40,32},{48,40},{56,48},{64,5... | collective-permute-start | bytes 2064392 | tf_op jit(solution)/shard_map/ppermute | solution.py:23
  77.5 1.4 %fusion.48 = (bf16[1,1]{1,0:T(2,128)(2,1)}, bf16[1,1]{1,0:T(2,128)(2,1)}, bf16[1,1]{1,0:T(2,128)(2,1)}) fusion(bf16[200,896]{1,0:T(8,128)(2,1)} %copy-done.5), kind=kLoop, calls=%fused_computation.101 | loop fusion | bytes 12 | tf_op jit(solution)/shard_map/slice | solution.py:334
  80.9 1.4 %fusion.49 = (bf16[1,1]{1,0:T(2,128)(2,1)}, bf16[1,1]{1,0:T(2,128)(2,1)}, bf16[1,1]{1,0:T(2,128)(2,1)}) fusion(bf16[200,896]{1,0:T(8,128)(2,1)} %copy-done.6), kind=kLoop, calls=%fused_computation.102 | loop fusion | bytes 12 | tf_op jit(solution)/shard_map/slice | solution.py:334
  84.4 6.4 %collective-permute-done.4 = bf16[2,192,896]{2,1,0:T(8,128)(2,1)S(1)} collective-permute-done((bf16[2,192,896]{2,1,0:T(8,128)(2,1)S(1)}, bf16[2,192,896]{2,1,0:T(8,128)(2,1)S(1)}, u32[]{:S(2)}, u32[]{:S(2)}) %collective-permute-start.4) | collective-permute-done | bytes 688160 | tf_op jit(solution)/shard_map/ppermute | solution.py:23
  90.9 1.3 %select_select_fusion = (bf16[2,192,896]{2,1,0:T(8,128)(2,1)}, bf16[2,192,896]{2,1,0:T(8,128)(2,1)}) fusion(pred[2]{0:T(512)(128)(4,1)S(1)} %get-tuple-element.91, pred[2]{0:T(512)(128)(4,1)S(1)} %get-tuple-element.92, bf16[192,896]{1,0:T(8,128)(2,1)S(1)} %get-tuple-element.69, bf16[192,896]{1,0:T(8,128)(2,1)S(1)} %get-tuple-element.67, ...), kind=kLoop, calls=%fused_computation.30 | loop fusion | flops 1376256 | bytes 2752516 | tf_op jit(solution)/shard_map/jit(_where)/select_n | solution.py:342
  92.2 20.9 %reduce-scatter.2.cloned.1.call-done = bf16[64,3584]{1,0:T(8,128)(2,1)} async-done(((bf16[512,3584]{1,0:T(8,128)(2,1)}), bf16[64,3584]{1,0:T(8,128)(2,1)}) %reduce-scatter.2.cloned.1.call-update) | async-done | bytes 458768 | tf_op jit(solution)/shard_map/reduce_scatter | solution.py:325
  (50 shorter events, 2.2 us)
Async XLA Ops:
  7.2 17.0 %copy-start.8 = (s32[1,4]{1,0:T(1,128)S(1)}, s32[1,4]{1,0:T(1,128)}, u32[]{:S(2)}) copy-start(s32[1,4]{1,0:T(1,128)} %param.20) | copy-start | bytes 52
  7.2 105.9 %reduce-scatter.2.cloned.1.call-start = ((), (), s32[]{:S(2)}) async-start(), calls=%async_computation.1 | async-start | bytes 4128768 | tf_op jit(solution)/shard_map/reduce_scatter | solution.py:325
  19.1 12.4 %collective-permute-start = (bf16[200,896]{1,0:T(8,128)(2,1)S(1)}, bf16[200,896]{1,0:T(8,128)(2,1)S(1)}, u32[]{:S(2)}, u32[]{:S(2)}) collective-permute-start(bf16[200,896]{1,0:T(8,128)(2,1)S(1)} %fusion.26), channel_id=1, source_target_pairs={{0,8},{8,16},{16,24},{24,32},{32,40},{40,48},{48,56},{56,64},{64,7... | collective-permute-start | bytes 1075208 | tf_op jit(solution)/shard_map/ppermute | solution.py:23
  20.9 10.6 %collective-permute-start.1 = (bf16[200,896]{1,0:T(8,128)(2,1)S(1)}, bf16[200,896]{1,0:T(8,128)(2,1)S(1)}, u32[]{:S(2)}, u32[]{:S(2)}) collective-permute-start(bf16[200,896]{1,0:T(8,128)(2,1)S(1)} %fusion.27), channel_id=1, source_target_pairs={{0,248},{8,0},{16,8},{24,16},{32,24},{40,32},{48,40},{56,48},{64,5... | collective-permute-start | bytes 1075208 | tf_op jit(solution)/shard_map/ppermute | solution.py:23
  24.5 0.9 copy-start.7
  31.5 16.8 %copy-start.1 = (bf16[512,896]{1,0:T(8,128)(2,1)S(1)}, bf16[512,896]{1,0:T(8,128)(2,1)}, u32[]{:S(2)}) copy-start(bf16[512,896]{1,0:T(8,128)(2,1)} %key_ref.2) | copy-start | bytes 2752516
  31.5 16.8 %copy-start.2 = (bf16[512,896]{1,0:T(8,128)(2,1)S(1)}, bf16[512,896]{1,0:T(8,128)(2,1)}, u32[]{:S(2)}) copy-start(bf16[512,896]{1,0:T(8,128)(2,1)} %value_ref.2) | copy-start | bytes 2752516
  31.5 0.7 copy-start.5
  32.2 0.7 copy-start.6
  41.7 15.0 %collective-permute-start.2 = (bf16[192,1024]{1,0:T(8,128)(2,1)}, bf16[192,1024]{1,0:T(8,128)(2,1)S(1)}, u32[]{:S(2)}, u32[]{:S(2)}) collective-permute-start(bf16[192,1024]{1,0:T(8,128)(2,1)} %get-tuple-element.37), channel_id=1, source_target_pairs={{0,248},{8,0},{16,8},{24,16},{32,24},{40,32},{48,40},{56,48},{64,5... | collective-permute-start | bytes 1179656 | tf_op jit(solution)/shard_map/ppermute | solution.py:23
  48.3 11.0 %collective-permute-start.3 = (bf16[192,1024]{1,0:T(8,128)(2,1)}, bf16[192,1024]{1,0:T(8,128)(2,1)S(1)}, u32[]{:S(2)}, u32[]{:S(2)}) collective-permute-start(bf16[192,1024]{1,0:T(8,128)(2,1)} %get-tuple-element.38), channel_id=1, source_target_pairs={{0,8},{8,16},{16,24},{24,32},{32,40},{40,48},{48,56},{56,64},{64,7... | collective-permute-start | bytes 1179656 | tf_op jit(solution)/shard_map/ppermute | solution.py:23
  49.0 10.6 %copy-start = (f32[512,128]{1,0:T(8,128)S(1)}, f32[512,128]{1,0:T(8,128)}, u32[]{:S(2)}) copy-start(f32[512,128]{1,0:T(8,128)} %get-tuple-element.36) | copy-start | bytes 786436
  56.7 3.2 %copy-start.3 = (bf16[192,1024]{1,0:T(8,128)(2,1)}, bf16[192,1024]{1,0:T(8,128)(2,1)S(1)}, u32[]{:S(2)}) copy-start(bf16[192,1024]{1,0:T(8,128)(2,1)S(1)} %collective-permute-done.2) | copy-start | bytes 1179652
  59.2 0.7 copy-start.4
  60.0 1.7 %copy-start.9 = (f32[512,896]{1,0:T(8,128)S(1)}, f32[512,896]{1,0:T(8,128)}, u32[]{:S(2)}) copy-start(f32[512,896]{1,0:T(8,128)} %get-tuple-element.35) | copy-start | bytes 5505028
  60.0 1.7 %slice-start = ((bf16[192,1024]{1,0:T(8,128)(2,1)}), bf16[192,896]{1,0:T(8,128)(2,1)S(1)}, s32[]{:S(2)}) async-start(bf16[192,1024]{1,0:T(8,128)(2,1)} %copy-done.3), calls=%async_computation.2 | async-start | bytes 688128 | tf_op jit(solution)/shard_map/slice | solution.py:280
  60.0 1.8 %slice-start.1 = ((bf16[192,1024]{1,0:T(8,128)(2,1)}), bf16[192,896]{1,0:T(8,128)(2,1)S(1)}, s32[]{:S(2)}) async-start(bf16[192,1024]{1,0:T(8,128)(2,1)} %copy-done.4), calls=%async_computation.3 | async-start | bytes 688128 | tf_op jit(solution)/shard_map/slice | solution.py:280
  72.3 18.5 %collective-permute-start.4 = (bf16[2,192,896]{2,1,0:T(8,128)(2,1)S(1)}, bf16[2,192,896]{2,1,0:T(8,128)(2,1)S(1)}, u32[]{:S(2)}, u32[]{:S(2)}) collective-permute-start(bf16[2,192,896]{2,1,0:T(8,128)(2,1)S(1)} %get-tuple-element.41), channel_id=1, source_target_pairs={{0,8},{8,16},{16,24},{24,32},{32,40},{40,48},{48,56},{56,64},{64,7... | collective-permute-start | bytes 2064392 | tf_op jit(solution)/shard_map/ppermute | solution.py:23
  72.4 18.5 %collective-permute-start.5 = (bf16[2,192,896]{2,1,0:T(8,128)(2,1)S(1)}, bf16[2,192,896]{2,1,0:T(8,128)(2,1)S(1)}, u32[]{:S(2)}, u32[]{:S(2)}) collective-permute-start(bf16[2,192,896]{2,1,0:T(8,128)(2,1)S(1)} %get-tuple-element.42), channel_id=1, source_target_pairs={{0,248},{8,0},{16,8},{24,16},{32,24},{40,32},{48,40},{56,48},{64,5... | collective-permute-start | bytes 2064392 | tf_op jit(solution)/shard_map/ppermute | solution.py:23
Sparse Core Ops, SparseCore 0:
  72.4 40.6 reduce-scatter.1

commit v15 on v14

--- a/solution.py
+++ b/solution.py
@@ -322,8 +322,18 @@
 
     numerator = own_numer * widened(own_scale) + prior_scaled * widened(prior_scale)
     attended = (numerator / widened(denominator)).astype(jnp.bfloat16)
+    head_rows = 2 * NEWCAP
+    late_attended = (
+        own_numer[head_rows:] / widened(own_total)[head_rows:]
+    ).astype(jnp.bfloat16)
     mixed = lax.psum_scatter(
-        jnp.dot(attended, out_proj, preferred_element_type=jnp.float32).astype(jnp.bfloat16),
+        jnp.concatenate(
+            [
+                jnp.dot(attended[:head_rows], out_proj, preferred_element_type=jnp.float32),
+                jnp.dot(late_attended, out_proj, preferred_element_type=jnp.float32),
+            ],
+            axis=0,
+        ).astype(jnp.bfloat16),
         "tp",
         scatter_dimension=0,
         tiled=True,

time: 120 us -> 125 us (1.042)
  other arithmetic: 3.64 us -> 6.42 us
  local copies, waits for them, and re-layouts: 11.2 us -> 13.8 us
    reduce_scatter x1, waiting for transfers between devices: 20.9 us -> 18.4 us  [body(): lax.psum_scatter(jnp.concatenate([jnp.dot(attended[:head_rows], out_proj,...]
    concatenate x0 -> x1, other arithmetic: none -> 2.03 us  [body(): jnp.concatenate([jnp.dot(attended[:head_rows], out_proj, preferred_elemen...]
    slice x3 -> x4, local copies, waits for them, and re-layouts: 1.73 us -> 3.76 us  [widened(): full = jnp.where(lane_head == h, per_head[:, h:h + 1], full)]
    ppermute x6, waiting for transfers between devices: 16.7 us -> 18.1 us  [shifted(): return lax.ppermute(value, axis, pairs)]
    dot_general x1 -> x2, matrix products: 10.5 us -> 11.5 us  [the longest x1 7.27 us: body(): jnp.dot(attended[:head_rows], out_proj, preferred_element_type=jnp.float32)]
  transfers between devices with their start and end apart: 7 -> 7, of which waited for: 4 -> 5; matrix products, arithmetic and copies ran while one was open for 5% -> 10% of each run, Pallas kernels for 5% -> 5%
where the time goes in v15:
time: 125 us
  waiting for transfers between devices  36.5 us (29%)
  between operations  28.2 us (23%)
  Pallas kernels  15 us (12%)
  local copies, waits for them, and re-layouts  13.8 us (11%)
  starting transfers between devices  13.1 us (10%)
  matrix products  11.5 us (9%)
  other arithmetic  6.42 us (5%)
    reduce_scatter x1, waiting for transfers between devices, body(): lax.psum_scatter(jnp.concatenate([jnp.dot(attended[:head_rows], out_proj,...  18.4 us
    ppermute x6, waiting for transfers between devices, shifted(): return lax.ppermute(value, axis, pairs)  18.1 us
    ppermute x6, starting transfers between devices, shifted(): return lax.ppermute(value, axis, pairs)  13 us
    pallas_call x1, Pallas kernels, serve_slots(): pl.pallas_call(functools.partial(prior_kernel, head_count), out_shape=(ja...  8.74 us
    dot_general x1, matrix products, body(): jnp.dot(attended[:head_rows], out_proj, preferred_element_type=jnp.float32)  7.27 us
    pallas_call x1, Pallas kernels, attend_own(): pl.pallas_call(functools.partial(own_kernel, head_count), out_shape=(jax....  6.22 us
    dot_general x1, matrix products, body(): jnp.dot(late_attended, out_proj, preferred_element_type=jnp.float32)  4.22 us
    slice x4, local copies, waits for them, and re-layouts, widened(): full = jnp.where(lane_head == h, per_head[:, h:h + 1], full)  3.76 us
  transfers between devices with their start and end apart: 7, of which 5 were waited for; matrix products, arithmetic and copies ran while one was open for 10% of the time, Pallas kernels for 5%

profile of v15, /device:TPU:8, one launch (start us, length us, event | category | flops | bytes accessed | tf_op | source)
XLA Modules:
  0.0 124.5 jit_solution(2926356560269708414)
XLA Ops:
  7.2 1.3 %fusion.62 = (s32[1,1]{1,0:T(1,128)}, s32[1,1]{1,0:T(1,128)}) fusion(s32[1,4]{1,0:T(1,128)} %param.20), kind=kLoop, calls=%fused_computation.126 | loop fusion | bytes 16 | tf_op jit(solution)/shard_map/slice | solution.py:228
  10.5 1.3 %fusion.61 = (s32[1,1]{1,0:T(1,128)}, s32[1,1]{1,0:T(1,128)}) fusion(s32[1,2]{1,0:T(1,128)} %param.23), kind=kLoop, calls=%fused_computation.125 | loop fusion | bytes 16 | tf_op jit(solution)/shard_map/slice | solution.py:240
  17.3 0.7 convert.37
  17.9 1.3 %constant_dynamic-slice_fusion = (bf16[192,896]{1,0:T(8,128)(2,1)S(1)}, bf16[192,896]{1,0:T(8,128)(2,1)S(1)}) fusion(bf16[512,896]{1,0:T(8,128)(2,1)} %query_ref.1, s32[]{:T(128)S(6)} %select_n.221, s32[]{:T(128)S(6)} %select_n.216), kind=kLoop, calls=%fused_computation.101 | loop fusion | bytes 1376264 | tf_op jit(solution)/shard_map/dynamic_slice | solution.py:234
  19.3 2.3 %collective-permute-start.1 = (bf16[200,896]{1,0:T(8,128)(2,1)S(1)}, bf16[200,896]{1,0:T(8,128)(2,1)S(1)}, u32[]{:S(2)}, u32[]{:S(2)}) collective-permute-start(bf16[200,896]{1,0:T(8,128)(2,1)S(1)} %fusion.28), channel_id=1, source_target_pairs={{0,248},{8,0},{16,8},{24,16},{32,24},{40,32},{48,40},{56,48},{64,5... | collective-permute-start | bytes 1075208 | tf_op jit(solution)/shard_map/ppermute | solution.py:23
  24.8 0.9 copy.14.seg_col_ref
  25.6 6.2 %shard_map.121 = (f32[512,896]{1,0:T(8,128)}, f32[512,128]{1,0:T(8,128)}) custom-call(bf16[512,896]{1,0:T(8,128)(2,1)} %query_ref.1, bf16[512,896]{1,0:T(8,128)(2,1)} %key_ref.2, bf16[512,896]{1,0:T(8,128)(2,1)} %value_ref.2, s32[512,1]{1,0:T(8,128)} %copy.14.seg_col_ref, s32[1,512]{1,0:T(1,128)} %bitcast.48), custom_call_target="tpu_custom_call" | custom-call | flops 1342177280 | bytes 4849664 | tf_op jit(solution)/shard_map/pallas_call | solution.py:181
  31.8 2.0 %slice_reduce_fusion.12 = (f32[512]{0:T(512)S(1)}, f32[512]{0:T(512)S(1)}, f32[512]{0:T(512)S(1)}, f32[512]{0:T(512)S(1)}) fusion(f32[512,128]{1,0:T(8,128)} %get-tuple-element.36), kind=kLoop, calls=%fused_computation.71 | loop fusion | bytes 16384 | tf_op jit(solution)/shard_map/slice | solution.py:320
  34.6 1.8 %collective-permute-done.left_ref = bf16[200,896]{1,0:T(8,128)(2,1)S(1)} collective-permute-done((bf16[200,896]{1,0:T(8,128)(2,1)S(1)}, bf16[200,896]{1,0:T(8,128)(2,1)S(1)}, u32[]{:S(2)}, u32[]{:S(2)}) %collective-permute-start) | collective-permute-done | bytes 358432 | tf_op jit(solution)/shard_map/ppermute | solution.py:23
  36.5 0.7 copy-done.6
  37.2 8.7 %shard_map.122 = (bf16[192,1024]{1,0:T(8,128)(2,1)}, bf16[192,1024]{1,0:T(8,128)(2,1)}) custom-call(bf16[200,896]{1,0:T(8,128)(2,1)} %copy-done.6, bf16[200,896]{1,0:T(8,128)(2,1)} %copy-done.5, bf16[2,1024,896]{2,1,0:T(8,128)(2,1)} %key_ref.3, bf16[2,1024,896]{2,1,0:T(8,128)(2,1)} %value_ref.3), custom_call_target="tpu_custom_call" | custom-call | flops 2013265920 | bytes 8843264 | tf_op jit(solution)/shard_map/pallas_call | solution.py:121
  45.9 5.5 %collective-permute-start.2 = (bf16[192,1024]{1,0:T(8,128)(2,1)}, bf16[192,1024]{1,0:T(8,128)(2,1)S(1)}, u32[]{:S(2)}, u32[]{:S(2)}) collective-permute-start(bf16[192,1024]{1,0:T(8,128)(2,1)} %get-tuple-element.37), channel_id=1, source_target_pairs={{0,248},{8,0},{16,8},{24,16},{32,24},{40,32},{48,40},{56,48},{64,5... | collective-permute-start | bytes 1179656 | tf_op jit(solution)/shard_map/ppermute | solution.py:23
  51.4 4.2 %convolution_convert_fusion.1 = bf16[128,3584]{1,0:T(8,128)(2,1)S(1)} fusion(bf16[896,3584]{1,0:T(8,128)(2,1)} %param.19, f32[512,896]{1,0:T(8,128)} %get-tuple-element.35, f32[128]{0:T(128)S(1)} %slice.266, f32[128]{0:T(128)S(1)} %slice.265, f32[128]{0:T(128)S(1)} %slice.264, f32[128]{0:T(128)S(1)} %slice.263, pred[896]{0:T(1024)(128)(4,1)S(1)} %get-tuple-element.92, ...), kind=kOutput, calls=%fused_computation.1 | convolution fusion | flops 823230464 | bytes 7804416 | tf_op jit(solution)/shard_map/dot_general | solution.py:333
  55.7 4.2 %collective-permute-done.2 = bf16[192,1024]{1,0:T(8,128)(2,1)S(1)} collective-permute-done((bf16[192,1024]{1,0:T(8,128)(2,1)}, bf16[192,1024]{1,0:T(8,128)(2,1)S(1)}, u32[]{:S(2)}, u32[]{:S(2)}) %collective-permute-start.2) | collective-permute-done | bytes 393248 | tf_op jit(solution)/shard_map/ppermute | solution.py:23
  59.8 5.4 %collective-permute-done.3 = bf16[192,1024]{1,0:T(8,128)(2,1)S(1)} collective-permute-done((bf16[192,1024]{1,0:T(8,128)(2,1)}, bf16[192,1024]{1,0:T(8,128)(2,1)S(1)}, u32[]{:S(2)}, u32[]{:S(2)}) %collective-permute-start.3) | collective-permute-done | bytes 393248 | tf_op jit(solution)/shard_map/ppermute | solution.py:23
  69.1 0.6 copy-done.9
  69.7 7.3 %convolution_convert_fusion = bf16[384,3584]{1,0:T(8,128)(2,1)S(1)} fusion(bf16[896,3584]{1,0:T(8,128)(2,1)} %param.19, f32[512,896]{1,0:T(8,128)S(1)} %get-tuple-element.82, f32[512,896]{1,0:T(8,128)S(1)} %get-tuple-element.81, f32[512,896]{1,0:T(8,128)S(1)} %copy-done.9, s32[]{:T(128)S(6)} %select_n.228, bf16[192,896]{1,0:T(8,128)(2,1)S(1)} %slice-done.1, ...), kind=kOutput, calls=%fused_computation | convolution fusion | flops 2472787968 | bytes 14356996 | tf_op jit(solution)/shard_map/dot_general | solution.py:332
  77.0 2.0 %pad_maximum_fusion = bf16[512,3584]{1,0:T(8,128)(2,1)} fusion(bf16[128,3584]{1,0:T(8,128)(2,1)S(1)} %convolution_convert_fusion.1, bf16[384,3584]{1,0:T(8,128)(2,1)S(1)} %convolution_convert_fusion), kind=kLoop, calls=%fused_computation.2 | loop fusion | flops 7340032 | bytes 7340032 | tf_op jit(solution)/shard_map/concatenate | solution.py:330
  79.1 5.1 %collective-permute-start.5 = (bf16[2,192,896]{2,1,0:T(8,128)(2,1)S(1)}, bf16[2,192,896]{2,1,0:T(8,128)(2,1)S(1)}, u32[]{:S(2)}, u32[]{:S(2)}) collective-permute-start(bf16[2,192,896]{2,1,0:T(8,128)(2,1)S(1)} %get-tuple-element.42), channel_id=1, source_target_pairs={{0,248},{8,0},{16,8},{24,16},{32,24},{40,32},{48,40},{56,48},{64,5... | collective-permute-start | bytes 2064392 | tf_op jit(solution)/shard_map/ppermute | solution.py:23
  84.3 1.4 %fusion.60 = (bf16[1,1]{1,0:T(2,128)(2,1)}, bf16[1,1]{1,0:T(2,128)(2,1)}, bf16[1,1]{1,0:T(2,128)(2,1)}) fusion(bf16[200,896]{1,0:T(8,128)(2,1)} %copy-done.5), kind=kLoop, calls=%fused_computation.124 | loop fusion | bytes 12 | tf_op jit(solution)/shard_map/slice | solution.py:344
  87.7 1.5 %fusion.59 = (bf16[1,1]{1,0:T(2,128)(2,1)}, bf16[1,1]{1,0:T(2,128)(2,1)}, bf16[1,1]{1,0:T(2,128)(2,1)}) fusion(bf16[200,896]{1,0:T(8,128)(2,1)} %copy-done.6), kind=kLoop, calls=%fused_computation.123 | loop fusion | bytes 12 | tf_op jit(solution)/shard_map/slice | solution.py:344
  91.1 6.8 %collective-permute-done.4 = bf16[2,192,896]{2,1,0:T(8,128)(2,1)S(1)} collective-permute-done((bf16[2,192,896]{2,1,0:T(8,128)(2,1)S(1)}, bf16[2,192,896]{2,1,0:T(8,128)(2,1)S(1)}, u32[]{:S(2)}, u32[]{:S(2)}) %collective-permute-start.4) | collective-permute-done | bytes 688160 | tf_op jit(solution)/shard_map/ppermute | solution.py:23
  98.0 1.3 %select_select_fusion.2 = (bf16[2,192,896]{2,1,0:T(8,128)(2,1)}, bf16[2,192,896]{2,1,0:T(8,128)(2,1)}) fusion(pred[2]{0:T(512)(128)(4,1)S(1)} %get-tuple-element.97, pred[2]{0:T(512)(128)(4,1)S(1)} %get-tuple-element.98, bf16[192,896]{1,0:T(8,128)(2,1)S(1)} %get-tuple-element.73, bf16[192,896]{1,0:T(8,128)(2,1)S(1)} %get-tuple-element.71, ...), kind=kLoop, calls=%fused_computation.33 | loop fusion | flops 1376256 | bytes 2752516 | tf_op jit(solution)/shard_map/jit(_where)/select_n | solution.py:352
  99.3 18.4 %reduce-scatter.2.cloned.1.call-done = bf16[64,3584]{1,0:T(8,128)(2,1)} async-done(((bf16[512,3584]{1,0:T(8,128)(2,1)}), bf16[64,3584]{1,0:T(8,128)(2,1)}) %reduce-scatter.2.cloned.1.call-update) | async-done | bytes 458768 | tf_op jit(solution)/shard_map/reduce_scatter | solution.py:329
  (59 shorter events, 5.4 us)
Async XLA Ops:
  7.2 17.3 %copy-start.8 = (s32[1,4]{1,0:T(1,128)S(1)}, s32[1,4]{1,0:T(1,128)}, u32[]{:S(2)}) copy-start(s32[1,4]{1,0:T(1,128)} %param.20) | copy-start | bytes 52
  7.2 110.5 %reduce-scatter.2.cloned.1.call-start = ((), (), s32[]{:S(2)}) async-start(), calls=%async_computation.1 | async-start | bytes 4128768 | tf_op jit(solution)/shard_map/reduce_scatter | solution.py:329
  19.3 15.3 %collective-permute-start.1 = (bf16[200,896]{1,0:T(8,128)(2,1)S(1)}, bf16[200,896]{1,0:T(8,128)(2,1)S(1)}, u32[]{:S(2)}, u32[]{:S(2)}) collective-permute-start(bf16[200,896]{1,0:T(8,128)(2,1)S(1)} %fusion.28), channel_id=1, source_target_pairs={{0,248},{8,0},{16,8},{24,16},{32,24},{40,32},{48,40},{56,48},{64,5... | collective-permute-start | bytes 1075208 | tf_op jit(solution)/shard_map/ppermute | solution.py:23
  21.7 14.7 %collective-permute-start = (bf16[200,896]{1,0:T(8,128)(2,1)S(1)}, bf16[200,896]{1,0:T(8,128)(2,1)S(1)}, u32[]{:S(2)}, u32[]{:S(2)}) collective-permute-start(bf16[200,896]{1,0:T(8,128)(2,1)S(1)} %fusion.27), channel_id=1, source_target_pairs={{0,8},{8,16},{16,24},{24,32},{32,40},{40,48},{48,56},{56,64},{64,7... | collective-permute-start | bytes 1075208 | tf_op jit(solution)/shard_map/ppermute | solution.py:23
  24.8 0.9 copy-start.7
  25.6 8.3 %copy-start.2 = (bf16[512,896]{1,0:T(8,128)(2,1)S(1)}, bf16[512,896]{1,0:T(8,128)(2,1)}, u32[]{:S(2)}) copy-start(bf16[512,896]{1,0:T(8,128)(2,1)} %key_ref.2) | copy-start | bytes 2752516
  25.6 8.3 %copy-start.3 = (bf16[512,896]{1,0:T(8,128)(2,1)S(1)}, bf16[512,896]{1,0:T(8,128)(2,1)}, u32[]{:S(2)}) copy-start(bf16[512,896]{1,0:T(8,128)(2,1)} %value_ref.2) | copy-start | bytes 2752516
  34.6 1.8 %copy-start.5 = (bf16[200,896]{1,0:T(8,128)(2,1)}, bf16[200,896]{1,0:T(8,128)(2,1)S(1)}, u32[]{:S(2)}) copy-start(bf16[200,896]{1,0:T(8,128)(2,1)S(1)} %collective-permute-done.1.right_ref) | copy-start | bytes 1075204
  36.5 0.7 copy-start.6
  45.9 13.9 %collective-permute-start.2 = (bf16[192,1024]{1,0:T(8,128)(2,1)}, bf16[192,1024]{1,0:T(8,128)(2,1)S(1)}, u32[]{:S(2)}, u32[]{:S(2)}) collective-permute-start(bf16[192,1024]{1,0:T(8,128)(2,1)} %get-tuple-element.37), channel_id=1, source_target_pairs={{0,248},{8,0},{16,8},{24,16},{32,24},{40,32},{48,40},{56,48},{64,5... | collective-permute-start | bytes 1179656 | tf_op jit(solution)/shard_map/ppermute | solution.py:23
  51.4 13.8 %collective-permute-start.3 = (bf16[192,1024]{1,0:T(8,128)(2,1)}, bf16[192,1024]{1,0:T(8,128)(2,1)S(1)}, u32[]{:S(2)}, u32[]{:S(2)}) collective-permute-start(bf16[192,1024]{1,0:T(8,128)(2,1)} %get-tuple-element.38), channel_id=1, source_target_pairs={{0,8},{8,16},{16,24},{24,32},{32,40},{40,48},{48,56},{56,64},{64,7... | collective-permute-start | bytes 1179656 | tf_op jit(solution)/shard_map/ppermute | solution.py:23
  55.6 9.9 %copy-start = (f32[512,128]{1,0:T(8,128)S(1)}, f32[512,128]{1,0:T(8,128)}, u32[]{:S(2)}) copy-start(f32[512,128]{1,0:T(8,128)} %get-tuple-element.36) | copy-start | bytes 786436
  59.8 6.1 %copy-start.4 = (bf16[192,1024]{1,0:T(8,128)(2,1)}, bf16[192,1024]{1,0:T(8,128)(2,1)S(1)}, u32[]{:S(2)}) copy-start(bf16[192,1024]{1,0:T(8,128)(2,1)S(1)} %collective-permute-done.2) | copy-start | bytes 1179652
  65.2 0.7 copy-start.1
  66.0 1.2 slice-start
  68.1 1.0 slice-start.1
  68.1 1.6 %copy-start.9 = (f32[512,896]{1,0:T(8,128)S(1)}, f32[512,896]{1,0:T(8,128)}, u32[]{:S(2)}) copy-start(f32[512,896]{1,0:T(8,128)} %get-tuple-element.35) | copy-start | bytes 5505028
  79.1 18.8 %collective-permute-start.4 = (bf16[2,192,896]{2,1,0:T(8,128)(2,1)S(1)}, bf16[2,192,896]{2,1,0:T(8,128)(2,1)S(1)}, u32[]{:S(2)}, u32[]{:S(2)}) collective-permute-start(bf16[2,192,896]{2,1,0:T(8,128)(2,1)S(1)} %get-tuple-element.41), channel_id=1, source_target_pairs={{0,8},{8,16},{16,24},{24,32},{32,40},{40,48},{48,56},{56,64},{64,7... | collective-permute-start | bytes 2064392 | tf_op jit(solution)/shard_map/ppermute | solution.py:23
  79.1 18.8 %collective-permute-start.5 = (bf16[2,192,896]{2,1,0:T(8,128)(2,1)S(1)}, bf16[2,192,896]{2,1,0:T(8,128)(2,1)S(1)}, u32[]{:S(2)}, u32[]{:S(2)}) collective-permute-start(bf16[2,192,896]{2,1,0:T(8,128)(2,1)S(1)} %get-tuple-element.42), channel_id=1, source_target_pairs={{0,248},{8,0},{16,8},{24,16},{32,24},{40,32},{48,40},{56,48},{64,5... | collective-permute-start | bytes 2064392 | tf_op jit(solution)/shard_map/ppermute | solution.py:23
Sparse Core Ops, SparseCore 0:
  79.2 38.4 reduce-scatter.1
